TPU v7x, 512 devices: a whole 4x8x8 slice. The times are simulated.
512 devices in a mesh: section: 8 (over z), ctx: 8 (over y_hi, x), tp: 8 (over y_lo, core).
Axes of the slice: x: 4, y: 8 (y_hi: 2, y_lo: 4; y = y_hi * 4 + y_lo), z: 8, core: 2. Of those that a mesh axis runs over, the one named last changes fastest.
Arguments:
- block_order: int32 [16], replicated, may hold values from 0 to 15, each once
- plan: int32 [8], replicated, may hold values from 0 to 1
- q_box: bfloat16 [8, 2, 1408, 8192], P('section', None, 'ctx', 'tp'), may hold values from -8 to 8
- k_box: bfloat16 [8, 2, 1408, 1024], P('section', None, ('ctx', 'tp')), may hold values from -8 to 8
- v_box: bfloat16 [8, 2, 1408, 1024], P('section', None, ('ctx', 'tp')), may hold values from -6 to 6
- grad_out: bfloat16 [8, 1408, 8192], P('section', 'ctx', 'tp'), may hold values from -6 to 6
Outputs:
- attn_out: bfloat16 [8, 1408, 8192], P('section', 'ctx', 'tp')
- grad_q: bfloat16 [8, 1408, 8192], P('section', 'ctx', 'tp')
- grad_k: float32 [8, 1408, 1024], P('section', ('ctx', 'tp'))
- grad_v: float32 [8, 1408, 1024], P('section', ('ctx', 'tp'))
Inputs may be any that keep to these rules, and one draw needn't show every extreme that they name: `block_order`: a permutation: every block sits in exactly one storage slot, slot j covering storage rows j * 88 to (j + 1) * 88 - 1.
All inputs are finite; a program needn't handle non-finite values.
Results may differ from a plain program's by a relative error of at most 0.012.
Values may be sent and summed in bfloat16 or wider, within the bound.
No kernel may reach another device: no remote copies, remote signals or barrier semaphores. Data moves between devices by JAX's collectives and lax.ppermute only.
A program may use at most 64 MiB of HBM per device.

v0:
```python
import jax
import jax.numpy as jnp
from jax import lax
from jax.sharding import PartitionSpec as P

HEAD_DIM = 128


NEG = -1e30


def passed_along(block, axis, distance):
    devices = range(lax.axis_size(axis))
    route = [((i - distance) % len(devices), i) for i in devices]
    return lax.ppermute(block, axis, route)


def body(block_order, plan, q_box, k_box, v_box, grad_out):
    tp_count = lax.axis_size("tp")
    ctx_count = lax.axis_size("ctx")
    tok_rows = q_box.shape[2]
    seq_rows = tok_rows * ctx_count
    block_len = tok_rows // 2
    head_size = HEAD_DIM
    heads_local = q_box.shape[3] // head_size
    kv_local = k_box.shape[3] // head_size // tp_count
    group = heads_local // kv_local
    kv_width = kv_local * head_size
    scale = head_size ** (-0.5)
    section_rank = lax.axis_index("section")
    tp_rank = lax.axis_index("tp")
    arrived = passed_along((q_box[0], k_box[0], v_box[0]), "section", 1)
    wanted = lax.dynamic_index_in_dim(plan, section_rank, 0, keepdims=False)
    queries = lax.dynamic_index_in_dim(arrived[0], wanted, 0, keepdims=False)
    key_rows = lax.dynamic_index_in_dim(arrived[1], wanted, 0, keepdims=False)
    value_rows = lax.dynamic_index_in_dim(arrived[2], wanted, 0, keepdims=False)
    cotangent = passed_along(grad_out[0], "section", -1)
    positions = (
        block_order[:, None] * block_len + jnp.arange(block_len, dtype=jnp.int32)[None, :]
    ).reshape(seq_rows)
    query_pos = lax.dynamic_slice_in_dim(positions, lax.axis_index("ctx") * tok_rows, tok_rows)
    key_full, value_full = (
        lax.all_gather(key_rows, ("ctx", "tp"), axis=0, tiled=True),
        lax.all_gather(value_rows, ("ctx", "tp"), axis=0, tiled=True),
    )
    key_store = lax.dynamic_slice_in_dim(key_full, tp_rank * kv_width, kv_width, 1)
    value_store = lax.dynamic_slice_in_dim(value_full, tp_rank * kv_width, kv_width, 1)
    q_split = queries.reshape(tok_rows, kv_local, group, head_size).transpose(1, 2, 0, 3)
    do_split = cotangent.reshape(tok_rows, kv_local, group, head_size).transpose(1, 2, 0, 3)
    key_split = key_store.reshape(seq_rows, kv_local, head_size).transpose(1, 0, 2)
    value_split = value_store.reshape(seq_rows, kv_local, head_size).transpose(1, 0, 2)
    visible_all = positions[None, :] <= query_pos[:, None]

    def per_group(inputs):
        q_group, do_group, key_head, value_head = inputs

        def per_head(sums, head_inputs):
            key_grad, value_grad = sums
            q_one, do_one = head_inputs
            scores = jnp.dot(q_one, key_head.T, preferred_element_type=jnp.float32) * scale
            scores = jnp.where(visible_all, scores, NEG)
            top_score = jnp.max(scores, axis=1, keepdims=True)
            totals = jnp.sum(
                jnp.where(visible_all, jnp.exp(scores - top_score), 0.0), axis=1, keepdims=True
            )
            log_total = top_score + jnp.log(totals)
            probs = jnp.where(visible_all, jnp.exp(scores - log_total), 0.0)
            probs_low = probs.astype(jnp.bfloat16)
            attended = jnp.dot(probs_low, value_head, preferred_element_type=jnp.float32)
            delta = jnp.sum(do_one.astype(jnp.float32) * attended, axis=1, keepdims=True)
            dprobs = jnp.dot(do_one, value_head.T, preferred_element_type=jnp.float32)
            dscores = (probs * (dprobs - delta)).astype(jnp.bfloat16)
            q_grad = (
                jnp.dot(dscores, key_head, preferred_element_type=jnp.float32) * scale
            ).astype(jnp.bfloat16)
            key_grad = (
                key_grad + jnp.dot(dscores.T, q_one, preferred_element_type=jnp.float32) * scale
            )
            value_grad = value_grad + jnp.dot(
                probs_low.T, do_one, preferred_element_type=jnp.float32
            )
            return ((key_grad, value_grad), (attended.astype(jnp.bfloat16), q_grad))

        zero_rows = jnp.zeros((seq_rows, head_size), jnp.float32)
        (key_grad, value_grad), (attended, q_grad) = lax.scan(
            per_head, (zero_rows, zero_rows), (q_group, do_group)
        )
        return (attended, q_grad, key_grad, value_grad)

    attended, q_grad, key_grad, value_grad = lax.map(
        per_group, (q_split, do_split, key_split, value_split)
    )
    attended_flat = attended.transpose(2, 0, 1, 3).reshape(tok_rows, heads_local * head_size)
    q_grad_flat = q_grad.transpose(2, 0, 1, 3).reshape(tok_rows, heads_local * head_size)
    key_terms = key_grad.transpose(1, 0, 2).reshape(seq_rows, kv_width)
    value_terms = value_grad.transpose(1, 0, 2).reshape(seq_rows, kv_width)
    grad_terms = jnp.concatenate([key_terms, value_terms], axis=1)
    own_grads = lax.psum_scatter(grad_terms, "ctx", scatter_dimension=0, tiled=True)
    key_part = own_grads[:, :kv_width]
    value_part = own_grads[:, kv_width:]
    k_grad_tokens, v_grad_tokens = (
        lax.all_to_all(key_part, "tp", split_axis=0, concat_axis=1, tiled=True),
        lax.all_to_all(value_part, "tp", split_axis=0, concat_axis=1, tiled=True),
    )
    return (attended_flat[None], q_grad_flat[None], k_grad_tokens[None], v_grad_tokens[None])


def solution(mesh):
    in_specs = (
        P(),
        P(),
        P("section", None, "ctx", "tp"),
        P("section", None, ("ctx", "tp"), None),
        P("section", None, ("ctx", "tp"), None),
        P("section", "ctx", "tp"),
    )
    out_specs = (
        P("section", "ctx", "tp"),
        P("section", "ctx", "tp"),
        P("section", ("ctx", "tp"), None),
        P("section", ("ctx", "tp"), None),
    )
    return jax.shard_map(body, mesh=mesh, in_specs=in_specs, out_specs=out_specs, check_vma=False)
```

profile of v0, /device:TPU:1, one launch (start us, length us, event | category | flops | bytes accessed | tf_op | source)
XLA Modules:
  0.0 454.2 jit_solution(15236497514800470888)
XLA Ops:
  7.2 4.8 %collective-permute-start.3 = (bf16[2,22,1024]{2,0,1:T(2,128)(2,1)}, bf16[2,22,1024]{2,0,1:T(2,128)(2,1)S(1)}, u32[]{:S(2)}, u32[]{:S(2)}) collective-permute-start(bf16[2,22,1024]{2,0,1:T(2,128)(2,1)} %bitcast.117), channel_id=1, source_target_pairs={{448,0},{0,64},{64,128},{128,192},{192,256},{256,320},{320,384},{3... | collective-permute-start | bytes 270344 | tf_op jit(solution)/shard_map/ppermute | solution.py:15
  12.0 1.2 dynamic_slice.45
  15.2 6.0 %collective-permute-done.3 = bf16[2,22,1024]{2,0,1:T(2,128)(2,1)S(1)} collective-permute-done((bf16[2,22,1024]{2,0,1:T(2,128)(2,1)}, bf16[2,22,1024]{2,0,1:T(2,128)(2,1)S(1)}, u32[]{:S(2)}, u32[]{:S(2)}) %collective-permute-start.3) | collective-permute-done | bytes 90144 | tf_op jit(solution)/shard_map/ppermute | solution.py:15
  22.0 1.9 collective-permute-start.1
  24.0 4.8 %collective-permute-done.1 = bf16[2,22,1024]{2,0,1:T(2,128)(2,1)S(1)} collective-permute-done((bf16[2,22,1024]{2,0,1:T(2,128)(2,1)}, bf16[2,22,1024]{2,0,1:T(2,128)(2,1)S(1)}, u32[]{:S(2)}, u32[]{:S(2)}) %collective-permute-start.1) | collective-permute-done | bytes 90144 | tf_op jit(solution)/shard_map/ppermute | solution.py:15
  29.5 1.9 collective-permute-start
  31.5 4.6 %collective-permute-start.2 = (bf16[176,1024]{1,0:T(8,128)(2,1)}, bf16[176,1024]{1,0:T(8,128)(2,1)S(1)}, u32[]{:S(2)}, u32[]{:S(2)}) collective-permute-start(bf16[176,1024]{1,0:T(8,128)(2,1)} %bitcast.116), channel_id=1, source_target_pairs={{64,0},{128,64},{192,128},{256,192},{320,256},{384,320},{448,384},... | collective-permute-start | bytes 1081352 | tf_op jit(solution)/shard_map/ppermute | solution.py:15
  37.0 4.4 collective-permute-done.2
  42.3 5.9 %collective-permute-done = bf16[2,176,1024]{2,1,0:T(8,128)(2,1)S(1)} collective-permute-done((bf16[2,176,1024]{2,1,0:T(8,128)(2,1)}, bf16[2,176,1024]{2,1,0:T(8,128)(2,1)S(1)}, u32[]{:S(2)}, u32[]{:S(2)}) %collective-permute-start) | collective-permute-done | bytes 720928 | tf_op jit(solution)/shard_map/ppermute | solution.py:15
  49.0 92.7 %all-gather.7.cloned.1.call-done = bf16[1,1408,1024]{2,0,1:T(2,128)(2,1)} async-done(((bf16[1,22,1024]{2,0,1:T(2,128)(2,1)}), bf16[1,1408,1024]{2,0,1:T(2,128)(2,1)}) %all-gather.7.cloned.1.call-update) | async-done | bytes 2883600 | tf_op jit(solution)/shard_map/all_gather | solution.py:44
  141.7 1.8 constant_dynamic-slice_fusion
  143.5 118.6 %all-gather.5.cloned.1.call-done = bf16[1,1408,1024]{2,0,1:T(2,128)(2,1)} async-done(((bf16[1,22,1024]{2,0,1:T(2,128)(2,1)}), bf16[1,1408,1024]{2,0,1:T(2,128)(2,1)}) %all-gather.5.cloned.1.call-update) | async-done | bytes 2883600 | tf_op jit(solution)/shard_map/all_gather | solution.py:43
  262.2 1.8 constant_dynamic-slice_fusion.2
  264.0 68.6 %while.30 = (s32[]{:T(128)}, f32[1408,128]{1,0:T(8,128)S(1)}, f32[1408,128]{1,0:T(8,128)S(1)}, bf16[8,176,128]{2,1,0:T(8,128)(2,1)}, bf16[8,176,128]{2,1,0:T(8,1...) while((s32[]{:T(128)}, f32[1408,128]{1,0:T(8,128)S(1)}, ...), condition=%wide.region_4.5_spmd.clone, body=%wide.region_0.4_spmd.clone.sunk | while | flops 386129568 | bytes 11705100 | solution.py:85
  264.0 1.2 fusion.61
  265.9 1.2 multiply_reduce_fusion.2
  267.1 1.2 fusion.64
  268.3 1.4 fusion.65
  270.6 1.4 convolution_add_fusion.2
  272.6 1.2 fusion.61
  276.8 1.4 fusion.65
  279.2 1.4 convolution_add_fusion.2
  281.2 1.2 fusion.61
  283.1 1.2 multiply_reduce_fusion.2
  285.4 1.4 fusion.65
  287.7 1.4 convolution_add_fusion.2
  289.7 1.2 fusion.61
  294.0 1.4 fusion.65
  296.3 1.4 convolution_add_fusion.2
  298.3 1.2 fusion.61
  300.2 1.2 multiply_reduce_fusion.2
  302.6 1.4 fusion.65
  304.9 1.4 convolution_add_fusion.2
  306.9 1.2 fusion.61
  311.1 1.4 fusion.65
  313.5 1.4 convolution_add_fusion.2
  315.5 1.2 fusion.61
  319.7 1.4 fusion.65
  322.0 1.4 convolution_add_fusion.2
  324.0 1.2 fusion.61
  328.3 1.4 fusion.65
  330.6 1.4 convolution_add_fusion.2
  332.6 1.2 pad_maximum_fusion
  333.8 89.6 %reduce-scatter.2.cloned.1.call-done = f32[176,256]{1,0:T(8,128)} async-done(((f32[1408,256]{1,0:T(8,128)}), f32[176,256]{1,0:T(8,128)}) %reduce-scatter.2.cloned.1.call-update) | async-done | bytes 180240 | tf_op jit(solution)/shard_map/reduce_scatter | solution.py:98
  425.0 7.0 %all-to-all-start = ((f32[8,22,128]{2,1,0:T(8,128)}), f32[8,22,128]{2,1,0:T(8,128)S(1)}, u32[]{:S(2)}, u32[]{:S(2)}) async-start(f32[8,22,128]{2,1,0:T(8,128)} %all_to_all.24), calls=%async_computation.1 | async-start | bytes 196608 | tf_op jit(solution)/shard_map/all_to_all | solution.py:102
  432.6 4.8 %all-to-all-done = f32[8,22,128]{2,1,0:T(8,128)S(1)} async-done(((f32[8,22,128]{2,1,0:T(8,128)}), f32[8,22,128]{2,1,0:T(8,128)S(1)}, u32[]{:S(2)}, u32[]{:S(2)}) %all-to-all-start) | async-done | bytes 90144 | tf_op jit(solution)/shard_map/all_to_all | solution.py:102
  437.4 4.2 all-to-all-start.1
  445.2 1.8 all-to-all-done.1
  (86 shorter events, 42.7 us)
Async XLA Ops:
  7.2 134.5 %all-gather.7.cloned.1.call-start = ((), (), s32[]{:S(2)}) async-start(), calls=%async_computation.5 | async-start | bytes 5857280 | tf_op jit(solution)/shard_map/all_gather | solution.py:44
  7.2 14.0 %collective-permute-start.3 = (bf16[2,22,1024]{2,0,1:T(2,128)(2,1)}, bf16[2,22,1024]{2,0,1:T(2,128)(2,1)S(1)}, u32[]{:S(2)}, u32[]{:S(2)}) collective-permute-start(bf16[2,22,1024]{2,0,1:T(2,128)(2,1)} %bitcast.117), channel_id=1, source_target_pairs={{448,0},{0,64},{64,128},{128,192},{192,256},{256,320},{320,384},{3... | collective-permute-start | bytes 270344 | tf_op jit(solution)/shard_map/ppermute | solution.py:15
  22.0 240.2 %all-gather.5.cloned.1.call-start = ((), (), s32[]{:S(2)}) async-start(), calls=%async_computation.4 | async-start | bytes 5857280 | tf_op jit(solution)/shard_map/all_gather | solution.py:43
  22.0 6.7 %collective-permute-start.1 = (bf16[2,22,1024]{2,0,1:T(2,128)(2,1)}, bf16[2,22,1024]{2,0,1:T(2,128)(2,1)S(1)}, u32[]{:S(2)}, u32[]{:S(2)}) collective-permute-start(bf16[2,22,1024]{2,0,1:T(2,128)(2,1)} %bitcast.118), channel_id=1, source_target_pairs={{448,0},{0,64},{64,128},{128,192},{192,256},{256,320},{320,384},{3... | collective-permute-start | bytes 270344 | tf_op jit(solution)/shard_map/ppermute | solution.py:15
  29.5 393.9 %reduce-scatter.2.cloned.1.call-start = ((), (), s32[]{:S(2)}) async-start(), calls=%async_computation.3 | async-start | bytes 1622016 | tf_op jit(solution)/shard_map/reduce_scatter | solution.py:98
  29.5 18.6 %collective-permute-start = (bf16[2,176,1024]{2,1,0:T(8,128)(2,1)}, bf16[2,176,1024]{2,1,0:T(8,128)(2,1)S(1)}, u32[]{:S(2)}, u32[]{:S(2)}) collective-permute-start(bf16[2,176,1024]{2,1,0:T(8,128)(2,1)} %bitcast.115), channel_id=1, source_target_pairs={{448,0},{0,64},{64,128},{128,192},{192,256},{256,320},{320,384},{3... | collective-permute-start | bytes 2162696 | tf_op jit(solution)/shard_map/ppermute | solution.py:15
  31.5 10.0 %collective-permute-start.2 = (bf16[176,1024]{1,0:T(8,128)(2,1)}, bf16[176,1024]{1,0:T(8,128)(2,1)S(1)}, u32[]{:S(2)}, u32[]{:S(2)}) collective-permute-start(bf16[176,1024]{1,0:T(8,128)(2,1)} %bitcast.116), channel_id=1, source_target_pairs={{64,0},{128,64},{192,128},{256,192},{320,256},{384,320},{448,384},... | collective-permute-start | bytes 1081352 | tf_op jit(solution)/shard_map/ppermute | solution.py:15
  332.6 111.0 %copy-start = (bf16[8,176,128]{2,1,0:T(8,128)(2,1)S(1)}, bf16[8,176,128]{2,1,0:T(8,128)(2,1)}, u32[]{:S(2)}) copy-start(bf16[8,176,128]{2,1,0:T(8,128)(2,1)} %get-tuple-element.90) | copy-start | bytes 1081348
  425.0 12.4 %all-to-all-start = ((f32[8,22,128]{2,1,0:T(8,128)}), f32[8,22,128]{2,1,0:T(8,128)S(1)}, u32[]{:S(2)}, u32[]{:S(2)}) async-start(f32[8,22,128]{2,1,0:T(8,128)} %all_to_all.24), calls=%async_computation.1 | async-start | bytes 196608 | tf_op jit(solution)/shard_map/all_to_all | solution.py:102
  437.4 9.6 %all-to-all-start.1 = ((f32[8,22,128]{2,1,0:T(8,128)}), f32[8,22,128]{2,1,0:T(8,128)S(1)}, u32[]{:S(2)}, u32[]{:S(2)}) async-start(f32[8,22,128]{2,1,0:T(8,128)} %all_to_all.27), calls=%async_computation.2 | async-start | bytes 196608 | tf_op jit(solution)/shard_map/all_to_all | solution.py:103
Sparse Core Ops, SparseCore 0:
  22.1 119.5 all-gather.6
  144.4 117.6 all-gather.4
  334.0 89.4 reduce-scatter.1
where the time goes:
time: 457 us; the launch traced here: 454 us
  waiting for transfers between devices  329 us (72%)
  matrix products  57.9 us (13%)
  starting transfers between devices  24.5 us (5%)
  local copies, waits for them, and re-layouts  19.7 us (4%)
  between operations  15.8 us (3%)
  other arithmetic  7.34 us (2%)
    all_gather x1, waiting for transfers between devices, body(): lax.all_gather(key_rows, ('ctx', 'tp'), axis=0, tiled=True)  119 us
    all_gather x1, waiting for transfers between devices, body(): lax.all_gather(value_rows, ('ctx', 'tp'), axis=0, tiled=True)  92.7 us
    reduce_scatter x1, waiting for transfers between devices, body(): lax.psum_scatter(grad_terms, 'ctx', scatter_dimension=0, tiled=True)  89.6 us
    ppermute x4, waiting for transfers between devices, passed_along(): return lax.ppermute(block, axis, route)  21.1 us
    ppermute x4, starting transfers between devices, passed_along(): return lax.ppermute(block, axis, route)  13.2 us
    dot_general x8, matrix products, per_head(): jnp.dot(dscores.T, q_one, preferred_element_type=jnp.float32) * scale  11.2 us
    dot_general x8, matrix products, per_head(): jnp.dot(probs_low.T, do_one, preferred_element_type=jnp.float32)  11 us
    dot_general x8, matrix products, per_head(): jnp.dot(q_one, key_head.T, preferred_element_type=jnp.float32) * scale  9.57 us
  transfers between devices with their start and end apart: 9, of which 9 were waited for; matrix products, arithmetic and copies ran while one was open for 2% of the time, Pallas kernels for 0%

commit v1 on v0

v1 whole, which is shorter than its diff:
```python
import jax
import jax.numpy as jnp
from jax import lax
from jax.sharding import PartitionSpec as P

HEAD_DIM = 128


NEG = -1e30


def passed_along(block, axis, distance):
    devices = range(lax.axis_size(axis))
    route = [((i - distance) % len(devices), i) for i in devices]
    return lax.ppermute(block, axis, route)


def body(block_order, plan, q_box, k_box, v_box, grad_out):
    tp_count = lax.axis_size("tp")
    ctx_count = lax.axis_size("ctx")
    section_count = lax.axis_size("section")
    tok_rows = q_box.shape[2]
    kv_rows = k_box.shape[2]
    seq_rows = tok_rows * ctx_count
    block_len = seq_rows // block_order.shape[0]
    head_size = HEAD_DIM
    heads_local = q_box.shape[3] // head_size
    kv_local = k_box.shape[3] // head_size // tp_count
    group = heads_local // kv_local
    kv_width = kv_local * head_size
    scale = head_size ** (-0.5)
    section_rank = lax.axis_index("section")

    receiver = (section_rank + 1) % section_count
    wanted = lax.dynamic_index_in_dim(plan, receiver, 0, keepdims=False)
    q_send = lax.dynamic_index_in_dim(q_box[0], wanted, 0, keepdims=False)
    k_send = lax.dynamic_index_in_dim(k_box[0], wanted, 0, keepdims=False)
    v_send = lax.dynamic_index_in_dim(v_box[0], wanted, 0, keepdims=False)
    kv_send = jnp.stack(
        [k_send.reshape(kv_rows, -1, head_size), v_send.reshape(kv_rows, -1, head_size)], axis=2
    ).reshape(kv_rows, -1)
    queries, kv_rows_in = passed_along((q_send, kv_send), "section", 1)
    cotangent = passed_along(grad_out[0], "section", -1)

    kv_tok = lax.all_to_all(kv_rows_in, "tp", split_axis=1, concat_axis=0, tiled=True)
    kv_full = lax.all_gather(kv_tok, "ctx", axis=0, tiled=True)
    kv_full = kv_full.reshape(seq_rows, kv_local, 2, head_size)
    key_heads = kv_full[:, :, 0, :]
    value_heads = kv_full[:, :, 1, :]

    positions = (
        block_order[:, None] * block_len + jnp.arange(block_len, dtype=jnp.int32)[None, :]
    ).reshape(seq_rows)
    query_pos = lax.dynamic_slice_in_dim(positions, lax.axis_index("ctx") * tok_rows, tok_rows)
    visible = (positions[None, :] <= query_pos[:, None])[None, None]

    q4 = queries.reshape(tok_rows, kv_local, group, head_size)
    do4 = cotangent.reshape(tok_rows, kv_local, group, head_size)
    scores = jnp.einsum("qgjd,kgd->gjqk", q4, key_heads, preferred_element_type=jnp.float32) * scale
    scores = jnp.where(visible, scores, NEG)
    top_score = jnp.max(scores, axis=-1, keepdims=True)
    totals = jnp.sum(jnp.where(visible, jnp.exp(scores - top_score), 0.0), axis=-1, keepdims=True)
    log_total = top_score + jnp.log(totals)
    probs = jnp.where(visible, jnp.exp(scores - log_total), 0.0)
    probs_low = probs.astype(jnp.bfloat16)
    attended = jnp.einsum(
        "gjqk,kgd->qgjd", probs_low, value_heads, preferred_element_type=jnp.float32
    )
    delta = jnp.sum(do4.astype(jnp.float32) * attended, axis=-1)
    dprobs = jnp.einsum("qgjd,kgd->gjqk", do4, value_heads, preferred_element_type=jnp.float32)
    dscores = (probs * (dprobs - jnp.transpose(delta, (1, 2, 0))[..., None])).astype(jnp.bfloat16)
    q_grad = (
        jnp.einsum("gjqk,kgd->qgjd", dscores, key_heads, preferred_element_type=jnp.float32) * scale
    ).astype(jnp.bfloat16)
    key_grad = jnp.einsum("gjqk,qgjd->kgd", dscores, q4, preferred_element_type=jnp.float32) * scale
    value_grad = jnp.einsum("gjqk,qgjd->kgd", probs_low, do4, preferred_element_type=jnp.float32)

    attended_flat = attended.astype(jnp.bfloat16).reshape(tok_rows, heads_local * head_size)
    q_grad_flat = q_grad.reshape(tok_rows, heads_local * head_size)
    grad_terms = jnp.stack([key_grad, value_grad], axis=2).reshape(seq_rows, 2 * kv_width)
    own_grads = lax.psum_scatter(grad_terms, "ctx", scatter_dimension=0, tiled=True)
    tok_grads = lax.all_to_all(own_grads, "tp", split_axis=0, concat_axis=1, tiled=True)
    tok_grads = tok_grads.reshape(kv_rows, -1, 2, head_size)
    k_grad_tokens = tok_grads[:, :, 0, :].reshape(kv_rows, -1)
    v_grad_tokens = tok_grads[:, :, 1, :].reshape(kv_rows, -1)
    return (attended_flat[None], q_grad_flat[None], k_grad_tokens[None], v_grad_tokens[None])


def solution(mesh):
    in_specs = (
        P(),
        P(),
        P("section", None, "ctx", "tp"),
        P("section", None, ("ctx", "tp"), None),
        P("section", None, ("ctx", "tp"), None),
        P("section", "ctx", "tp"),
    )
    out_specs = (
        P("section", "ctx", "tp"),
        P("section", "ctx", "tp"),
        P("section", ("ctx", "tp"), None),
        P("section", ("ctx", "tp"), None),
    )
    return jax.shard_map(body, mesh=mesh, in_specs=in_specs, out_specs=out_specs, check_vma=False)
```

time: 457 us -> 213 us (0.47)
  waiting for transfers between devices: 329 us -> 99.2 us
  matrix products: 57.9 us -> 12.3 us
  blocking collectives: 0 us -> 41.5 us
  local copies, waits for them, and re-layouts: 19.7 us -> 10.9 us
  starting transfers between devices: 24.5 us -> 29.4 us
    all_gather x2 -> x0, waiting for transfers between devices: 211 us -> none  [the longest x1 119 us: body(): lax.all_gather(key_rows, ('ctx', 'tp'), axis=0, tiled=True)]
    dot_general x48 -> x6, matrix products: 57.9 us -> 12.3 us  [the longest x1 3.32 us: body(): jnp.einsum('gjqk,kgd->qgjd', dscores, key_heads, preferred_element_type=j...]
    all_gather x0 -> x1, blocking collectives: none -> 41.5 us  [body(): kv_full = lax.all_gather(kv_tok, 'ctx', axis=0, tiled=True)]
    ppermute x4 -> x3, waiting for transfers between devices: 21.1 us -> 1.04 us  [passed_along(): return lax.ppermute(block, axis, route)]
    dynamic_update_slice x8 -> x0, local copies, waits for them, and re-layouts: 5.03 us -> none  [per_group(): lax.scan(per_head, (zero_rows, zero_rows), (q_group, do_group))]
    ppermute x4 -> x3, starting transfers between devices: 13.2 us -> 15.4 us  [passed_along(): return lax.ppermute(block, axis, route)]
  transfers between devices with their start and end apart: 9 -> 6, of which waited for: 9 -> 4; matrix products, arithmetic and copies ran while one was open for 2% -> 5% of each run, Pallas kernels for 0% -> 0%
where the time goes in v1:
time: 213 us
  waiting for transfers between devices  99.2 us (47%)
  blocking collectives  41.5 us (19%)
  starting transfers between devices  29.4 us (14%)
  between operations  16.2 us (8%)
  matrix products  12.3 us (6%)
  local copies, waits for them, and re-layouts  10.9 us (5%)
  other arithmetic  3.13 us (1%)
    reduce_scatter x1, waiting for transfers between devices, body(): lax.psum_scatter(grad_terms, 'ctx', scatter_dimension=0, tiled=True)  90.8 us
    all_gather x1, blocking collectives, body(): kv_full = lax.all_gather(kv_tok, 'ctx', axis=0, tiled=True)  41.5 us
    ppermute x3, starting transfers between devices, passed_along(): return lax.ppermute(block, axis, route)  15.4 us
    all_to_all x1, starting transfers between devices, body(): lax.all_to_all(kv_rows_in, 'tp', split_axis=1, concat_axis=0, tiled=True)  6.98 us
    all_to_all x1, starting transfers between devices, body(): lax.all_to_all(own_grads, 'tp', split_axis=0, concat_axis=1, tiled=True)  6.96 us
    all_to_all x1, waiting for transfers between devices, body(): lax.all_to_all(kv_rows_in, 'tp', split_axis=1, concat_axis=0, tiled=True)  5.15 us
  transfers between devices with their start and end apart: 6, of which 4 were waited for; matrix products, arithmetic and copies ran while one was open for 5% of the time, Pallas kernels for 0%

profile of v1, /device:TPU:1, one launch (start us, length us, event | category | flops | bytes accessed | tf_op | source)
XLA Modules:
  0.0 212.7 jit_solution(3541561579943129193)
XLA Ops:
  7.2 0.0 copy-start
  7.2 11.6 %collective-permute-start.2 = (bf16[176,1024]{1,0:T(8,128)(2,1)}, bf16[176,1024]{1,0:T(8,128)(2,1)S(1)}, u32[]{:S(2)}, u32[]{:S(2)}) collective-permute-start(bf16[176,1024]{1,0:T(8,128)(2,1)} %bitcast.163), channel_id=1, source_target_pairs={{64,0},{128,64},{192,128},{256,192},{320,256},{384,320},{448,384},... | collective-permute-start | bytes 1081352 | tf_op jit(solution)/shard_map/ppermute | solution.py:15
  18.8 1.2 dynamic_slice.18
  22.0 1.5 dynamic-slice_reduce_fusion
  23.6 0.1 copy.26
  23.7 1.9 collective-permute-start
  25.6 0.0 copy-done
  25.6 0.8 dynamic-slice_bitcast_fusion
  26.4 1.9 collective-permute-start.1
  28.3 0.7 broadcast_multiply_fusion
  29.0 0.1 iota_add_fusion
  29.1 0.1 add.59
  29.1 0.1 dynamic_slice.21
  29.2 1.0 collective-permute-done
  30.3 0.7 copy.27
  31.0 7.0 %all-to-all-start = ((bf16[22,8,256]{2,0,1:T(8,128)(2,1)}), bf16[22,8,256]{2,0,1:T(8,128)(2,1)S(1)}, u32[]{:S(2)}, u32[]{:S(2)}) async-start(bf16[22,8,256]{2,0,1:T(8,128)(2,1)} %copy.27), calls=%async_computation | async-start | bytes 196608 | tf_op jit(solution)/shard_map/all_to_all | solution.py:45
  37.9 0.0 reduce-scatter.2.cloned.1.call-start
  37.9 0.2 broadcast_compare_fusion
  38.2 5.1 %all-to-all-done = bf16[22,8,256]{2,0,1:T(8,128)(2,1)S(1)} async-done(((bf16[22,8,256]{2,0,1:T(8,128)(2,1)}), bf16[22,8,256]{2,0,1:T(8,128)(2,1)S(1)}, u32[]{:S(2)}, u32[]{:S(2)}) %all-to-all-start) | async-done | bytes 90144 | tf_op jit(solution)/shard_map/all_to_all | solution.py:45
  43.3 41.5 %all_gather.3 = bf16[1408,256]{1,0:T(8,128)(2,1)S(1)} all-gather(bf16[176,256]{1,0:T(8,128)(2,1)S(1)} %all_to_all.29), channel_id=1, replica_groups=mesh['section'=8,'ctx'=8,'tp'=8] {'ctx'}, dimensions={0}, use_global_device_ids=true | all-gather | bytes 811008 | tf_op jit(solution)/shard_map/all_gather | solution.py:46
  84.9 0.3 copy.28
  85.2 0.0 collective-permute-done.2
  85.2 0.1 convert_bitcast_fusion
  85.3 0.1 copy.47
  85.4 0.0 collective-permute-done.1
  85.4 2.0 fusion.30
  87.4 2.0 select_reduce_fusion
  89.4 0.1 copy.48
  89.5 1.8 fusion.18
  91.3 2.7 %fusion.6 = bf16[8,176,1408]{2,1,0:T(8,128)(2,1)S(1)} fusion(f32[8,176]{1,0:T(8,128)S(1)} %bitcast.162, f32[1,8,176,1408]{3,2,1,0:T(8,128)S(1)} %get-tuple-element.13, f32[8,176]{1,0:T(8,128)S(1)} %log_add_fusion, pred[176,1408]{1,0:T(8,128)(4,1)S(1)} %broadcast_compare_fusion, bf16[1408,1,2,128]{0,3,2,1:T(8,128)(2,1)S(1)} %bitcast.146, ...), kind=kOutput, calls=%fused_computation.10 | convolution fusion | flops 517423104 | bytes 12879872 | tf_op jit(solution)/shard_map/qgjd,kgd->gjqk/dot_general | solution.py:70
  94.0 0.0 copy-start.1
  94.0 0.9 fusion.13
  94.9 1.7 convolution_bitcast_fusion
  96.6 0.0 copy-done.1
  96.6 0.1 pad_maximum_fusion
  96.7 1.5 copy.38
  98.2 0.0 reduce-scatter.2.cloned.1.call-update
  98.2 0.1 copy.32
  98.3 0.9 broadcast_in_dim_reshape.7
  99.2 90.8 %reduce-scatter.2.cloned.1.call-done = f32[176,256]{1,0:T(8,128)} async-done(((f32[1408,256]{1,0:T(8,128)}), f32[176,256]{1,0:T(8,128)}) %reduce-scatter.2.cloned.1.call-update) | async-done | bytes 180240 | tf_op jit(solution)/shard_map/reduce_scatter | solution.py:81
  190.0 1.6 all_to_all.30
  191.6 7.0 %all-to-all-start.1 = ((f32[8,22,256]{2,1,0:T(8,128)}), f32[8,22,256]{2,1,0:T(8,128)S(1)}, u32[]{:S(2)}, u32[]{:S(2)}) async-start(f32[8,22,256]{2,1,0:T(8,128)} %all_to_all.30), calls=%async_computation.2 | async-start | bytes 393216 | tf_op jit(solution)/shard_map/all_to_all | solution.py:82
  198.6 3.3 %fusion.17 = bf16[176,1,8,128]{3,0,2,1:T(8,128)(2,1)S(1)} fusion(bf16[8,176,1408]{2,1,0:T(8,128)(2,1)} %copy-done.1, bf16[1408,1,2,128]{0,3,2,1:T(8,128)(2,1)S(1)} %bitcast.147), kind=kOutput, calls=%fused_computation.19 | convolution fusion | flops 507871232 | bytes 4685824 | tf_op jit(solution)/shard_map/gjqk,kgd->qgjd/dot_general | solution.py:73
  201.9 0.1 copy.35
  202.0 0.9 broadcast_in_dim_reshape.8
  202.9 2.2 %all-to-all-done.1 = f32[8,22,256]{2,1,0:T(8,128)S(1)} async-done(((f32[8,22,256]{2,1,0:T(8,128)}), f32[8,22,256]{2,1,0:T(8,128)S(1)}, u32[]{:S(2)}, u32[]{:S(2)}) %all-to-all-start.1) | async-done | bytes 180256 | tf_op jit(solution)/shard_map/all_to_all | solution.py:82
  205.1 0.1 copy.75
  205.2 0.7 fusion.29
  (10 shorter events, 0.1 us)
Async XLA Ops:
  7.2 18.5 %copy-start = (bf16[1,2,176,1024]{3,2,1,0:T(8,128)(2,1)S(1)}, bf16[1,2,176,1024]{3,2,1,0:T(8,128)(2,1)}, u32[]{:S(2)}) copy-start(bf16[1,2,176,1024]{3,2,1,0:T(8,128)(2,1)} %param.8) | copy-start | bytes 2162692
  7.2 78.0 %collective-permute-start.2 = (bf16[176,1024]{1,0:T(8,128)(2,1)}, bf16[176,1024]{1,0:T(8,128)(2,1)S(1)}, u32[]{:S(2)}, u32[]{:S(2)}) collective-permute-start(bf16[176,1024]{1,0:T(8,128)(2,1)} %bitcast.163), channel_id=1, source_target_pairs={{64,0},{128,64},{192,128},{256,192},{320,256},{384,320},{448,384},... | collective-permute-start | bytes 1081352 | tf_op jit(solution)/shard_map/ppermute | solution.py:15
  23.7 6.6 %collective-permute-start = (bf16[22,2048]{1,0:T(8,128)(2,1)S(1)}, bf16[22,2048]{1,0:T(8,128)(2,1)S(1)}, u32[]{:S(2)}, u32[]{:S(2)}) collective-permute-start(bf16[22,2048]{1,0:T(8,128)(2,1)S(1)} %reshape.167), channel_id=1, source_target_pairs={{448,0},{0,64},{64,128},{128,192},{192,256},{256,320},{320,384},{3... | collective-permute-start | bytes 270344 | tf_op jit(solution)/shard_map/ppermute | solution.py:15
  26.4 59.0 %collective-permute-start.1 = (bf16[176,1024]{1,0:T(8,128)(2,1)}, bf16[176,1024]{1,0:T(8,128)(2,1)S(1)}, u32[]{:S(2)}, u32[]{:S(2)}) collective-permute-start(bf16[176,1024]{1,0:T(8,128)(2,1)} %dynamic-slice_bitcast_fusion), channel_id=1, source_target_pairs={{448,0},{0,64},{64,128},{128,192},{192,256},{256,320},{320,384},{3... | collective-permute-start | bytes 1081352 | tf_op jit(solution)/shard_map/ppermute | solution.py:15
  31.0 12.3 %all-to-all-start = ((bf16[22,8,256]{2,0,1:T(8,128)(2,1)}), bf16[22,8,256]{2,0,1:T(8,128)(2,1)S(1)}, u32[]{:S(2)}, u32[]{:S(2)}) async-start(bf16[22,8,256]{2,0,1:T(8,128)(2,1)} %copy.27), calls=%async_computation | async-start | bytes 196608 | tf_op jit(solution)/shard_map/all_to_all | solution.py:45
  37.9 152.1 %reduce-scatter.2.cloned.1.call-start = ((), (), s32[]{:S(2)}) async-start(), calls=%async_computation.3 | async-start | bytes 1622016 | tf_op jit(solution)/shard_map/reduce_scatter | solution.py:81
  94.0 2.6 %copy-start.1 = (bf16[8,176,1408]{2,1,0:T(8,128)(2,1)}, bf16[8,176,1408]{2,1,0:T(8,128)(2,1)S(1)}, u32[]{:S(2)}) copy-start(bf16[8,176,1408]{2,1,0:T(8,128)(2,1)S(1)} %fusion.6) | copy-start | bytes 11894788
  191.6 13.5 %all-to-all-start.1 = ((f32[8,22,256]{2,1,0:T(8,128)}), f32[8,22,256]{2,1,0:T(8,128)S(1)}, u32[]{:S(2)}, u32[]{:S(2)}) async-start(f32[8,22,256]{2,1,0:T(8,128)} %all_to_all.30), calls=%async_computation.2 | async-start | bytes 393216 | tf_op jit(solution)/shard_map/all_to_all | solution.py:82
Sparse Core Ops, SparseCore 0:
  98.4 91.6 reduce-scatter.1

commit v2 on v1

--- a/solution.py
+++ b/solution.py
@@ -4,6 +4,7 @@
 from jax.sharding import PartitionSpec as P
 
 HEAD_DIM = 128
+CTX_INNER = 4
 
 
 NEG = -1e30
@@ -43,16 +44,38 @@
     cotangent = passed_along(grad_out[0], "section", -1)
 
     kv_tok = lax.all_to_all(kv_rows_in, "tp", split_axis=1, concat_axis=0, tiled=True)
-    kv_full = lax.all_gather(kv_tok, "ctx", axis=0, tiled=True)
-    kv_full = kv_full.reshape(seq_rows, kv_local, 2, head_size)
+    inner_count = CTX_INNER
+    outer_count = ctx_count // inner_count
+    ctx_rank = lax.axis_index("ctx")
+    inner_rank = ctx_rank % inner_count
+    outer_rank = ctx_rank // inner_count
+    swap = [(c, (c + inner_count) % ctx_count) for c in range(ctx_count)]
+
+    def inner_shift(k):
+        return [
+            (o * inner_count + i, o * inner_count + (i + k) % inner_count)
+            for o in range(outer_count)
+            for i in range(inner_count)
+        ]
+
+    partner = lax.ppermute(kv_tok, "ctx", swap)
+    pair = jnp.stack([kv_tok, partner])
+    arrived_kv = [pair] + [lax.ppermute(pair, "ctx", inner_shift(k)) for k in range(1, inner_count)]
+    kv_full = jnp.stack(arrived_kv).reshape(seq_rows, kv_local, 2, head_size)
     key_heads = kv_full[:, :, 0, :]
     value_heads = kv_full[:, :, 1, :]
 
     positions = (
         block_order[:, None] * block_len + jnp.arange(block_len, dtype=jnp.int32)[None, :]
-    ).reshape(seq_rows)
-    query_pos = lax.dynamic_slice_in_dim(positions, lax.axis_index("ctx") * tok_rows, tok_rows)
-    visible = (positions[None, :] <= query_pos[:, None])[None, None]
+    ).reshape(ctx_count, tok_rows)
+    shift_ids = jnp.arange(inner_count, dtype=jnp.int32)[:, None]
+    side_ids = jnp.arange(outer_count, dtype=jnp.int32)[None, :]
+    key_ctx = ((outer_rank + side_ids) % outer_count) * inner_count + (
+        (inner_rank - shift_ids) % inner_count
+    )
+    key_pos = jnp.take(positions, key_ctx.reshape(-1), axis=0).reshape(seq_rows)
+    query_pos = lax.dynamic_index_in_dim(positions, ctx_rank, 0, keepdims=False)
+    visible = (key_pos[None, :] <= query_pos[:, None])[None, None]
 
     q4 = queries.reshape(tok_rows, kv_local, group, head_size)
     do4 = cotangent.reshape(tok_rows, kv_local, group, head_size)
@@ -77,8 +100,13 @@
 
     attended_flat = attended.astype(jnp.bfloat16).reshape(tok_rows, heads_local * head_size)
     q_grad_flat = q_grad.reshape(tok_rows, heads_local * head_size)
-    grad_terms = jnp.stack([key_grad, value_grad], axis=2).reshape(seq_rows, 2 * kv_width)
-    own_grads = lax.psum_scatter(grad_terms, "ctx", scatter_dimension=0, tiled=True)
+    grad_terms = jnp.stack([key_grad, value_grad], axis=2).reshape(
+        inner_count, outer_count, tok_rows, 2 * kv_width
+    )
+    gathered = grad_terms[0]
+    for k in range(1, inner_count):
+        gathered = gathered + lax.ppermute(grad_terms[(-k) % inner_count], "ctx", inner_shift(k))
+    own_grads = gathered[0] + lax.ppermute(gathered[1], "ctx", swap)
     tok_grads = lax.all_to_all(own_grads, "tp", split_axis=0, concat_axis=1, tiled=True)
     tok_grads = tok_grads.reshape(kv_rows, -1, 2, head_size)
     k_grad_tokens = tok_grads[:, :, 0, :].reshape(kv_rows, -1)

time: 213 us -> 135 us (0.63)
  waiting for transfers between devices: 99.2 us -> 34.1 us
  blocking collectives: 41.5 us -> 0 us
  starting transfers between devices: 29.4 us -> 62.2 us
  between operations: 16.2 us -> 3.08 us
  local copies, waits for them, and re-layouts: 10.9 us -> 17.3 us
    reduce_scatter x1 -> x0, waiting for transfers between devices: 90.8 us -> none  [body(): lax.psum_scatter(grad_terms, 'ctx', scatter_dimension=0, tiled=True)]
    all_gather x1 -> x0, blocking collectives: 41.5 us -> none  [body(): kv_full = lax.all_gather(kv_tok, 'ctx', axis=0, tiled=True)]
    ppermute x0 -> x8, starting transfers between devices: none -> 35.5 us  [the longest x1 10.4 us: body(): own_grads = gathered[0] + lax.ppermute(gathered[1], 'ctx', swap)]
    ppermute x0 -> x8, waiting for transfers between devices: none -> 25.9 us  [the longest x3 12.2 us: body(): lax.ppermute(grad_terms[-k % inner_count], 'ctx', inner_shift(k))]
    squeeze x0 -> x5, local copies, waits for them, and re-layouts: none -> 4.39 us  [the longest x3 4.09 us: body(): grad_terms[-k % inner_count]]
    all_to_all x1, starting transfers between devices: 6.96 us -> 3.77 us  [body(): lax.all_to_all(own_grads, 'tp', split_axis=0, concat_axis=1, tiled=True)]
    slice x0 -> x5, local copies, waits for them, and re-layouts: none -> 2.54 us  [the longest x3 1.29 us: body(): grad_terms[-k % inner_count]]
  transfers between devices with their start and end apart: 6 -> 13, of which waited for: 4 -> 9; matrix products, arithmetic and copies ran while one was open for 5% -> 12% of each run, Pallas kernels for 0% -> 0%
where the time goes in v2:
time: 135 us
  starting transfers between devices  62.2 us (46%)
  waiting for transfers between devices  34.1 us (25%)
  local copies, waits for them, and re-layouts  17.3 us (13%)
  matrix products  13.1 us (10%)
  other arithmetic  4.74 us (4%)
  between operations  3.08 us (2%)
    ppermute x3, starting transfers between devices, passed_along(): return lax.ppermute(block, axis, route)  15.5 us
    ppermute x3, waiting for transfers between devices, body(): lax.ppermute(grad_terms[-k % inner_count], 'ctx', inner_shift(k))  12.2 us
    ppermute x1, starting transfers between devices, body(): own_grads = gathered[0] + lax.ppermute(gathered[1], 'ctx', swap)  10.4 us
    ppermute x3, starting transfers between devices, body(): lax.ppermute(grad_terms[-k % inner_count], 'ctx', inner_shift(k))  9.89 us
    ppermute x3, starting transfers between devices, body(): lax.ppermute(pair, 'ctx', inner_shift(k))  9.33 us
    all_to_all x1, starting transfers between devices, body(): lax.all_to_all(kv_rows_in, 'tp', split_axis=1, concat_axis=0, tiled=True)  7.47 us
    ppermute x1, waiting for transfers between devices, body(): own_grads = gathered[0] + lax.ppermute(gathered[1], 'ctx', swap)  6.86 us
    ppermute x1, starting transfers between devices, body(): partner = lax.ppermute(kv_tok, 'ctx', swap)  5.88 us
  transfers between devices with their start and end apart: 13, of which 9 were waited for; matrix products, arithmetic and copies ran while one was open for 12% of the time, Pallas kernels for 0%

profile of v2, /device:TPU:1, one launch (start us, length us, event | category | flops | bytes accessed | tf_op | source)
XLA Modules:
  0.0 134.6 jit_solution(10313098276582439752)
XLA Ops:
  0.6 11.6 %collective-permute-start.6 = (bf16[176,1024]{1,0:T(8,128)(2,1)}, bf16[176,1024]{1,0:T(8,128)(2,1)S(1)}, u32[]{:S(2)}, u32[]{:S(2)}) collective-permute-start(bf16[176,1024]{1,0:T(8,128)(2,1)} %bitcast.183), channel_id=1, source_target_pairs={{64,0},{128,64},{192,128},{256,192},{320,256},{384,320},{448,384},... | collective-permute-start | bytes 1081352 | tf_op jit(solution)/shard_map/ppermute | solution.py:16
  12.3 1.2 dynamic_slice.19
  15.5 1.5 %dynamic-slice_reduce_fusion = (bf16[22,1024]{1,0:T(8,128)(2,1)S(1)}, bf16[22,1024]{1,0:T(8,128)(2,1)S(1)}) fusion(bf16[1,2,22,1024]{3,1,2,0:T(2,128)(2,1)} %param.10, s32[]{:T(128)S(6)} %select_n.91, bf16[1,2,22,1024]{3,1,2,0:T(2,128)(2,1)} %param.9), kind=kLoop, calls=%fused_computation.51 | loop fusion | bytes 180228 | tf_op jit(solution)/shard_map/jit(dynamic_index_in_dim)/dynamic_slice | solution.py:39
  17.2 1.9 %collective-permute-start = (bf16[22,2048]{1,0:T(8,128)(2,1)S(1)}, bf16[22,2048]{1,0:T(8,128)(2,1)S(1)}, u32[]{:S(2)}, u32[]{:S(2)}) collective-permute-start(bf16[22,2048]{1,0:T(8,128)(2,1)S(1)} %reshape.263), channel_id=1, source_target_pairs={{448,0},{0,64},{64,128},{128,192},{192,256},{256,320},{320,384},{3... | collective-permute-start | bytes 270344 | tf_op jit(solution)/shard_map/ppermute | solution.py:16
  19.1 1.9 %collective-permute-start.5 = (bf16[176,1024]{1,0:T(8,128)(2,1)S(1)}, bf16[176,1024]{1,0:T(8,128)(2,1)S(1)}, u32[]{:S(2)}, u32[]{:S(2)}) collective-permute-start(bf16[176,1024]{1,0:T(8,128)(2,1)S(1)} %dynamic-slice_bitcast_fusion), channel_id=1, source_target_pairs={{448,0},{0,64},{64,128},{128,192},{192,256},{256,320},{320,384},{3... | collective-permute-start | bytes 1081352 | tf_op jit(solution)/shard_map/ppermute | solution.py:16
  21.4 0.7 broadcast_multiply_fusion
  22.4 0.6 gather_fusion
  23.0 0.8 collective-permute-done
  23.8 0.7 copy.32
  24.4 7.5 %all-to-all-start = ((bf16[22,8,256]{2,0,1:T(8,128)(2,1)}), bf16[22,8,256]{2,0,1:T(8,128)(2,1)S(1)}, u32[]{:S(2)}, u32[]{:S(2)}) async-start(bf16[22,8,256]{2,0,1:T(8,128)(2,1)} %copy.32), calls=%async_computation | async-start | bytes 196608 | tf_op jit(solution)/shard_map/all_to_all | solution.py:46
  32.1 5.2 %all-to-all-done = bf16[22,8,256]{2,0,1:T(8,128)(2,1)S(1)} async-done(((bf16[22,8,256]{2,0,1:T(8,128)(2,1)}), bf16[22,8,256]{2,0,1:T(8,128)(2,1)S(1)}, u32[]{:S(2)}, u32[]{:S(2)}) %all-to-all-start) | async-done | bytes 90144 | tf_op jit(solution)/shard_map/all_to_all | solution.py:46
  37.3 5.9 %collective-permute-start.1 = (bf16[176,256]{1,0:T(8,128)(2,1)S(1)}, bf16[176,256]{1,0:T(8,128)(2,1)S(1)}, u32[]{:S(2)}, u32[]{:S(2)}) collective-permute-start(bf16[176,256]{1,0:T(8,128)(2,1)S(1)} %all_to_all.29), channel_id=1, source_target_pairs={{0,32},{8,40},{16,48},{24,56},{32,0},{40,8},{48,16},{56,24},{1,33}... | collective-permute-start | bytes 270344 | tf_op jit(solution)/shard_map/ppermute | solution.py:61
  43.4 3.1 %collective-permute-done.1 = bf16[176,256]{1,0:T(8,128)(2,1)S(1)} collective-permute-done((bf16[176,256]{1,0:T(8,128)(2,1)S(1)}, bf16[176,256]{1,0:T(8,128)(2,1)S(1)}, u32[]{:S(2)}, u32[]{:S(2)}) %collective-permute-start.1) | collective-permute-done | bytes 90144 | tf_op jit(solution)/shard_map/ppermute | solution.py:61
  46.6 4.4 %collective-permute-start.4 = (bf16[2,176,256]{2,1,0:T(8,128)(2,1)S(1)}, bf16[2,176,256]{2,1,0:T(8,128)(2,1)S(1)}, u32[]{:S(2)}, u32[]{:S(2)}) collective-permute-start(bf16[2,176,256]{2,1,0:T(8,128)(2,1)S(1)} %get-tuple-element.19), channel_id=1, source_target_pairs={{0,24},{8,0},{16,8},{24,16},{32,56},{40,32},{48,40},{56,48},{1,25}... | collective-permute-start | bytes 540680 | tf_op jit(solution)/shard_map/ppermute | solution.py:63
  51.0 2.4 %collective-permute-start.3 = (bf16[2,176,256]{2,1,0:T(8,128)(2,1)S(1)}, bf16[2,176,256]{2,1,0:T(8,128)(2,1)S(1)}, u32[]{:S(2)}, u32[]{:S(2)}) collective-permute-start(bf16[2,176,256]{2,1,0:T(8,128)(2,1)S(1)} %get-tuple-element.19), channel_id=1, source_target_pairs={{0,16},{8,24},{16,0},{24,8},{32,48},{40,56},{48,32},{56,40},{1,17}... | collective-permute-start | bytes 540680 | tf_op jit(solution)/shard_map/ppermute | solution.py:63
  53.4 2.5 %collective-permute-start.2 = (bf16[2,176,256]{2,1,0:T(8,128)(2,1)S(1)}, bf16[2,176,256]{2,1,0:T(8,128)(2,1)S(1)}, u32[]{:S(2)}, u32[]{:S(2)}) collective-permute-start(bf16[2,176,256]{2,1,0:T(8,128)(2,1)S(1)} %get-tuple-element.19), channel_id=1, source_target_pairs={{0,8},{8,16},{16,24},{24,0},{32,40},{40,48},{48,56},{56,32},{1,9},... | collective-permute-start | bytes 540680 | tf_op jit(solution)/shard_map/ppermute | solution.py:63
  56.0 1.0 copy.57
  57.1 1.6 %collective-permute-done.3 = bf16[2,176,256]{2,1,0:T(8,128)(2,1)S(1)} collective-permute-done((bf16[2,176,256]{2,1,0:T(8,128)(2,1)S(1)}, bf16[2,176,256]{2,1,0:T(8,128)(2,1)S(1)}, u32[]{:S(2)}, u32[]{:S(2)}) %collective-permute-start.3) | collective-permute-done | bytes 180256 | tf_op jit(solution)/shard_map/ppermute | solution.py:63
  58.7 2.1 %collective-permute-done.2 = bf16[2,176,256]{2,1,0:T(8,128)(2,1)S(1)} collective-permute-done((bf16[2,176,256]{2,1,0:T(8,128)(2,1)S(1)}, bf16[2,176,256]{2,1,0:T(8,128)(2,1)S(1)}, u32[]{:S(2)}, u32[]{:S(2)}) %collective-permute-start.2) | collective-permute-done | bytes 180256 | tf_op jit(solution)/shard_map/ppermute | solution.py:63
  61.2 1.1 fusion.38
  62.2 1.9 %fusion.40 = (f32[8,176]{1,0:T(8,128)S(1)}, f32[1,8,176,1408]{3,2,1,0:T(8,128)S(1)}) fusion(bf16[1408,1,1,128]{3,2,0,1:T(2,128)(2,1)S(1)} %get-tuple-element.15, pred[176,1408]{1,0:T(8,128)(4,1)S(1)} %broadcast_compare_fusion, bf16[176,1024]{1,0:T(8,128)(2,1)S(1)} %collective-permute-done.5), kind=kOutput, calls=%fused_computation.80 | convolution fusion | flops 513456768 | bytes 8904192 | tf_op jit(solution)/shard_map/qgjd,kgd->gjqk/dot_general | solution.py:82
  64.1 2.0 %select_reduce_fusion = f32[8,176]{1,0:T(8,128)S(1)} fusion(f32[1,8,176,1408]{3,2,1,0:T(8,128)S(1)} %get-tuple-element.21, f32[8,176]{1,0:T(8,128)S(1)} %get-tuple-element.20, pred[176,1408]{1,0:T(8,128)(4,1)S(1)} %broadcast_compare_fusion), kind=kLoop, calls=%fused_computation.6 | loop fusion | flops 5945984 | bytes 8188928 | tf_op jit(solution)/shard_map/reduce_sum | solution.py:85
  66.2 2.5 %fusion.18 = (f32[176,8]{0,1:T(8,128)S(1)}, bf16[176,1,8,128]{3,0,2,1:T(8,128)(2,1)}) fusion(f32[176,1,8,128]{3,2,0,1:T(8,128)S(1)} %bitcast.166, f32[1,8,176,1408]{3,2,1,0:T(8,128)S(1)} %get-tuple-element.21, f32[8,176]{1,0:T(8,128)S(1)} %log_add_fusion, pred[176,1408]{1,0:T(8,128)(4,1)S(1)} %broadcast_compare_fusion, ...), kind=kOutput, calls=%fused_computation.28 | convolution fusion | flops 513997440 | bytes 9630720 | tf_op jit(solution)/shard_map/gjqk,kgd->qgjd/dot_general | solution.py:89
  68.7 2.9 %fusion.6 = bf16[8,176,1408]{2,1,0:T(8,128)(2,1)S(1)} fusion(f32[8,176]{1,0:T(8,128)S(1)} %bitcast.181, f32[1,8,176,1408]{3,2,1,0:T(8,128)S(1)} %get-tuple-element.21, f32[8,176]{1,0:T(8,128)S(1)} %log_add_fusion, pred[176,1408]{1,0:T(8,128)(4,1)S(1)} %broadcast_compare_fusion, bf16[1408,1,1,128]{3,2,0,1:T(2,128)(2,1)S(1)} %get-tuple-element.14, ...), kind=kOutput, calls=%fused_computation.11 | convolution fusion | flops 517423104 | bytes 12874752 | tf_op jit(solution)/shard_map/qgjd,kgd->gjqk/dot_general | solution.py:93
  71.6 0.9 fusion.13
  72.5 1.7 %convolution_bitcast_fusion = f32[1408,1,1,128]{0,3,2,1:T(8,128)S(1)} fusion(f32[1,8,176,1408]{3,2,1,0:T(8,128)S(1)} %get-tuple-element.21, f32[8,176]{1,0:T(8,128)S(1)} %log_add_fusion, pred[176,1408]{1,0:T(8,128)(4,1)S(1)} %broadcast_compare_fusion, bf16[176,1024]{1,0:T(8,128)(2,1)S(1)} %collective-permute-done.6), kind=kOutput, calls=%fused_computation.12 | convolution fusion | flops 513458176 | bytes 9264640 | tf_op jit(solution)/shard_map/gjqk,qgjd->kgd/dot_general | solution.py:99
  74.1 0.4 fusion.23
  74.5 0.9 copy.46
  75.4 2.0 %squeeze.45 = f32[2,176,256]{2,1,0:T(8,128)} reshape(f32[352,1,2,128]{3,2,0,1:T(2,128)} %copy.46) | data formatting | bytes 720896 | tf_op jit(solution)/shard_map/squeeze | solution.py:108
  77.4 2.3 %collective-permute-start.9 = (f32[2,176,256]{2,1,0:T(8,128)}, f32[2,176,256]{2,1,0:T(8,128)S(1)}, u32[]{:S(2)}, u32[]{:S(2)}) collective-permute-start(f32[2,176,256]{2,1,0:T(8,128)} %squeeze.45), channel_id=1, source_target_pairs={{0,24},{8,0},{16,8},{24,16},{32,56},{40,32},{48,40},{56,48},{1,25}... | collective-permute-start | bytes 1081352 | tf_op jit(solution)/shard_map/ppermute | solution.py:108
  79.9 1.0 squeeze.44
  80.9 4.9 %collective-permute-start.8 = (f32[2,176,256]{2,1,0:T(8,128)}, f32[2,176,256]{2,1,0:T(8,128)S(1)}, u32[]{:S(2)}, u32[]{:S(2)}) collective-permute-start(f32[2,176,256]{2,1,0:T(8,128)} %squeeze.44), channel_id=1, source_target_pairs={{0,16},{8,24},{16,0},{24,8},{32,48},{40,56},{48,32},{56,40},{1,17}... | collective-permute-start | bytes 1081352 | tf_op jit(solution)/shard_map/ppermute | solution.py:108
  86.0 1.1 squeeze.43
  87.0 2.7 %collective-permute-start.7 = (f32[2,176,256]{2,1,0:T(8,128)}, f32[2,176,256]{2,1,0:T(8,128)}, u32[]{:S(2)}, u32[]{:S(2)}) collective-permute-start(f32[2,176,256]{2,1,0:T(8,128)} %squeeze.43), channel_id=1, source_target_pairs={{0,8},{8,16},{16,24},{24,0},{32,40},{40,48},{48,56},{56,32},{1,9},... | collective-permute-start | bytes 1081352 | tf_op jit(solution)/shard_map/ppermute | solution.py:108
  90.0 0.3 squeeze.42
  90.3 0.5 collective-permute-done.8
  90.8 11.7 %collective-permute-done.7 = f32[2,176,256]{2,1,0:T(8,128)} collective-permute-done((f32[2,176,256]{2,1,0:T(8,128)}, f32[2,176,256]{2,1,0:T(8,128)}, u32[]{:S(2)}, u32[]{:S(2)}) %collective-permute-start.7) | collective-permute-done | bytes 360480 | tf_op jit(solution)/shard_map/ppermute | solution.py:108
  102.5 1.1 add_add_fusion
  103.6 10.4 %collective-permute-start.10 = (f32[176,256]{1,0:T(8,128)S(1)}, f32[176,256]{1,0:T(8,128)S(1)}, u32[]{:S(2)}, u32[]{:S(2)}) collective-permute-start(f32[176,256]{1,0:T(8,128)S(1)} %slice_bitcast_fusion), channel_id=1, source_target_pairs={{0,32},{8,40},{16,48},{24,56},{32,0},{40,8},{48,16},{56,24},{1,33}... | collective-permute-start | bytes 540680 | tf_op jit(solution)/shard_map/ppermute | solution.py:109
  114.0 1.1 copy.36
  115.1 0.9 broadcast_in_dim_reshape.7
  116.0 6.9 %collective-permute-done.10 = f32[176,256]{1,0:T(8,128)S(1)} collective-permute-done((f32[176,256]{1,0:T(8,128)S(1)}, f32[176,256]{1,0:T(8,128)S(1)}, u32[]{:S(2)}, u32[]{:S(2)}) %collective-permute-start.10) | collective-permute-done | bytes 180256 | tf_op jit(solution)/shard_map/ppermute | solution.py:109
  122.8 0.7 all_to_all.30
  123.5 3.8 %all-to-all-start.1 = ((f32[8,22,256]{2,1,0:T(8,128)}), f32[8,22,256]{2,1,0:T(8,128)S(1)}, u32[]{:S(2)}, u32[]{:S(2)}) async-start(f32[8,22,256]{2,1,0:T(8,128)} %all_to_all.30), calls=%async_computation.1 | async-start | bytes 393216 | tf_op jit(solution)/shard_map/all_to_all | solution.py:110
  127.3 3.3 %fusion.17 = bf16[176,1,8,128]{3,0,2,1:T(8,128)(2,1)S(1)} fusion(bf16[8,176,1408]{2,1,0:T(8,128)(2,1)} %copy-done.1, bf16[1408,1,1,128]{3,2,0,1:T(2,128)(2,1)S(1)} %get-tuple-element.15), kind=kOutput, calls=%fused_computation.25 | convolution fusion | flops 507871232 | bytes 4685824 | tf_op jit(solution)/shard_map/gjqk,kgd->qgjd/dot_general | solution.py:96
  130.7 0.9 broadcast_in_dim_reshape.8
  131.6 2.2 %all-to-all-done.1 = f32[8,22,256]{2,1,0:T(8,128)S(1)} async-done(((f32[8,22,256]{2,1,0:T(8,128)}), f32[8,22,256]{2,1,0:T(8,128)S(1)}, u32[]{:S(2)}, u32[]{:S(2)}) %all-to-all-start.1) | async-done | bytes 180256 | tf_op jit(solution)/shard_map/all_to_all | solution.py:110
  133.9 0.7 fusion.39
  (53 shorter events, 2.5 us)
Async XLA Ops:
  0.6 18.5 %copy-start = (bf16[1,2,176,1024]{3,2,1,0:T(8,128)(2,1)S(1)}, bf16[1,2,176,1024]{3,2,1,0:T(8,128)(2,1)}, u32[]{:S(2)}) copy-start(bf16[1,2,176,1024]{3,2,1,0:T(8,128)(2,1)} %param.8) | copy-start | bytes 2162692
  0.6 55.3 %collective-permute-start.6 = (bf16[176,1024]{1,0:T(8,128)(2,1)}, bf16[176,1024]{1,0:T(8,128)(2,1)S(1)}, u32[]{:S(2)}, u32[]{:S(2)}) collective-permute-start(bf16[176,1024]{1,0:T(8,128)(2,1)} %bitcast.183), channel_id=1, source_target_pairs={{64,0},{128,64},{192,128},{256,192},{320,256},{384,320},{448,384},... | collective-permute-start | bytes 1081352 | tf_op jit(solution)/shard_map/ppermute | solution.py:16
  17.2 6.6 %collective-permute-start = (bf16[22,2048]{1,0:T(8,128)(2,1)S(1)}, bf16[22,2048]{1,0:T(8,128)(2,1)S(1)}, u32[]{:S(2)}, u32[]{:S(2)}) collective-permute-start(bf16[22,2048]{1,0:T(8,128)(2,1)S(1)} %reshape.263), channel_id=1, source_target_pairs={{448,0},{0,64},{64,128},{128,192},{192,256},{256,320},{320,384},{3... | collective-permute-start | bytes 270344 | tf_op jit(solution)/shard_map/ppermute | solution.py:16
  19.1 37.9 %collective-permute-start.5 = (bf16[176,1024]{1,0:T(8,128)(2,1)S(1)}, bf16[176,1024]{1,0:T(8,128)(2,1)S(1)}, u32[]{:S(2)}, u32[]{:S(2)}) collective-permute-start(bf16[176,1024]{1,0:T(8,128)(2,1)S(1)} %dynamic-slice_bitcast_fusion), channel_id=1, source_target_pairs={{448,0},{0,64},{64,128},{128,192},{192,256},{256,320},{320,384},{3... | collective-permute-start | bytes 1081352 | tf_op jit(solution)/shard_map/ppermute | solution.py:16
  24.4 12.8 %all-to-all-start = ((bf16[22,8,256]{2,0,1:T(8,128)(2,1)}), bf16[22,8,256]{2,0,1:T(8,128)(2,1)S(1)}, u32[]{:S(2)}, u32[]{:S(2)}) async-start(bf16[22,8,256]{2,0,1:T(8,128)(2,1)} %copy.32), calls=%async_computation | async-start | bytes 196608 | tf_op jit(solution)/shard_map/all_to_all | solution.py:46
  37.3 9.3 %collective-permute-start.1 = (bf16[176,256]{1,0:T(8,128)(2,1)S(1)}, bf16[176,256]{1,0:T(8,128)(2,1)S(1)}, u32[]{:S(2)}, u32[]{:S(2)}) collective-permute-start(bf16[176,256]{1,0:T(8,128)(2,1)S(1)} %all_to_all.29), channel_id=1, source_target_pairs={{0,32},{8,40},{16,48},{24,56},{32,0},{40,8},{48,16},{56,24},{1,33}... | collective-permute-start | bytes 270344 | tf_op jit(solution)/shard_map/ppermute | solution.py:61
  46.6 10.5 %collective-permute-start.4 = (bf16[2,176,256]{2,1,0:T(8,128)(2,1)S(1)}, bf16[2,176,256]{2,1,0:T(8,128)(2,1)S(1)}, u32[]{:S(2)}, u32[]{:S(2)}) collective-permute-start(bf16[2,176,256]{2,1,0:T(8,128)(2,1)S(1)} %get-tuple-element.19), channel_id=1, source_target_pairs={{0,24},{8,0},{16,8},{24,16},{32,56},{40,32},{48,40},{56,48},{1,25}... | collective-permute-start | bytes 540680 | tf_op jit(solution)/shard_map/ppermute | solution.py:63
  51.0 7.7 %collective-permute-start.3 = (bf16[2,176,256]{2,1,0:T(8,128)(2,1)S(1)}, bf16[2,176,256]{2,1,0:T(8,128)(2,1)S(1)}, u32[]{:S(2)}, u32[]{:S(2)}) collective-permute-start(bf16[2,176,256]{2,1,0:T(8,128)(2,1)S(1)} %get-tuple-element.19), channel_id=1, source_target_pairs={{0,16},{8,24},{16,0},{24,8},{32,48},{40,56},{48,32},{56,40},{1,17}... | collective-permute-start | bytes 540680 | tf_op jit(solution)/shard_map/ppermute | solution.py:63
  53.4 7.4 %collective-permute-start.2 = (bf16[2,176,256]{2,1,0:T(8,128)(2,1)S(1)}, bf16[2,176,256]{2,1,0:T(8,128)(2,1)S(1)}, u32[]{:S(2)}, u32[]{:S(2)}) collective-permute-start(bf16[2,176,256]{2,1,0:T(8,128)(2,1)S(1)} %get-tuple-element.19), channel_id=1, source_target_pairs={{0,8},{8,16},{16,24},{24,0},{32,40},{40,48},{48,56},{56,32},{1,9},... | collective-permute-start | bytes 540680 | tf_op jit(solution)/shard_map/ppermute | solution.py:63
  62.2 4.0 %copy-start.2 = (f32[22,8,8,128]{3,2,1,0:T(8,128)S(1)}, f32[22,8,8,128]{3,2,1,0:T(8,128)}, u32[]{:S(2)}) copy-start(f32[22,8,8,128]{3,2,1,0:T(8,128)} %copy.57) | copy-start | bytes 2162692
  71.6 2.5 %copy-start.1 = (bf16[8,176,1408]{2,1,0:T(8,128)(2,1)}, bf16[8,176,1408]{2,1,0:T(8,128)(2,1)S(1)}, u32[]{:S(2)}) copy-start(bf16[8,176,1408]{2,1,0:T(8,128)(2,1)S(1)} %fusion.6) | copy-start | bytes 11894788
  77.4 12.9 %collective-permute-start.9 = (f32[2,176,256]{2,1,0:T(8,128)}, f32[2,176,256]{2,1,0:T(8,128)S(1)}, u32[]{:S(2)}, u32[]{:S(2)}) collective-permute-start(f32[2,176,256]{2,1,0:T(8,128)} %squeeze.45), channel_id=1, source_target_pairs={{0,24},{8,0},{16,8},{24,16},{32,56},{40,32},{48,40},{56,48},{1,25}... | collective-permute-start | bytes 1081352 | tf_op jit(solution)/shard_map/ppermute | solution.py:108
  80.9 9.9 %collective-permute-start.8 = (f32[2,176,256]{2,1,0:T(8,128)}, f32[2,176,256]{2,1,0:T(8,128)S(1)}, u32[]{:S(2)}, u32[]{:S(2)}) collective-permute-start(f32[2,176,256]{2,1,0:T(8,128)} %squeeze.44), channel_id=1, source_target_pairs={{0,16},{8,24},{16,0},{24,8},{32,48},{40,56},{48,32},{56,40},{1,17}... | collective-permute-start | bytes 1081352 | tf_op jit(solution)/shard_map/ppermute | solution.py:108
  87.0 15.4 %collective-permute-start.7 = (f32[2,176,256]{2,1,0:T(8,128)}, f32[2,176,256]{2,1,0:T(8,128)}, u32[]{:S(2)}, u32[]{:S(2)}) collective-permute-start(f32[2,176,256]{2,1,0:T(8,128)} %squeeze.43), channel_id=1, source_target_pairs={{0,8},{8,16},{16,24},{24,0},{32,40},{40,48},{48,56},{56,32},{1,9},... | collective-permute-start | bytes 1081352 | tf_op jit(solution)/shard_map/ppermute | solution.py:108
  103.6 19.2 %collective-permute-start.10 = (f32[176,256]{1,0:T(8,128)S(1)}, f32[176,256]{1,0:T(8,128)S(1)}, u32[]{:S(2)}, u32[]{:S(2)}) collective-permute-start(f32[176,256]{1,0:T(8,128)S(1)} %slice_bitcast_fusion), channel_id=1, source_target_pairs={{0,32},{8,40},{16,48},{24,56},{32,0},{40,8},{48,16},{56,24},{1,33}... | collective-permute-start | bytes 540680 | tf_op jit(solution)/shard_map/ppermute | solution.py:109
  123.5 10.3 %all-to-all-start.1 = ((f32[8,22,256]{2,1,0:T(8,128)}), f32[8,22,256]{2,1,0:T(8,128)S(1)}, u32[]{:S(2)}, u32[]{:S(2)}) async-start(f32[8,22,256]{2,1,0:T(8,128)} %all_to_all.30), calls=%async_computation.1 | async-start | bytes 393216 | tf_op jit(solution)/shard_map/all_to_all | solution.py:110

commit v3 on v1

--- a/solution.py
+++ b/solution.py
@@ -42,17 +42,22 @@
     queries, kv_rows_in = passed_along((q_send, kv_send), "section", 1)
     cotangent = passed_along(grad_out[0], "section", -1)
 
-    kv_tok = lax.all_to_all(kv_rows_in, "tp", split_axis=1, concat_axis=0, tiled=True)
-    kv_full = lax.all_gather(kv_tok, "ctx", axis=0, tiled=True)
+    plane = ("ctx", "tp")
+    kv_pieces = kv_rows_in.reshape(1, kv_rows, tp_count, 2 * kv_width).transpose(0, 2, 1, 3)
+    kv_pieces = jnp.broadcast_to(kv_pieces, (ctx_count, tp_count, kv_rows, 2 * kv_width))
+    kv_pieces = kv_pieces.reshape(ctx_count * tp_count * kv_rows, 2 * kv_width)
+    kv_full = lax.all_to_all(kv_pieces, plane, split_axis=0, concat_axis=0, tiled=True)
     kv_full = kv_full.reshape(seq_rows, kv_local, 2, head_size)
     key_heads = kv_full[:, :, 0, :]
     value_heads = kv_full[:, :, 1, :]
+    ctx_rank = lax.axis_index("ctx")
 
     positions = (
         block_order[:, None] * block_len + jnp.arange(block_len, dtype=jnp.int32)[None, :]
-    ).reshape(seq_rows)
-    query_pos = lax.dynamic_slice_in_dim(positions, lax.axis_index("ctx") * tok_rows, tok_rows)
-    visible = (positions[None, :] <= query_pos[:, None])[None, None]
+    ).reshape(ctx_count, tok_rows)
+    key_pos = positions.reshape(seq_rows)
+    query_pos = lax.dynamic_index_in_dim(positions, ctx_rank, 0, keepdims=False)
+    visible = (key_pos[None, :] <= query_pos[:, None])[None, None]
 
     q4 = queries.reshape(tok_rows, kv_local, group, head_size)
     do4 = cotangent.reshape(tok_rows, kv_local, group, head_size)
@@ -78,11 +83,11 @@
     attended_flat = attended.astype(jnp.bfloat16).reshape(tok_rows, heads_local * head_size)
     q_grad_flat = q_grad.reshape(tok_rows, heads_local * head_size)
     grad_terms = jnp.stack([key_grad, value_grad], axis=2).reshape(seq_rows, 2 * kv_width)
-    own_grads = lax.psum_scatter(grad_terms, "ctx", scatter_dimension=0, tiled=True)
-    tok_grads = lax.all_to_all(own_grads, "tp", split_axis=0, concat_axis=1, tiled=True)
-    tok_grads = tok_grads.reshape(kv_rows, -1, 2, head_size)
-    k_grad_tokens = tok_grads[:, :, 0, :].reshape(kv_rows, -1)
-    v_grad_tokens = tok_grads[:, :, 1, :].reshape(kv_rows, -1)
+    grad_parts = lax.all_to_all(grad_terms, plane, split_axis=0, concat_axis=0, tiled=True)
+    grad_parts = grad_parts.reshape(ctx_count, tp_count, kv_rows, kv_local, 2, head_size)
+    own_grads = jnp.sum(grad_parts, axis=0)
+    k_grad_tokens = own_grads[:, :, :, 0, :].transpose(1, 0, 2, 3).reshape(kv_rows, -1)
+    v_grad_tokens = own_grads[:, :, :, 1, :].transpose(1, 0, 2, 3).reshape(kv_rows, -1)
     return (attended_flat[None], q_grad_flat[None], k_grad_tokens[None], v_grad_tokens[None])
 
 

time: 213 us -> 125 us (0.59)
  waiting for transfers between devices: 99.2 us -> 51.7 us
  blocking collectives: 41.5 us -> 0 us
  between operations: 16.2 us -> 2.91 us
  local copies, waits for them, and re-layouts: 10.9 us -> 18.6 us
  starting transfers between devices: 29.4 us -> 31.6 us
    reduce_scatter x1 -> x0, waiting for transfers between devices: 90.8 us -> none  [body(): lax.psum_scatter(grad_terms, 'ctx', scatter_dimension=0, tiled=True)]
    all_gather x1 -> x0, blocking collectives: 41.5 us -> none  [body(): kv_full = lax.all_gather(kv_tok, 'ctx', axis=0, tiled=True)]
    all_to_all x2, waiting for transfers between devices: 7.36 us -> 43 us  [the longest x1 32.7 us: body(): lax.all_to_all(grad_terms, plane, split_axis=0, concat_axis=0, tiled=True)]
    ppermute x3, waiting for transfers between devices: 1.04 us -> 8.77 us  [passed_along(): return lax.ppermute(block, axis, route)]
    another operation x0 -> x2, local copies, waits for them, and re-layouts: none -> 2.96 us  [the longest x1 2.15 us: body(): jnp.stack([key_grad, value_grad], axis=2).reshape(seq_rows, 2 * kv_width)]
    all_to_all x2, starting transfers between devices: 13.9 us -> 16.3 us  [the longest x1 11.4 us: body(): lax.all_to_all(kv_pieces, plane, split_axis=0, concat_axis=0, tiled=True)]
  transfers between devices with their start and end apart: 6 -> 5, of which waited for: 4 -> 4; matrix products, arithmetic and copies ran while one was open for 5% -> 9% of each run, Pallas kernels for 0% -> 0%
where the time goes in v3:
time: 125 us; the launch traced here: 124 us
  waiting for transfers between devices  51.7 us (41%)
  starting transfers between devices  31.6 us (25%)
  local copies, waits for them, and re-layouts  18.6 us (15%)
  matrix products  14.1 us (11%)
  other arithmetic  5.03 us (4%)
  between operations  2.91 us (2%)
    all_to_all x1, waiting for transfers between devices, body(): lax.all_to_all(grad_terms, plane, split_axis=0, concat_axis=0, tiled=True)  32.7 us
    ppermute x3, starting transfers between devices, passed_along(): return lax.ppermute(block, axis, route)  15.3 us
    all_to_all x1, starting transfers between devices, body(): lax.all_to_all(kv_pieces, plane, split_axis=0, concat_axis=0, tiled=True)  11.4 us
    all_to_all x1, waiting for transfers between devices, body(): lax.all_to_all(kv_pieces, plane, split_axis=0, concat_axis=0, tiled=True)  10.3 us
    ppermute x3, waiting for transfers between devices, passed_along(): return lax.ppermute(block, axis, route)  8.77 us
    all_to_all x1, starting transfers between devices, body(): lax.all_to_all(grad_terms, plane, split_axis=0, concat_axis=0, tiled=True)  4.93 us
    dot_general x1, matrix products, body(): jnp.einsum('gjqk,kgd->qgjd', dscores, key_heads, preferred_element_type=j...  3.31 us
    all_to_all x1, local copies, waits for them, and re-layouts, body(): lax.all_to_all(grad_terms, plane, split_axis=0, concat_axis=0, tiled=True)  3.21 us
  transfers between devices with their start and end apart: 5, of which 4 were waited for; matrix products, arithmetic and copies ran while one was open for 9% of the time, Pallas kernels for 0%

profile of v3, /device:TPU:1, one launch (start us, length us, event | category | flops | bytes accessed | tf_op | source)
XLA Modules:
  0.0 124.1 jit_solution(16071574485957683344)
XLA Ops:
  0.6 0.0 copy-start
  0.7 1.3 %dynamic_slice.19 = s32[1]{0:T(128)} dynamic-slice(s32[8]{0:T(128)} %param.7, s32[]{:T(128)S(6)} %select_n.33), dynamic_slice_sizes={1} | dynamic-slice | bytes 12 | tf_op jit(solution)/shard_map/jit(dynamic_index_in_dim)/dynamic_slice | solution.py:35
  3.9 1.5 %dynamic-slice_reduce_fusion = (bf16[22,1024]{1,0:T(8,128)(2,1)S(1)}, bf16[22,1024]{1,0:T(8,128)(2,1)S(1)}) fusion(bf16[1,2,22,1024]{3,1,2,0:T(2,128)(2,1)} %param.10, s32[]{:T(128)S(6)} %select_n.34, bf16[1,2,22,1024]{3,1,2,0:T(2,128)(2,1)} %param.9), kind=kLoop, calls=%fused_computation.38 | loop fusion | bytes 180228 | tf_op jit(solution)/shard_map/jit(dynamic_index_in_dim)/dynamic_slice | solution.py:38
  5.5 0.1 copy.55
  5.6 4.8 %collective-permute-start = (bf16[22,2048]{1,0:T(8,128)(2,1)S(1)}, bf16[22,2048]{1,0:T(8,128)(2,1)S(1)}, u32[]{:S(2)}, u32[]{:S(2)}) collective-permute-start(bf16[22,2048]{1,0:T(8,128)(2,1)S(1)} %reshape.175), channel_id=1, source_target_pairs={{448,0},{0,64},{64,128},{128,192},{192,256},{256,320},{320,384},{3... | collective-permute-start | bytes 270344 | tf_op jit(solution)/shard_map/ppermute | solution.py:15
  10.4 8.6 %collective-permute-start.2 = (bf16[176,1024]{1,0:T(8,128)(2,1)}, bf16[176,1024]{1,0:T(8,128)(2,1)S(1)}, u32[]{:S(2)}, u32[]{:S(2)}) collective-permute-start(bf16[176,1024]{1,0:T(8,128)(2,1)} %bitcast.167), channel_id=1, source_target_pairs={{64,0},{128,64},{192,128},{256,192},{320,256},{384,320},{448,384},... | collective-permute-start | bytes 1081352 | tf_op jit(solution)/shard_map/ppermute | solution.py:15
  19.0 0.6 collective-permute-done
  19.6 0.9 broadcast_in_dim.37
  20.6 11.4 %all-to-all-start = ((bf16[64,22,256]{2,1,0:T(8,128)(2,1)}), bf16[64,22,256]{2,1,0:T(8,128)(2,1)S(1)}, u32[]{:S(2)}, u32[]{:S(2)}) async-start(bf16[64,22,256]{2,1,0:T(8,128)(2,1)} %bitcast.3), calls=%async_computation | async-start | bytes 1572864 | tf_op jit(solution)/shard_map/all_to_all | solution.py:49
  31.9 0.0 copy-done
  32.0 1.9 %collective-permute-start.1 = (bf16[176,1024]{1,0:T(8,128)(2,1)S(1)}, bf16[176,1024]{1,0:T(8,128)(2,1)S(1)}, u32[]{:S(2)}, u32[]{:S(2)}) collective-permute-start(bf16[176,1024]{1,0:T(8,128)(2,1)S(1)} %dynamic-slice_bitcast_fusion), channel_id=1, source_target_pairs={{448,0},{0,64},{64,128},{128,192},{192,256},{256,320},{320,384},{3... | collective-permute-start | bytes 1081352 | tf_op jit(solution)/shard_map/ppermute | solution.py:15
  33.9 0.7 broadcast_multiply_fusion
  34.6 0.1 add.73
  34.7 0.1 iota_add_fusion
  34.7 0.1 add.72
  34.8 0.1 add.74
  34.9 0.1 add.75
  35.0 0.1 add.77
  35.1 0.2 broadcast_compare_fusion
  35.3 0.0 collective-permute-done.2
  35.3 0.1 convert_bitcast_fusion
  35.4 1.0 copy.80
  36.4 8.2 %collective-permute-done.1 = bf16[176,1024]{1,0:T(8,128)(2,1)S(1)} collective-permute-done((bf16[176,1024]{1,0:T(8,128)(2,1)S(1)}, bf16[176,1024]{1,0:T(8,128)(2,1)S(1)}, u32[]{:S(2)}, u32[]{:S(2)}) %collective-permute-start.1) | collective-permute-done | bytes 360480 | tf_op jit(solution)/shard_map/ppermute | solution.py:15
  44.6 0.9 copy.81
  45.5 10.3 %all-to-all-done = bf16[64,22,256]{2,1,0:T(8,128)(2,1)S(1)} async-done(((bf16[64,22,256]{2,1,0:T(8,128)(2,1)}), bf16[64,22,256]{2,1,0:T(8,128)(2,1)S(1)}, u32[]{:S(2)}, u32[]{:S(2)}) %all-to-all-start) | async-done | bytes 720928 | tf_op jit(solution)/shard_map/all_to_all | solution.py:49
  55.8 0.3 reshape.177
  56.0 1.1 fusion.29
  57.1 2.9 %fusion.30 = (f32[8,176]{1,0:T(8,128)S(1)}, f32[1,8,176,1408]{3,2,1,0:T(8,128)S(1)}) fusion(bf16[1408,1,1,128]{3,2,0,1:T(2,128)(2,1)S(1)} %get-tuple-element.11, pred[176,1408]{1,0:T(8,128)(4,1)S(1)} %broadcast_compare_fusion, bf16[176,1024]{1,0:T(8,128)(2,1)} %copy-done.2), kind=kOutput, calls=%fused_computation.49 | convolution fusion | flops 513456768 | bytes 8904192 | tf_op jit(solution)/shard_map/qgjd,kgd->gjqk/dot_general | solution.py:64
  60.1 2.0 %select_reduce_fusion = f32[8,176]{1,0:T(8,128)S(1)} fusion(f32[1,8,176,1408]{3,2,1,0:T(8,128)S(1)} %get-tuple-element.15, f32[8,176]{1,0:T(8,128)S(1)} %get-tuple-element.14, pred[176,1408]{1,0:T(8,128)(4,1)S(1)} %broadcast_compare_fusion), kind=kLoop, calls=%fused_computation.5 | loop fusion | flops 5945984 | bytes 8188928 | tf_op jit(solution)/shard_map/reduce_sum | solution.py:67
  62.1 2.5 %fusion.18 = (f32[176,8]{0,1:T(8,128)S(1)}, bf16[176,1,8,128]{3,0,2,1:T(8,128)(2,1)}) fusion(f32[176,1,8,128]{3,2,0,1:T(8,128)S(1)} %bitcast.156, f32[1,8,176,1408]{3,2,1,0:T(8,128)S(1)} %get-tuple-element.15, f32[8,176]{1,0:T(8,128)S(1)} %log_add_fusion, pred[176,1408]{1,0:T(8,128)(4,1)S(1)} %broadcast_compare_fusion, ...), kind=kOutput, calls=%fused_computation.21 | convolution fusion | flops 513997440 | bytes 9630720 | tf_op jit(solution)/shard_map/gjqk,kgd->qgjd/dot_general | solution.py:71
  64.6 2.9 %fusion.6 = bf16[8,176,1408]{2,1,0:T(8,128)(2,1)S(1)} fusion(f32[8,176]{1,0:T(8,128)S(1)} %bitcast.165, f32[1,8,176,1408]{3,2,1,0:T(8,128)S(1)} %get-tuple-element.15, f32[8,176]{1,0:T(8,128)S(1)} %log_add_fusion, pred[176,1408]{1,0:T(8,128)(4,1)S(1)} %broadcast_compare_fusion, bf16[1408,1,1,128]{3,2,0,1:T(2,128)(2,1)S(1)} %get-tuple-element.10, ...), kind=kOutput, calls=%fused_computation.10 | convolution fusion | flops 517423104 | bytes 12874752 | tf_op jit(solution)/shard_map/qgjd,kgd->gjqk/dot_general | solution.py:75
  67.5 0.0 copy-start.1
  67.5 0.9 fusion.13
  68.4 1.7 %convolution_bitcast_fusion = f32[1408,1,1,128]{0,3,2,1:T(8,128)S(1)} fusion(f32[1,8,176,1408]{3,2,1,0:T(8,128)S(1)} %get-tuple-element.15, f32[8,176]{1,0:T(8,128)S(1)} %log_add_fusion, pred[176,1408]{1,0:T(8,128)(4,1)S(1)} %broadcast_compare_fusion, bf16[176,1024]{1,0:T(8,128)(2,1)S(1)} %collective-permute-done.2), kind=kOutput, calls=%fused_computation.11 | convolution fusion | flops 513458176 | bytes 9264640 | tf_op jit(solution)/shard_map/gjqk,qgjd->kgd/dot_general | solution.py:81
  70.1 0.1 pad_maximum_fusion
  70.2 2.2 %copy.67 = f32[1408,1,2,128]{3,2,0,1:T(2,128)} copy(f32[1408,1,2,128]{0,3,2,1:T(8,128)S(1)} %pad_maximum_fusion) | data formatting | bytes 2883584 | tf_op jit(solution)/shard_map/stack | solution.py:85
  72.3 3.2 %all_to_all.14 = f32[64,22,256]{2,1,0:T(8,128)} reshape(f32[1408,1,2,128]{3,2,0,1:T(2,128)} %copy.67) | data formatting | bytes 2883584 | tf_op jit(solution)/shard_map/all_to_all | solution.py:86
  75.5 4.9 %all-to-all-start.1 = ((f32[64,22,256]{2,1,0:T(8,128)}), f32[64,22,256]{2,1,0:T(8,128)S(1)}, u32[]{:S(2)}, u32[]{:S(2)}) async-start(f32[64,22,256]{2,1,0:T(8,128)} %all_to_all.14), calls=%async_computation.1 | async-start | bytes 3145728 | tf_op jit(solution)/shard_map/all_to_all | solution.py:86
  80.5 1.1 copy.60
  81.5 0.9 broadcast_in_dim_reshape.12
  82.4 3.3 %fusion.17 = bf16[176,1,8,128]{3,0,2,1:T(8,128)(2,1)S(1)} fusion(bf16[8,176,1408]{2,1,0:T(8,128)(2,1)} %copy-done.1, bf16[1408,1,1,128]{3,2,0,1:T(2,128)(2,1)S(1)} %get-tuple-element.11), kind=kOutput, calls=%fused_computation.19 | convolution fusion | flops 507871232 | bytes 4685824 | tf_op jit(solution)/shard_map/gjqk,kgd->qgjd/dot_general | solution.py:78
  85.8 0.1 copy.63
  85.9 0.9 broadcast_in_dim_reshape.13
  86.7 32.7 %all-to-all-done.1 = f32[64,22,256]{2,1,0:T(8,128)S(1)} async-done(((f32[64,22,256]{2,1,0:T(8,128)}), f32[64,22,256]{2,1,0:T(8,128)S(1)}, u32[]{:S(2)}, u32[]{:S(2)}) %all-to-all-start.1) | async-done | bytes 1441824 | tf_op jit(solution)/shard_map/all_to_all | solution.py:86
  119.4 1.9 %reshape.190 = f32[8,8,22,2,128]{4,3,2,1,0:T(2,128)} reshape(f32[64,22,256]{2,1,0:T(8,128)S(1)} %all-to-all-done.1) | data formatting | bytes 2883584 | tf_op jit(solution)/shard_map/reshape | solution.py:87
  121.3 1.9 %reduce_sum.34 = f32[8,22,2,128]{3,2,1,0:T(2,128)S(1)} reduce(f32[8,8,22,2,128]{4,3,2,1,0:T(2,128)} %reshape.190, f32[]{:T(128)} %constant.57.clone.1), dimensions={0}, to_apply=%region_3.4 | reduce | flops 315392 | bytes 1622020 | tf_op jit(solution)/shard_map/reduce_sum | solution.py:88
  123.2 0.1 copy.118
  123.3 0.8 slice_bitcast_fusion
  (20 shorter events, 0.2 us)
Async XLA Ops:
  0.6 31.3 %copy-start = (bf16[1,2,176,1024]{3,2,1,0:T(8,128)(2,1)S(1)}, bf16[1,2,176,1024]{3,2,1,0:T(8,128)(2,1)}, u32[]{:S(2)}) copy-start(bf16[1,2,176,1024]{3,2,1,0:T(8,128)(2,1)} %param.8) | copy-start | bytes 2162692
  5.6 14.0 %collective-permute-start = (bf16[22,2048]{1,0:T(8,128)(2,1)S(1)}, bf16[22,2048]{1,0:T(8,128)(2,1)S(1)}, u32[]{:S(2)}, u32[]{:S(2)}) collective-permute-start(bf16[22,2048]{1,0:T(8,128)(2,1)S(1)} %reshape.175), channel_id=1, source_target_pairs={{448,0},{0,64},{64,128},{128,192},{192,256},{256,320},{320,384},{3... | collective-permute-start | bytes 270344 | tf_op jit(solution)/shard_map/ppermute | solution.py:15
  10.4 24.9 %collective-permute-start.2 = (bf16[176,1024]{1,0:T(8,128)(2,1)}, bf16[176,1024]{1,0:T(8,128)(2,1)S(1)}, u32[]{:S(2)}, u32[]{:S(2)}) collective-permute-start(bf16[176,1024]{1,0:T(8,128)(2,1)} %bitcast.167), channel_id=1, source_target_pairs={{64,0},{128,64},{192,128},{256,192},{320,256},{384,320},{448,384},... | collective-permute-start | bytes 1081352 | tf_op jit(solution)/shard_map/ppermute | solution.py:15
  20.6 35.2 %all-to-all-start = ((bf16[64,22,256]{2,1,0:T(8,128)(2,1)}), bf16[64,22,256]{2,1,0:T(8,128)(2,1)S(1)}, u32[]{:S(2)}, u32[]{:S(2)}) async-start(bf16[64,22,256]{2,1,0:T(8,128)(2,1)} %bitcast.3), calls=%async_computation | async-start | bytes 1572864 | tf_op jit(solution)/shard_map/all_to_all | solution.py:49
  32.0 12.6 %collective-permute-start.1 = (bf16[176,1024]{1,0:T(8,128)(2,1)S(1)}, bf16[176,1024]{1,0:T(8,128)(2,1)S(1)}, u32[]{:S(2)}, u32[]{:S(2)}) collective-permute-start(bf16[176,1024]{1,0:T(8,128)(2,1)S(1)} %dynamic-slice_bitcast_fusion), channel_id=1, source_target_pairs={{448,0},{0,64},{64,128},{128,192},{192,256},{256,320},{320,384},{3... | collective-permute-start | bytes 1081352 | tf_op jit(solution)/shard_map/ppermute | solution.py:15
  44.6 11.1 %copy-start.2 = (bf16[176,1024]{1,0:T(8,128)(2,1)}, bf16[176,1024]{1,0:T(8,128)(2,1)S(1)}, u32[]{:S(2)}) copy-start(bf16[176,1024]{1,0:T(8,128)(2,1)S(1)} %collective-permute-done.1) | copy-start | bytes 1081348
  57.1 5.0 %copy-start.3 = (f32[22,8,8,128]{3,2,1,0:T(8,128)S(1)}, f32[22,8,8,128]{3,2,1,0:T(8,128)}, u32[]{:S(2)}) copy-start(f32[22,8,8,128]{3,2,1,0:T(8,128)} %copy.80) | copy-start | bytes 2162692
  64.6 2.9 %copy-start.4 = (bf16[22,8,8,128]{3,2,1,0:T(8,128)(2,1)S(1)}, bf16[22,8,8,128]{3,2,1,0:T(8,128)(2,1)}, u32[]{:S(2)}) copy-start(bf16[22,8,8,128]{3,2,1,0:T(8,128)(2,1)} %copy.81) | copy-start | bytes 1081348
  67.5 2.6 %copy-start.1 = (bf16[8,176,1408]{2,1,0:T(8,128)(2,1)}, bf16[8,176,1408]{2,1,0:T(8,128)(2,1)S(1)}, u32[]{:S(2)}) copy-start(bf16[8,176,1408]{2,1,0:T(8,128)(2,1)S(1)} %fusion.6) | copy-start | bytes 11894788
  75.5 43.9 %all-to-all-start.1 = ((f32[64,22,256]{2,1,0:T(8,128)}), f32[64,22,256]{2,1,0:T(8,128)S(1)}, u32[]{:S(2)}, u32[]{:S(2)}) async-start(f32[64,22,256]{2,1,0:T(8,128)} %all_to_all.14), calls=%async_computation.1 | async-start | bytes 3145728 | tf_op jit(solution)/shard_map/all_to_all | solution.py:86

commit v4 on v3

--- a/solution.py
+++ b/solution.py
@@ -82,12 +82,14 @@
 
     attended_flat = attended.astype(jnp.bfloat16).reshape(tok_rows, heads_local * head_size)
     q_grad_flat = q_grad.reshape(tok_rows, heads_local * head_size)
-    grad_terms = jnp.stack([key_grad, value_grad], axis=2).reshape(seq_rows, 2 * kv_width)
-    grad_parts = lax.all_to_all(grad_terms, plane, split_axis=0, concat_axis=0, tiled=True)
-    grad_parts = grad_parts.reshape(ctx_count, tp_count, kv_rows, kv_local, 2, head_size)
-    own_grads = jnp.sum(grad_parts, axis=0)
-    k_grad_tokens = own_grads[:, :, :, 0, :].transpose(1, 0, 2, 3).reshape(kv_rows, -1)
-    v_grad_tokens = own_grads[:, :, :, 1, :].transpose(1, 0, 2, 3).reshape(kv_rows, -1)
+    def to_owners(term):
+        sent = term.reshape(seq_rows, kv_width).astype(jnp.bfloat16)
+        parts = lax.all_to_all(sent, plane, split_axis=0, concat_axis=0, tiled=True)
+        parts = parts.reshape(ctx_count, tp_count, kv_rows, kv_width).astype(jnp.float32)
+        return jnp.sum(parts, axis=0).transpose(1, 0, 2).reshape(kv_rows, -1)
+
+    v_grad_tokens = to_owners(value_grad)
+    k_grad_tokens = to_owners(key_grad)
     return (attended_flat[None], q_grad_flat[None], k_grad_tokens[None], v_grad_tokens[None])
 
 

time: 125 us -> 113 us (0.904)
  waiting for transfers between devices: 51.7 us -> 37.9 us
  starting transfers between devices: 31.6 us -> 35.8 us
  local copies, waits for them, and re-layouts: 18.6 us -> 15.7 us
  matrix products: 14.1 us -> 16.8 us
  other arithmetic: 5.03 us -> 3.18 us
    all_to_all x1 -> x2, waiting for transfers between devices: 32.7 us -> 18.8 us  [to_owners(): parts = lax.all_to_all(sent, plane, split_axis=0, concat_axis=0, tiled=True)]
    all_to_all x1 -> x2, starting transfers between devices: 4.93 us -> 9.13 us  [to_owners(): parts = lax.all_to_all(sent, plane, split_axis=0, concat_axis=0, tiled=True)]
    dot_general x1, matrix products: 1.66 us -> 5.84 us  [body(): jnp.einsum('gjqk,qgjd->kgd', probs_low, do4, preferred_element_type=jnp.f...]
    all_to_all x1 -> x0, local copies, waits for them, and re-layouts: 3.21 us -> none  [body(): lax.all_to_all(grad_terms, plane, split_axis=0, concat_axis=0, tiled=True)]
    another operation x2 -> x0, local copies, waits for them, and re-layouts: 2.96 us -> none  [the longest x1 2.15 us: body(): jnp.stack([key_grad, value_grad], axis=2).reshape(seq_rows, 2 * kv_width)]
    convert_element_type x0 -> x3, local copies, waits for them, and re-layouts: none -> 2.91 us  [to_owners(): sent = term.reshape(seq_rows, kv_width).astype(jnp.bfloat16)]
    unnamed x16 -> x15, local copies, waits for them, and re-layouts: 1.99 us -> 3.9 us
    reshape x1 -> x0, local copies, waits for them, and re-layouts: 1.86 us -> none  [body(): grad_parts.reshape(ctx_count, tp_count, kv_rows, kv_local, 2, head_size)]
  transfers between devices with their start and end apart: 5 -> 6, of which waited for: 4 -> 5; matrix products, arithmetic and copies ran while one was open for 9% -> 16% of each run, Pallas kernels for 0% -> 0%
where the time goes in v4:
time: 113 us; the launch traced here: 112 us
  waiting for transfers between devices  37.9 us (34%)
  starting transfers between devices  35.8 us (32%)
  matrix products  16.8 us (15%)
  local copies, waits for them, and re-layouts  15.7 us (14%)
  other arithmetic  3.18 us (3%)
  between operations  2.91 us (3%)
    all_to_all x2, waiting for transfers between devices, to_owners(): parts = lax.all_to_all(sent, plane, split_axis=0, concat_axis=0, tiled=True)  18.8 us
    ppermute x3, starting transfers between devices, passed_along(): return lax.ppermute(block, axis, route)  15.3 us
    all_to_all x1, starting transfers between devices, body(): lax.all_to_all(kv_pieces, plane, split_axis=0, concat_axis=0, tiled=True)  11.4 us
    all_to_all x1, waiting for transfers between devices, body(): lax.all_to_all(kv_pieces, plane, split_axis=0, concat_axis=0, tiled=True)  10.3 us
    all_to_all x2, starting transfers between devices, to_owners(): parts = lax.all_to_all(sent, plane, split_axis=0, concat_axis=0, tiled=True)  9.13 us
    ppermute x3, waiting for transfers between devices, passed_along(): return lax.ppermute(block, axis, route)  8.72 us
    dot_general x1, matrix products, body(): jnp.einsum('gjqk,qgjd->kgd', probs_low, do4, preferred_element_type=jnp.f...  5.84 us
    unnamed x15, local copies, waits for them, and re-layouts  3.9 us
  transfers between devices with their start and end apart: 6, of which 5 were waited for; matrix products, arithmetic and copies ran while one was open for 16% of the time, Pallas kernels for 0%

profile of v4, /device:TPU:1, one launch (start us, length us, event | category | flops | bytes accessed | tf_op | source)
XLA Modules:
  0.0 112.3 jit_solution(956708706103712073)
XLA Ops:
  0.6 0.0 copy-start
  0.7 1.3 %dynamic_slice.19 = s32[1]{0:T(128)} dynamic-slice(s32[8]{0:T(128)} %param.7, s32[]{:T(128)S(6)} %select_n.33), dynamic_slice_sizes={1} | dynamic-slice | bytes 12 | tf_op jit(solution)/shard_map/jit(dynamic_index_in_dim)/dynamic_slice | solution.py:35
  3.9 1.5 %dynamic-slice_reduce_fusion = (bf16[22,1024]{1,0:T(8,128)(2,1)S(1)}, bf16[22,1024]{1,0:T(8,128)(2,1)S(1)}) fusion(bf16[1,2,22,1024]{3,1,2,0:T(2,128)(2,1)} %param.10, s32[]{:T(128)S(6)} %select_n.34, bf16[1,2,22,1024]{3,1,2,0:T(2,128)(2,1)} %param.9), kind=kLoop, calls=%fused_computation.39 | loop fusion | bytes 180228 | tf_op jit(solution)/shard_map/jit(dynamic_index_in_dim)/dynamic_slice | solution.py:38
  5.5 0.1 copy.35
  5.6 4.8 %collective-permute-start = (bf16[22,2048]{1,0:T(8,128)(2,1)S(1)}, bf16[22,2048]{1,0:T(8,128)(2,1)S(1)}, u32[]{:S(2)}, u32[]{:S(2)}) collective-permute-start(bf16[22,2048]{1,0:T(8,128)(2,1)S(1)} %reshape.186), channel_id=1, source_target_pairs={{448,0},{0,64},{64,128},{128,192},{192,256},{256,320},{320,384},{3... | collective-permute-start | bytes 270344 | tf_op jit(solution)/shard_map/ppermute | solution.py:15
  10.4 8.6 %collective-permute-start.2 = (bf16[176,1024]{1,0:T(8,128)(2,1)}, bf16[176,1024]{1,0:T(8,128)(2,1)S(1)}, u32[]{:S(2)}, u32[]{:S(2)}) collective-permute-start(bf16[176,1024]{1,0:T(8,128)(2,1)} %bitcast.169), channel_id=1, source_target_pairs={{64,0},{128,64},{192,128},{256,192},{320,256},{384,320},{448,384},... | collective-permute-start | bytes 1081352 | tf_op jit(solution)/shard_map/ppermute | solution.py:15
  19.0 0.6 collective-permute-done
  19.6 0.9 broadcast_in_dim.37
  20.6 11.4 %all-to-all-start = ((bf16[64,22,256]{2,1,0:T(8,128)(2,1)}), bf16[64,22,256]{2,1,0:T(8,128)(2,1)S(1)}, u32[]{:S(2)}, u32[]{:S(2)}) async-start(bf16[64,22,256]{2,1,0:T(8,128)(2,1)} %bitcast.3), calls=%async_computation | async-start | bytes 1572864 | tf_op jit(solution)/shard_map/all_to_all | solution.py:49
  32.0 1.9 %collective-permute-start.1 = (bf16[176,1024]{1,0:T(8,128)(2,1)S(1)}, bf16[176,1024]{1,0:T(8,128)(2,1)S(1)}, u32[]{:S(2)}, u32[]{:S(2)}) collective-permute-start(bf16[176,1024]{1,0:T(8,128)(2,1)S(1)} %dynamic-slice_bitcast_fusion), channel_id=1, source_target_pairs={{448,0},{0,64},{64,128},{128,192},{192,256},{256,320},{320,384},{3... | collective-permute-start | bytes 1081352 | tf_op jit(solution)/shard_map/ppermute | solution.py:15
  33.9 0.7 broadcast_multiply_fusion
  34.6 0.1 add.73
  34.7 0.1 iota_add_fusion
  34.7 0.1 add.72
  34.8 0.1 add.74
  34.9 0.1 add.75
  35.0 0.1 add.77
  35.1 0.2 broadcast_compare_fusion
  35.3 0.1 convert_bitcast_fusion
  35.4 1.1 copy.58
  36.5 8.2 %collective-permute-done.1 = bf16[176,1024]{1,0:T(8,128)(2,1)S(1)} collective-permute-done((bf16[176,1024]{1,0:T(8,128)(2,1)S(1)}, bf16[176,1024]{1,0:T(8,128)(2,1)S(1)}, u32[]{:S(2)}, u32[]{:S(2)}) %collective-permute-start.1) | collective-permute-done | bytes 360480 | tf_op jit(solution)/shard_map/ppermute | solution.py:15
  44.6 0.8 copy.59
  45.4 10.3 %all-to-all-done = bf16[64,22,256]{2,1,0:T(8,128)(2,1)S(1)} async-done(((bf16[64,22,256]{2,1,0:T(8,128)(2,1)}), bf16[64,22,256]{2,1,0:T(8,128)(2,1)S(1)}, u32[]{:S(2)}, u32[]{:S(2)}) %all-to-all-start) | async-done | bytes 720928 | tf_op jit(solution)/shard_map/all_to_all | solution.py:49
  55.8 0.3 reshape.188
  56.0 1.1 fusion.34
  57.1 1.9 %fusion.35 = (f32[8,176]{1,0:T(8,128)S(1)}, f32[1,8,176,1408]{3,2,1,0:T(8,128)S(1)}) fusion(bf16[1408,1,1,128]{3,2,0,1:T(2,128)(2,1)S(1)} %get-tuple-element.11, pred[176,1408]{1,0:T(8,128)(4,1)S(1)} %broadcast_compare_fusion, bf16[176,1024]{1,0:T(8,128)(2,1)S(1)} %collective-permute-done.1), kind=kOutput, calls=%fused_computation.50 | convolution fusion | flops 513456768 | bytes 8904192 | tf_op jit(solution)/shard_map/qgjd,kgd->gjqk/dot_general | solution.py:64
  59.0 2.0 %select_reduce_fusion = f32[8,176]{1,0:T(8,128)S(1)} fusion(f32[1,8,176,1408]{3,2,1,0:T(8,128)S(1)} %get-tuple-element.13, f32[8,176]{1,0:T(8,128)S(1)} %get-tuple-element.12, pred[176,1408]{1,0:T(8,128)(4,1)S(1)} %broadcast_compare_fusion), kind=kLoop, calls=%fused_computation.5 | loop fusion | flops 5945984 | bytes 8188928 | tf_op jit(solution)/shard_map/reduce_sum | solution.py:67
  61.1 1.9 %fusion.23 = (f32[176,8]{0,1:T(8,128)S(1)}, bf16[176,1,8,128]{3,0,2,1:T(8,128)(2,1)S(1)}) fusion(f32[176,1,8,128]{3,2,0,1:T(8,128)S(1)} %bitcast.155, f32[1,8,176,1408]{3,2,1,0:T(8,128)S(1)} %get-tuple-element.13, f32[8,176]{1,0:T(8,128)S(1)} %log_add_fusion, pred[176,1408]{1,0:T(8,128)(4,1)S(1)} %broadcast_compare_fusion, ...), kind=kOutput, calls=%fused_computation.25 | convolution fusion | flops 513997440 | bytes 9630720 | tf_op jit(solution)/shard_map/gjqk,kgd->qgjd/dot_general | solution.py:71
  63.0 2.9 %fusion.6 = bf16[8,176,1408]{2,1,0:T(8,128)(2,1)S(1)} fusion(f32[8,176]{1,0:T(8,128)S(1)} %bitcast.167, f32[1,8,176,1408]{3,2,1,0:T(8,128)S(1)} %get-tuple-element.13, f32[8,176]{1,0:T(8,128)S(1)} %log_add_fusion, pred[176,1408]{1,0:T(8,128)(4,1)S(1)} %broadcast_compare_fusion, bf16[1408,1,1,128]{3,2,0,1:T(2,128)(2,1)S(1)} %get-tuple-element.10, ...), kind=kOutput, calls=%fused_computation.10 | convolution fusion | flops 517423104 | bytes 12874752 | tf_op jit(solution)/shard_map/qgjd,kgd->gjqk/dot_general | solution.py:75
  66.0 2.0 %copy-done.2 = bf16[8,176,1408]{2,1,0:T(8,128)(2,1)} copy-done((bf16[8,176,1408]{2,1,0:T(8,128)(2,1)}, bf16[8,176,1408]{2,1,0:T(8,128)(2,1)S(1)}, u32[]{:S(2)}) %copy-start.2) | copy-done | bytes 3964952
  67.9 0.9 fusion.17
  68.8 0.2 copy.45
  69.1 0.9 convert_element_type.84
  69.9 4.9 %all-to-all-start.1 = ((bf16[64,22,128]{2,1,0:T(8,128)(2,1)}), bf16[64,22,128]{2,1,0:T(8,128)(2,1)S(1)}, u32[]{:S(2)}, u32[]{:S(2)}) async-start(bf16[64,22,128]{2,1,0:T(8,128)(2,1)} %convert_element_type.84), calls=%async_computation.1 | async-start | bytes 786432 | tf_op jit(solution)/shard_map/all_to_all | solution.py:87
  74.9 5.8 %fusion.20 = bf16[1408,1,128]{2,0,1:T(8,128)(2,1)} fusion(f32[1,8,176,1408]{3,2,1,0:T(8,128)} %copy-done.1, f32[8,176]{1,0:T(8,128)S(1)} %log_add_fusion, pred[176,1408]{1,0:T(8,128)(4,1)S(1)} %broadcast_compare_fusion, bf16[176,1024]{1,0:T(8,128)(2,1)S(1)} %collective-permute-done.2), kind=kOutput, calls=%fused_computation.17 | convolution fusion | flops 513638400 | bytes 8904192 | tf_op jit(solution)/shard_map/gjqk,qgjd->kgd/dot_general | solution.py:81
  80.7 1.8 %convert_element_type.91 = bf16[64,22,128]{2,1,0:T(8,128)(2,1)} reshape(bf16[1408,1,128]{2,0,1:T(8,128)(2,1)} %fusion.20) | data formatting | bytes 720896 | tf_op jit(solution)/shard_map/convert_element_type | solution.py:86
  82.5 8.6 %all-to-all-done.1 = bf16[64,22,128]{2,1,0:T(8,128)(2,1)S(1)} async-done(((bf16[64,22,128]{2,1,0:T(8,128)(2,1)}), bf16[64,22,128]{2,1,0:T(8,128)(2,1)S(1)}, u32[]{:S(2)}, u32[]{:S(2)}) %all-to-all-start.1) | async-done | bytes 360480 | tf_op jit(solution)/shard_map/all_to_all | solution.py:87
  91.1 4.2 %all-to-all-start.2 = ((bf16[64,22,128]{2,1,0:T(8,128)(2,1)}), bf16[64,22,128]{2,1,0:T(8,128)(2,1)S(1)}, u32[]{:S(2)}, u32[]{:S(2)}) async-start(bf16[64,22,128]{2,1,0:T(8,128)(2,1)} %convert_element_type.91), calls=%async_computation.2 | async-start | bytes 786432 | tf_op jit(solution)/shard_map/all_to_all | solution.py:87
  95.3 0.1 copy.40
  95.4 0.9 broadcast_in_dim_reshape.12
  96.3 3.3 %fusion.22 = bf16[176,1,8,128]{3,0,2,1:T(8,128)(2,1)S(1)} fusion(bf16[8,176,1408]{2,1,0:T(8,128)(2,1)} %copy-done.2, bf16[1408,1,1,128]{3,2,0,1:T(2,128)(2,1)S(1)} %get-tuple-element.11), kind=kOutput, calls=%fused_computation.21 | convolution fusion | flops 507871232 | bytes 4685824 | tf_op jit(solution)/shard_map/gjqk,kgd->qgjd/dot_general | solution.py:78
  99.6 0.1 copy.43
  99.7 0.9 broadcast_in_dim_reshape.13
  100.6 0.1 convert_reduce_fusion.1
  100.7 0.7 copy.46
  101.4 10.2 %all-to-all-done.2 = bf16[64,22,128]{2,1,0:T(8,128)(2,1)S(1)} async-done(((bf16[64,22,128]{2,1,0:T(8,128)(2,1)}), bf16[64,22,128]{2,1,0:T(8,128)(2,1)S(1)}, u32[]{:S(2)}, u32[]{:S(2)}) %all-to-all-start.2) | async-done | bytes 360480 | tf_op jit(solution)/shard_map/all_to_all | solution.py:87
  111.6 0.1 convert_reduce_fusion
  111.6 0.7 copy.48
  (22 shorter events, 0.2 us)
Async XLA Ops:
  0.6 31.3 %copy-start = (bf16[1,2,176,1024]{3,2,1,0:T(8,128)(2,1)S(1)}, bf16[1,2,176,1024]{3,2,1,0:T(8,128)(2,1)}, u32[]{:S(2)}) copy-start(bf16[1,2,176,1024]{3,2,1,0:T(8,128)(2,1)} %param.8) | copy-start | bytes 2162692
  5.6 14.0 %collective-permute-start = (bf16[22,2048]{1,0:T(8,128)(2,1)S(1)}, bf16[22,2048]{1,0:T(8,128)(2,1)S(1)}, u32[]{:S(2)}, u32[]{:S(2)}) collective-permute-start(bf16[22,2048]{1,0:T(8,128)(2,1)S(1)} %reshape.186), channel_id=1, source_target_pairs={{448,0},{0,64},{64,128},{128,192},{192,256},{256,320},{320,384},{3... | collective-permute-start | bytes 270344 | tf_op jit(solution)/shard_map/ppermute | solution.py:15
  10.4 24.9 %collective-permute-start.2 = (bf16[176,1024]{1,0:T(8,128)(2,1)}, bf16[176,1024]{1,0:T(8,128)(2,1)S(1)}, u32[]{:S(2)}, u32[]{:S(2)}) collective-permute-start(bf16[176,1024]{1,0:T(8,128)(2,1)} %bitcast.169), channel_id=1, source_target_pairs={{64,0},{128,64},{192,128},{256,192},{320,256},{384,320},{448,384},... | collective-permute-start | bytes 1081352 | tf_op jit(solution)/shard_map/ppermute | solution.py:15
  20.6 35.2 %all-to-all-start = ((bf16[64,22,256]{2,1,0:T(8,128)(2,1)}), bf16[64,22,256]{2,1,0:T(8,128)(2,1)S(1)}, u32[]{:S(2)}, u32[]{:S(2)}) async-start(bf16[64,22,256]{2,1,0:T(8,128)(2,1)} %bitcast.3), calls=%async_computation | async-start | bytes 1572864 | tf_op jit(solution)/shard_map/all_to_all | solution.py:49
  32.0 12.6 %collective-permute-start.1 = (bf16[176,1024]{1,0:T(8,128)(2,1)S(1)}, bf16[176,1024]{1,0:T(8,128)(2,1)S(1)}, u32[]{:S(2)}, u32[]{:S(2)}) collective-permute-start(bf16[176,1024]{1,0:T(8,128)(2,1)S(1)} %dynamic-slice_bitcast_fusion), channel_id=1, source_target_pairs={{448,0},{0,64},{64,128},{128,192},{192,256},{256,320},{320,384},{3... | collective-permute-start | bytes 1081352 | tf_op jit(solution)/shard_map/ppermute | solution.py:15
  57.1 4.0 %copy-start.3 = (f32[22,8,8,128]{3,2,1,0:T(8,128)S(1)}, f32[22,8,8,128]{3,2,1,0:T(8,128)}, u32[]{:S(2)}) copy-start(f32[22,8,8,128]{3,2,1,0:T(8,128)} %copy.58) | copy-start | bytes 2162692
  59.0 4.0 %copy-start.1 = (f32[1,8,176,1408]{3,2,1,0:T(8,128)}, f32[1,8,176,1408]{3,2,1,0:T(8,128)S(1)}, u32[]{:S(2)}) copy-start(f32[1,8,176,1408]{3,2,1,0:T(8,128)S(1)} %get-tuple-element.13) | copy-start | bytes 23789572
  63.0 4.9 %copy-start.4 = (bf16[22,8,8,128]{3,2,1,0:T(8,128)(2,1)S(1)}, bf16[22,8,8,128]{3,2,1,0:T(8,128)(2,1)}, u32[]{:S(2)}) copy-start(bf16[22,8,8,128]{3,2,1,0:T(8,128)(2,1)} %copy.59) | copy-start | bytes 1081348
  66.0 2.0 %copy-start.2 = (bf16[8,176,1408]{2,1,0:T(8,128)(2,1)}, bf16[8,176,1408]{2,1,0:T(8,128)(2,1)S(1)}, u32[]{:S(2)}) copy-start(bf16[8,176,1408]{2,1,0:T(8,128)(2,1)S(1)} %fusion.6) | copy-start | bytes 11894788
  69.9 21.2 %all-to-all-start.1 = ((bf16[64,22,128]{2,1,0:T(8,128)(2,1)}), bf16[64,22,128]{2,1,0:T(8,128)(2,1)S(1)}, u32[]{:S(2)}, u32[]{:S(2)}) async-start(bf16[64,22,128]{2,1,0:T(8,128)(2,1)} %convert_element_type.84), calls=%async_computation.1 | async-start | bytes 786432 | tf_op jit(solution)/shard_map/all_to_all | solution.py:87
  91.1 20.5 %all-to-all-start.2 = ((bf16[64,22,128]{2,1,0:T(8,128)(2,1)}), bf16[64,22,128]{2,1,0:T(8,128)(2,1)S(1)}, u32[]{:S(2)}, u32[]{:S(2)}) async-start(bf16[64,22,128]{2,1,0:T(8,128)(2,1)} %convert_element_type.91), calls=%async_computation.2 | async-start | bytes 786432 | tf_op jit(solution)/shard_map/all_to_all | solution.py:87

commit v5 on v3

--- a/solution.py
+++ b/solution.py
@@ -83,9 +83,11 @@
     attended_flat = attended.astype(jnp.bfloat16).reshape(tok_rows, heads_local * head_size)
     q_grad_flat = q_grad.reshape(tok_rows, heads_local * head_size)
     grad_terms = jnp.stack([key_grad, value_grad], axis=2).reshape(seq_rows, 2 * kv_width)
-    grad_parts = lax.all_to_all(grad_terms, plane, split_axis=0, concat_axis=0, tiled=True)
+    grad_parts = lax.all_to_all(
+        grad_terms.astype(jnp.bfloat16), plane, split_axis=0, concat_axis=0, tiled=True
+    )
     grad_parts = grad_parts.reshape(ctx_count, tp_count, kv_rows, kv_local, 2, head_size)
-    own_grads = jnp.sum(grad_parts, axis=0)
+    own_grads = jnp.sum(grad_parts.astype(jnp.float32), axis=0)
     k_grad_tokens = own_grads[:, :, :, 0, :].transpose(1, 0, 2, 3).reshape(kv_rows, -1)
     v_grad_tokens = own_grads[:, :, :, 1, :].transpose(1, 0, 2, 3).reshape(kv_rows, -1)
     return (attended_flat[None], q_grad_flat[None], k_grad_tokens[None], v_grad_tokens[None])

time: 125 us -> 105 us (0.84)
  waiting for transfers between devices: 51.7 us -> 37.6 us
  local copies, waits for them, and re-layouts: 18.6 us -> 14.7 us
  matrix products: 14.1 us -> 12.6 us
    all_to_all x1, waiting for transfers between devices: 32.7 us -> 18.5 us  [body(): lax.all_to_all(grad_terms.astype(jnp.bfloat16), plane, split_axis=0, conc...]
    convert_element_type x0 -> x2, local copies, waits for them, and re-layouts: none -> 3.33 us  [the longest x1 1.99 us: body(): own_grads = jnp.sum(grad_parts.astype(jnp.float32), axis=0)]
    all_to_all x1 -> x0, local copies, waits for them, and re-layouts: 3.21 us -> none  [body(): lax.all_to_all(grad_terms, plane, split_axis=0, concat_axis=0, tiled=True)]
    reshape x1 -> x0, local copies, waits for them, and re-layouts: 1.86 us -> none  [body(): grad_parts.reshape(ctx_count, tp_count, kv_rows, kv_local, 2, head_size)]
    convert_element_type x0 -> x1, other arithmetic: none -> 1.29 us  [body(): own_grads = jnp.sum(grad_parts.astype(jnp.float32), axis=0)]
where the time goes in v5:
time: 105 us
  waiting for transfers between devices  37.6 us (36%)
  starting transfers between devices  31.6 us (30%)
  local copies, waits for them, and re-layouts  14.7 us (14%)
  matrix products  12.6 us (12%)
  other arithmetic  5.15 us (5%)
  between operations  2.93 us (3%)
    all_to_all x1, waiting for transfers between devices, body(): lax.all_to_all(grad_terms.astype(jnp.bfloat16), plane, split_axis=0, conc...  18.5 us
    ppermute x3, starting transfers between devices, passed_along(): return lax.ppermute(block, axis, route)  15.3 us
    all_to_all x1, starting transfers between devices, body(): lax.all_to_all(kv_pieces, plane, split_axis=0, concat_axis=0, tiled=True)  11.4 us
    all_to_all x1, waiting for transfers between devices, body(): lax.all_to_all(kv_pieces, plane, split_axis=0, concat_axis=0, tiled=True)  10.3 us
    ppermute x3, waiting for transfers between devices, passed_along(): return lax.ppermute(block, axis, route)  8.77 us
    all_to_all x1, starting transfers between devices, body(): lax.all_to_all(grad_terms.astype(jnp.bfloat16), plane, split_axis=0, conc...  4.94 us
    dot_general x1, matrix products, body(): jnp.einsum('gjqk,kgd->qgjd', dscores, key_heads, preferred_element_type=j...  3.32 us
    dot_general x1, matrix products, body(): jnp.einsum('qgjd,kgd->gjqk', do4, value_heads, preferred_element_type=jnp...  2.92 us
  transfers between devices with their start and end apart: 5, of which 4 were waited for; matrix products, arithmetic and copies ran while one was open for 9% of the time, Pallas kernels for 0%

profile of v5, /device:TPU:1, one launch (start us, length us, event | category | flops | bytes accessed | tf_op | source)
XLA Modules:
  0.0 104.6 jit_solution(17306683377396170087)
XLA Ops:
  0.6 0.0 copy-start
  0.7 1.3 %dynamic_slice.19 = s32[1]{0:T(128)} dynamic-slice(s32[8]{0:T(128)} %param.7, s32[]{:T(128)S(6)} %select_n.33), dynamic_slice_sizes={1} | dynamic-slice | bytes 12 | tf_op jit(solution)/shard_map/jit(dynamic_index_in_dim)/dynamic_slice | solution.py:35
  3.9 1.5 %dynamic-slice_reduce_fusion = (bf16[22,1024]{1,0:T(8,128)(2,1)S(1)}, bf16[22,1024]{1,0:T(8,128)(2,1)S(1)}) fusion(bf16[1,2,22,1024]{3,1,2,0:T(2,128)(2,1)} %param.10, s32[]{:T(128)S(6)} %select_n.34, bf16[1,2,22,1024]{3,1,2,0:T(2,128)(2,1)} %param.9), kind=kLoop, calls=%fused_computation.41 | loop fusion | bytes 180228 | tf_op jit(solution)/shard_map/jit(dynamic_index_in_dim)/dynamic_slice | solution.py:38
  5.5 0.1 copy.83
  5.6 4.8 %collective-permute-start = (bf16[22,2048]{1,0:T(8,128)(2,1)S(1)}, bf16[22,2048]{1,0:T(8,128)(2,1)S(1)}, u32[]{:S(2)}, u32[]{:S(2)}) collective-permute-start(bf16[22,2048]{1,0:T(8,128)(2,1)S(1)} %reshape.191), channel_id=1, source_target_pairs={{448,0},{0,64},{64,128},{128,192},{192,256},{256,320},{320,384},{3... | collective-permute-start | bytes 270344 | tf_op jit(solution)/shard_map/ppermute | solution.py:15
  10.4 8.6 %collective-permute-start.2 = (bf16[176,1024]{1,0:T(8,128)(2,1)}, bf16[176,1024]{1,0:T(8,128)(2,1)S(1)}, u32[]{:S(2)}, u32[]{:S(2)}) collective-permute-start(bf16[176,1024]{1,0:T(8,128)(2,1)} %bitcast.173), channel_id=1, source_target_pairs={{64,0},{128,64},{192,128},{256,192},{320,256},{384,320},{448,384},... | collective-permute-start | bytes 1081352 | tf_op jit(solution)/shard_map/ppermute | solution.py:15
  19.0 0.6 collective-permute-done
  19.6 0.9 broadcast_in_dim.37
  20.6 11.4 %all-to-all-start = ((bf16[64,22,256]{2,1,0:T(8,128)(2,1)}), bf16[64,22,256]{2,1,0:T(8,128)(2,1)S(1)}, u32[]{:S(2)}, u32[]{:S(2)}) async-start(bf16[64,22,256]{2,1,0:T(8,128)(2,1)} %bitcast.3), calls=%async_computation | async-start | bytes 1572864 | tf_op jit(solution)/shard_map/all_to_all | solution.py:49
  31.9 0.0 copy-done
  32.0 1.9 %collective-permute-start.1 = (bf16[176,1024]{1,0:T(8,128)(2,1)S(1)}, bf16[176,1024]{1,0:T(8,128)(2,1)S(1)}, u32[]{:S(2)}, u32[]{:S(2)}) collective-permute-start(bf16[176,1024]{1,0:T(8,128)(2,1)S(1)} %dynamic-slice_bitcast_fusion), channel_id=1, source_target_pairs={{448,0},{0,64},{64,128},{128,192},{192,256},{256,320},{320,384},{3... | collective-permute-start | bytes 1081352 | tf_op jit(solution)/shard_map/ppermute | solution.py:15
  33.9 0.7 broadcast_multiply_fusion
  34.6 0.1 add.73
  34.7 0.1 iota_add_fusion
  34.7 0.1 add.72
  34.8 0.1 add.74
  34.9 0.1 add.75
  35.0 0.1 add.77
  35.1 0.2 broadcast_compare_fusion
  35.3 0.0 collective-permute-done.2
  35.3 0.1 convert_bitcast_fusion
  35.4 1.0 copy.106
  36.4 8.2 %collective-permute-done.1 = bf16[176,1024]{1,0:T(8,128)(2,1)S(1)} collective-permute-done((bf16[176,1024]{1,0:T(8,128)(2,1)S(1)}, bf16[176,1024]{1,0:T(8,128)(2,1)S(1)}, u32[]{:S(2)}, u32[]{:S(2)}) %collective-permute-start.1) | collective-permute-done | bytes 360480 | tf_op jit(solution)/shard_map/ppermute | solution.py:15
  44.6 0.8 copy.107
  45.4 10.3 %all-to-all-done = bf16[64,22,256]{2,1,0:T(8,128)(2,1)S(1)} async-done(((bf16[64,22,256]{2,1,0:T(8,128)(2,1)}), bf16[64,22,256]{2,1,0:T(8,128)(2,1)S(1)}, u32[]{:S(2)}, u32[]{:S(2)}) %all-to-all-start) | async-done | bytes 720928 | tf_op jit(solution)/shard_map/all_to_all | solution.py:49
  55.8 0.3 reshape.193
  56.0 1.1 %fusion.34 = (bf16[1408,1,1,128]{3,2,0,1:T(2,128)(2,1)S(1)}, bf16[1408,1,1,128]{3,2,0,1:T(2,128)(2,1)S(1)}) fusion(bf16[1408,1,2,128]{3,2,0,1:T(2,128)(2,1)S(1)} %reshape.193), kind=kLoop, calls=%fused_computation.51 | loop fusion | bytes 1441792 | tf_op jit(solution)/shard_map/slice | solution.py:52
  57.1 1.9 %fusion.35 = (f32[8,176]{1,0:T(8,128)S(1)}, f32[1,8,176,1408]{3,2,1,0:T(8,128)S(1)}) fusion(bf16[1408,1,1,128]{3,2,0,1:T(2,128)(2,1)S(1)} %get-tuple-element.11, pred[176,1408]{1,0:T(8,128)(4,1)S(1)} %broadcast_compare_fusion, bf16[176,1024]{1,0:T(8,128)(2,1)S(1)} %collective-permute-done.1), kind=kOutput, calls=%fused_computation.52 | convolution fusion | flops 513456768 | bytes 8904192 | tf_op jit(solution)/shard_map/qgjd,kgd->gjqk/dot_general | solution.py:64
  59.0 2.0 %select_reduce_fusion = f32[8,176]{1,0:T(8,128)S(1)} fusion(f32[1,8,176,1408]{3,2,1,0:T(8,128)S(1)} %get-tuple-element.15, f32[8,176]{1,0:T(8,128)S(1)} %get-tuple-element.14, pred[176,1408]{1,0:T(8,128)(4,1)S(1)} %broadcast_compare_fusion), kind=kLoop, calls=%fused_computation.5 | loop fusion | flops 5945984 | bytes 8188928 | tf_op jit(solution)/shard_map/reduce_sum | solution.py:67
  61.1 1.9 %fusion.23 = (f32[176,8]{0,1:T(8,128)S(1)}, bf16[176,1,8,128]{3,0,2,1:T(8,128)(2,1)S(1)}) fusion(f32[176,1,8,128]{3,2,0,1:T(8,128)S(1)} %bitcast.163, f32[1,8,176,1408]{3,2,1,0:T(8,128)S(1)} %get-tuple-element.15, f32[8,176]{1,0:T(8,128)S(1)} %log_add_fusion, pred[176,1408]{1,0:T(8,128)(4,1)S(1)} %broadcast_compare_fusion, ...), kind=kOutput, calls=%fused_computation.25 | convolution fusion | flops 513997440 | bytes 9630720 | tf_op jit(solution)/shard_map/gjqk,kgd->qgjd/dot_general | solution.py:71
  63.0 0.0 copy-start.3
  63.0 2.9 %fusion.6 = bf16[8,176,1408]{2,1,0:T(8,128)(2,1)S(1)} fusion(f32[8,176]{1,0:T(8,128)S(1)} %bitcast.171, f32[1,8,176,1408]{3,2,1,0:T(8,128)S(1)} %get-tuple-element.15, f32[8,176]{1,0:T(8,128)S(1)} %log_add_fusion, pred[176,1408]{1,0:T(8,128)(4,1)S(1)} %broadcast_compare_fusion, bf16[1408,1,1,128]{3,2,0,1:T(2,128)(2,1)S(1)} %get-tuple-element.10, ...), kind=kOutput, calls=%fused_computation.10 | convolution fusion | flops 517423104 | bytes 12874752 | tf_op jit(solution)/shard_map/qgjd,kgd->gjqk/dot_general | solution.py:75
  66.0 0.9 fusion.17
  66.8 1.7 %fusion.20 = bf16[1408,1,1,128]{0,3,2,1:T(8,128)(2,1)S(1)} fusion(f32[1,8,176,1408]{3,2,1,0:T(8,128)S(1)} %get-tuple-element.15, f32[8,176]{1,0:T(8,128)S(1)} %log_add_fusion, pred[176,1408]{1,0:T(8,128)(4,1)S(1)} %broadcast_compare_fusion, bf16[176,1024]{1,0:T(8,128)(2,1)S(1)} %collective-permute-done.2), kind=kOutput, calls=%fused_computation.17 | convolution fusion | flops 513638400 | bytes 8904192 | tf_op jit(solution)/shard_map/gjqk,qgjd->kgd/dot_general | solution.py:81
  68.5 0.1 pad_maximum_fusion
  68.6 1.0 copy.95
  69.6 1.3 %convert_element_type.59 = bf16[64,22,256]{2,1,0:T(8,128)(2,1)} reshape(bf16[1408,1,2,128]{3,2,0,1:T(2,128)(2,1)S(1)} %copy.95) | data formatting | bytes 1441792 | tf_op jit(solution)/shard_map/convert_element_type | solution.py:87
  71.0 4.9 %all-to-all-start.1 = ((bf16[64,22,256]{2,1,0:T(8,128)(2,1)}), bf16[64,22,256]{2,1,0:T(8,128)(2,1)S(1)}, u32[]{:S(2)}, u32[]{:S(2)}) async-start(bf16[64,22,256]{2,1,0:T(8,128)(2,1)} %convert_element_type.59), calls=%async_computation.1 | async-start | bytes 1572864 | tf_op jit(solution)/shard_map/all_to_all | solution.py:86
  75.9 0.1 copy.88
  76.0 0.9 broadcast_in_dim_reshape.12
  76.9 3.3 %fusion.22 = bf16[176,1,8,128]{3,0,2,1:T(8,128)(2,1)S(1)} fusion(bf16[8,176,1408]{2,1,0:T(8,128)(2,1)} %copy-done.1, bf16[1408,1,1,128]{3,2,0,1:T(2,128)(2,1)S(1)} %get-tuple-element.11), kind=kOutput, calls=%fused_computation.21 | convolution fusion | flops 507871232 | bytes 4685824 | tf_op jit(solution)/shard_map/gjqk,kgd->qgjd/dot_general | solution.py:78
  80.2 0.1 copy.91
  80.3 0.9 broadcast_in_dim_reshape.13
  81.2 18.5 %all-to-all-done.1 = bf16[64,22,256]{2,1,0:T(8,128)(2,1)S(1)} async-done(((bf16[64,22,256]{2,1,0:T(8,128)(2,1)}), bf16[64,22,256]{2,1,0:T(8,128)(2,1)S(1)}, u32[]{:S(2)}, u32[]{:S(2)}) %all-to-all-start.1) | async-done | bytes 720928 | tf_op jit(solution)/shard_map/all_to_all | solution.py:86
  99.7 1.3 %copy_convert_fusion = f32[64,22,256]{2,0,1:T(8,128)} fusion(bf16[64,22,256]{2,1,0:T(8,128)(2,1)S(1)} %all-to-all-done.1), kind=kLoop, calls=%fused_computation.23 | loop fusion | flops 360448 | bytes 2162688 | tf_op jit(solution)/shard_map/convert_element_type | solution.py:90
  101.0 2.0 %reshape.201 = f32[8,8,22,2,128]{4,3,1,0,2:T(2,128)S(1)} reshape(f32[64,22,256]{2,0,1:T(8,128)} %copy_convert_fusion) | data formatting | bytes 2883584 | tf_op jit(solution)/shard_map/convert_element_type | solution.py:90
  103.0 0.7 reduce_sum.34
  103.7 0.8 slice_bitcast_fusion
  (18 shorter events, 0.2 us)
Async XLA Ops:
  0.6 31.3 %copy-start = (bf16[1,2,176,1024]{3,2,1,0:T(8,128)(2,1)S(1)}, bf16[1,2,176,1024]{3,2,1,0:T(8,128)(2,1)}, u32[]{:S(2)}) copy-start(bf16[1,2,176,1024]{3,2,1,0:T(8,128)(2,1)} %param.8) | copy-start | bytes 2162692
  5.6 14.0 %collective-permute-start = (bf16[22,2048]{1,0:T(8,128)(2,1)S(1)}, bf16[22,2048]{1,0:T(8,128)(2,1)S(1)}, u32[]{:S(2)}, u32[]{:S(2)}) collective-permute-start(bf16[22,2048]{1,0:T(8,128)(2,1)S(1)} %reshape.191), channel_id=1, source_target_pairs={{448,0},{0,64},{64,128},{128,192},{192,256},{256,320},{320,384},{3... | collective-permute-start | bytes 270344 | tf_op jit(solution)/shard_map/ppermute | solution.py:15
  10.4 24.9 %collective-permute-start.2 = (bf16[176,1024]{1,0:T(8,128)(2,1)}, bf16[176,1024]{1,0:T(8,128)(2,1)S(1)}, u32[]{:S(2)}, u32[]{:S(2)}) collective-permute-start(bf16[176,1024]{1,0:T(8,128)(2,1)} %bitcast.173), channel_id=1, source_target_pairs={{64,0},{128,64},{192,128},{256,192},{320,256},{384,320},{448,384},... | collective-permute-start | bytes 1081352 | tf_op jit(solution)/shard_map/ppermute | solution.py:15
  20.6 35.2 %all-to-all-start = ((bf16[64,22,256]{2,1,0:T(8,128)(2,1)}), bf16[64,22,256]{2,1,0:T(8,128)(2,1)S(1)}, u32[]{:S(2)}, u32[]{:S(2)}) async-start(bf16[64,22,256]{2,1,0:T(8,128)(2,1)} %bitcast.3), calls=%async_computation | async-start | bytes 1572864 | tf_op jit(solution)/shard_map/all_to_all | solution.py:49
  32.0 12.6 %collective-permute-start.1 = (bf16[176,1024]{1,0:T(8,128)(2,1)S(1)}, bf16[176,1024]{1,0:T(8,128)(2,1)S(1)}, u32[]{:S(2)}, u32[]{:S(2)}) collective-permute-start(bf16[176,1024]{1,0:T(8,128)(2,1)S(1)} %dynamic-slice_bitcast_fusion), channel_id=1, source_target_pairs={{448,0},{0,64},{64,128},{128,192},{192,256},{256,320},{320,384},{3... | collective-permute-start | bytes 1081352 | tf_op jit(solution)/shard_map/ppermute | solution.py:15
  57.1 4.0 %copy-start.2 = (f32[22,8,8,128]{3,2,1,0:T(8,128)S(1)}, f32[22,8,8,128]{3,2,1,0:T(8,128)}, u32[]{:S(2)}) copy-start(f32[22,8,8,128]{3,2,1,0:T(8,128)} %copy.106) | copy-start | bytes 2162692
  63.0 3.0 %copy-start.3 = (bf16[22,8,8,128]{3,2,1,0:T(8,128)(2,1)S(1)}, bf16[22,8,8,128]{3,2,1,0:T(8,128)(2,1)}, u32[]{:S(2)}) copy-start(bf16[22,8,8,128]{3,2,1,0:T(8,128)(2,1)} %copy.107) | copy-start | bytes 1081348
  65.9 2.6 %copy-start.1 = (bf16[8,176,1408]{2,1,0:T(8,128)(2,1)}, bf16[8,176,1408]{2,1,0:T(8,128)(2,1)S(1)}, u32[]{:S(2)}) copy-start(bf16[8,176,1408]{2,1,0:T(8,128)(2,1)S(1)} %fusion.6) | copy-start | bytes 11894788
  71.0 28.7 %all-to-all-start.1 = ((bf16[64,22,256]{2,1,0:T(8,128)(2,1)}), bf16[64,22,256]{2,1,0:T(8,128)(2,1)S(1)}, u32[]{:S(2)}, u32[]{:S(2)}) async-start(bf16[64,22,256]{2,1,0:T(8,128)(2,1)} %convert_element_type.59), calls=%async_computation.1 | async-start | bytes 1572864 | tf_op jit(solution)/shard_map/all_to_all | solution.py:86

commit v6 on v5

--- a/solution.py
+++ b/solution.py
@@ -15,7 +15,7 @@
     return lax.ppermute(block, axis, route)
 
 
-def body(block_order, plan, q_box, k_box, v_box, grad_out):
+def plane_step(block_order, plan, q_box, k_box, v_box, grad_out):
     tp_count = lax.axis_size("tp")
     ctx_count = lax.axis_size("ctx")
     section_count = lax.axis_size("section")
@@ -39,14 +39,16 @@
     kv_send = jnp.stack(
         [k_send.reshape(kv_rows, -1, head_size), v_send.reshape(kv_rows, -1, head_size)], axis=2
     ).reshape(kv_rows, -1)
-    queries, kv_rows_in = passed_along((q_send, kv_send), "section", 1)
-    cotangent = passed_along(grad_out[0], "section", -1)
+    kv_rows_in = passed_along(kv_send, "section", 1)
+    queries = passed_along(q_send, "section", 1)
 
     plane = ("ctx", "tp")
     kv_pieces = kv_rows_in.reshape(1, kv_rows, tp_count, 2 * kv_width).transpose(0, 2, 1, 3)
     kv_pieces = jnp.broadcast_to(kv_pieces, (ctx_count, tp_count, kv_rows, 2 * kv_width))
     kv_pieces = kv_pieces.reshape(ctx_count * tp_count * kv_rows, 2 * kv_width)
+    kv_pieces, do_send = lax.optimization_barrier((kv_pieces, grad_out[0]))
     kv_full = lax.all_to_all(kv_pieces, plane, split_axis=0, concat_axis=0, tiled=True)
+    cotangent = passed_along(do_send, "section", -1)
     kv_full = kv_full.reshape(seq_rows, kv_local, 2, head_size)
     key_heads = kv_full[:, :, 0, :]
     value_heads = kv_full[:, :, 1, :]
@@ -108,4 +110,4 @@
         P("section", ("ctx", "tp"), None),
         P("section", ("ctx", "tp"), None),
     )
-    return jax.shard_map(body, mesh=mesh, in_specs=in_specs, out_specs=out_specs, check_vma=False)
+    return jax.shard_map(plane_step, mesh=mesh, in_specs=in_specs, out_specs=out_specs, check_vma=False)

time: 105 us -> 108 us (1.029)
  local copies, waits for them, and re-layouts: 14.7 us -> 18.8 us
  starting transfers between devices: 31.6 us -> 27.8 us
  waiting for transfers between devices: 37.6 us -> 40.3 us
    ppermute x3, waiting for transfers between devices: 8.77 us -> 15 us  [passed_along(): return lax.ppermute(block, axis, route)]
    ppermute x3, starting transfers between devices: 15.3 us -> 11.5 us  [passed_along(): return lax.ppermute(block, axis, route)]
    all_to_all x2, waiting for transfers between devices: 28.8 us -> 25.3 us  [the longest x1 17.5 us: plane_step(): lax.all_to_all(grad_terms.astype(jnp.bfloat16), plane, split_axis=0, conc...]
    unnamed x13 -> x20, local copies, waits for them, and re-layouts: 1.88 us -> 4.57 us
    another operation x2 -> x3, other arithmetic: 0.09 us -> 1.5 us  [the longest x1 0.08 us: body(): jnp.stack([key_grad, value_grad], axis=2).reshape(seq_rows, 2 * kv_width)]
  transfers between devices with their start and end apart: 5 -> 5, of which waited for: 4 -> 5; matrix products, arithmetic and copies ran while one was open for 9% -> 9% of each run, Pallas kernels for 0% -> 0%
where the time goes in v6:
time: 108 us
  waiting for transfers between devices  40.3 us (37%)
  starting transfers between devices  27.8 us (26%)
  local copies, waits for them, and re-layouts  18.8 us (17%)
  matrix products  11.9 us (11%)
  other arithmetic  5.9 us (5%)
  between operations  2.98 us (3%)
    all_to_all x1, waiting for transfers between devices, plane_step(): lax.all_to_all(grad_terms.astype(jnp.bfloat16), plane, split_axis=0, conc...  17.5 us
    ppermute x3, waiting for transfers between devices, passed_along(): return lax.ppermute(block, axis, route)  15 us
    ppermute x3, starting transfers between devices, passed_along(): return lax.ppermute(block, axis, route)  11.5 us
    all_to_all x1, starting transfers between devices, plane_step(): lax.all_to_all(kv_pieces, plane, split_axis=0, concat_axis=0, tiled=True)  11.4 us
    all_to_all x1, waiting for transfers between devices, plane_step(): lax.all_to_all(kv_pieces, plane, split_axis=0, concat_axis=0, tiled=True)  7.8 us
    all_to_all x1, starting transfers between devices, plane_step(): lax.all_to_all(grad_terms.astype(jnp.bfloat16), plane, split_axis=0, conc...  4.93 us
    unnamed x20, local copies, waits for them, and re-layouts  4.57 us
    dot_general x1, matrix products, plane_step(): jnp.einsum('gjqk,kgd->qgjd', dscores, key_heads, preferred_element_type=j...  3.31 us
  transfers between devices with their start and end apart: 5, of which 5 were waited for; matrix products, arithmetic and copies ran while one was open for 9% of the time, Pallas kernels for 0%

profile of v6, /device:TPU:1, one launch (start us, length us, event | category | flops | bytes accessed | tf_op | source)
XLA Modules:
  0.0 107.6 jit_solution(16213849512678094424)
XLA Ops:
  0.7 1.3 %dynamic_slice.19 = s32[1]{0:T(128)} dynamic-slice(s32[8]{0:T(128)} %param.7, s32[]{:T(128)S(6)} %select_n.33), dynamic_slice_sizes={1} | dynamic-slice | bytes 12 | tf_op jit(solution)/shard_map/jit(dynamic_index_in_dim)/dynamic_slice | solution.py:35
  4.0 1.5 %dynamic-slice_reduce_fusion = (bf16[22,1024]{1,0:T(8,128)(2,1)S(1)}, bf16[22,1024]{1,0:T(8,128)(2,1)S(1)}) fusion(bf16[1,2,22,1024]{3,1,2,0:T(2,128)(2,1)} %param.10, s32[]{:T(128)S(6)} %select_n.34, bf16[1,2,22,1024]{3,1,2,0:T(2,128)(2,1)} %param.9), kind=kLoop, calls=%fused_computation.41 | loop fusion | bytes 180228 | tf_op jit(solution)/shard_map/jit(dynamic_index_in_dim)/dynamic_slice | solution.py:38
  5.5 0.1 copy.77
  5.6 4.8 %collective-permute-start = (bf16[22,2048]{1,0:T(8,128)(2,1)S(1)}, bf16[22,2048]{1,0:T(8,128)(2,1)S(1)}, u32[]{:S(2)}, u32[]{:S(2)}) collective-permute-start(bf16[22,2048]{1,0:T(8,128)(2,1)S(1)} %reshape.192), channel_id=1, source_target_pairs={{448,0},{0,64},{64,128},{128,192},{192,256},{256,320},{320,384},{3... | collective-permute-start | bytes 270344 | tf_op jit(solution)/shard_map/ppermute | solution.py:15
  10.5 9.2 %collective-permute-done = bf16[22,2048]{1,0:T(8,128)(2,1)S(1)} collective-permute-done((bf16[22,2048]{1,0:T(8,128)(2,1)S(1)}, bf16[22,2048]{1,0:T(8,128)(2,1)S(1)}, u32[]{:S(2)}, u32[]{:S(2)}) %collective-permute-start) | collective-permute-done | bytes 90144 | tf_op jit(solution)/shard_map/ppermute | solution.py:15
  19.7 0.2 reshape.194
  19.9 1.1 %all_to_all.10 = bf16[64,22,256]{2,1,0:T(8,128)(2,1)} reshape(bf16[1408,256]{1,0:T(8,128)(2,1)S(1)} %reshape.194) | data formatting | bytes 1441792 | tf_op jit(solution)/shard_map/all_to_all | solution.py:50
  21.0 11.4 %all-to-all-start = ((bf16[64,22,256]{2,1,0:T(8,128)(2,1)}), bf16[64,22,256]{2,1,0:T(8,128)(2,1)S(1)}, u32[]{:S(2)}, u32[]{:S(2)}) async-start(bf16[64,22,256]{2,1,0:T(8,128)(2,1)} %all_to_all.10), calls=%async_computation | async-start | bytes 1572864 | tf_op jit(solution)/shard_map/all_to_all | solution.py:50
  32.4 1.9 %collective-permute-start.1 = (bf16[176,1024]{1,0:T(8,128)(2,1)S(1)}, bf16[176,1024]{1,0:T(8,128)(2,1)S(1)}, u32[]{:S(2)}, u32[]{:S(2)}) collective-permute-start(bf16[176,1024]{1,0:T(8,128)(2,1)S(1)} %dynamic-slice_bitcast_fusion), channel_id=1, source_target_pairs={{448,0},{0,64},{64,128},{128,192},{192,256},{256,320},{320,384},{3... | collective-permute-start | bytes 1081352 | tf_op jit(solution)/shard_map/ppermute | solution.py:15
  34.4 0.1 add.77
  34.5 0.1 add.73
  34.6 0.1 add.74
  34.6 0.1 add.75
  34.7 0.1 iota_add_fusion
  34.8 0.1 add.72
  34.9 4.8 %collective-permute-start.2 = (bf16[176,1024]{1,0:T(8,128)(2,1)S(1)}, bf16[176,1024]{1,0:T(8,128)(2,1)S(1)}, u32[]{:S(2)}, u32[]{:S(2)}) collective-permute-start(bf16[176,1024]{1,0:T(8,128)(2,1)S(1)} %bitcast.167), channel_id=1, source_target_pairs={{64,0},{128,64},{192,128},{256,192},{320,256},{384,320},{448,384},... | collective-permute-start | bytes 1081352 | tf_op jit(solution)/shard_map/ppermute | solution.py:15
  39.7 0.2 broadcast_compare_fusion
  39.9 5.2 %collective-permute-done.1 = bf16[176,1024]{1,0:T(8,128)(2,1)S(1)} collective-permute-done((bf16[176,1024]{1,0:T(8,128)(2,1)S(1)}, bf16[176,1024]{1,0:T(8,128)(2,1)S(1)}, u32[]{:S(2)}, u32[]{:S(2)}) %collective-permute-start.1) | collective-permute-done | bytes 360480 | tf_op jit(solution)/shard_map/ppermute | solution.py:15
  45.1 0.8 copy.98
  45.9 0.6 collective-permute-done.2
  46.5 0.8 copy.99
  47.3 0.1 convert_bitcast_fusion
  47.4 1.0 copy.97
  48.4 7.8 %all-to-all-done = bf16[64,22,256]{2,1,0:T(8,128)(2,1)S(1)} async-done(((bf16[64,22,256]{2,1,0:T(8,128)(2,1)}), bf16[64,22,256]{2,1,0:T(8,128)(2,1)S(1)}, u32[]{:S(2)}, u32[]{:S(2)}) %all-to-all-start) | async-done | bytes 720928 | tf_op jit(solution)/shard_map/all_to_all | solution.py:50
  56.2 0.3 reshape.195
  56.5 1.1 fusion.37
  57.6 1.9 %fusion.38 = (f32[8,176]{1,0:T(8,128)S(1)}, f32[1,8,176,1408]{3,2,1,0:T(8,128)S(1)}) fusion(bf16[1408,1,1,128]{3,2,0,1:T(2,128)(2,1)S(1)} %get-tuple-element.15, pred[176,1408]{1,0:T(8,128)(4,1)S(1)} %broadcast_compare_fusion, bf16[176,1024]{1,0:T(8,128)(2,1)S(1)} %collective-permute-done.1), kind=kOutput, calls=%fused_computation.50 | convolution fusion | flops 513456768 | bytes 8904192 | tf_op jit(solution)/shard_map/qgjd,kgd->gjqk/dot_general | solution.py:66
  59.4 2.0 %select_reduce_fusion = f32[8,176]{1,0:T(8,128)S(1)} fusion(f32[1,8,176,1408]{3,2,1,0:T(8,128)S(1)} %get-tuple-element.19, f32[8,176]{1,0:T(8,128)S(1)} %get-tuple-element.18, pred[176,1408]{1,0:T(8,128)(4,1)S(1)} %broadcast_compare_fusion), kind=kLoop, calls=%fused_computation.5 | loop fusion | flops 5945984 | bytes 8188928 | tf_op jit(solution)/shard_map/reduce_sum | solution.py:69
  61.5 1.4 %fusion.3 = bf16[8,176,1408]{2,1,0:T(8,128)(2,1)S(1)} fusion(f32[1,8,176,1408]{3,2,1,0:T(8,128)S(1)} %get-tuple-element.19, f32[8,176]{1,0:T(8,128)S(1)} %log_add_fusion, pred[176,1408]{1,0:T(8,128)(4,1)S(1)} %broadcast_compare_fusion), kind=kLoop, calls=%fused_computation.7 | loop fusion | flops 5947392 | bytes 12148224 | tf_op jit(solution)/shard_map/reshape.30
  62.9 0.9 fusion.27
  63.8 2.0 %fusion.32 = (f32[176,8]{0,1:T(8,128)S(1)}, bf16[176,1,8,128]{3,0,2,1:T(8,128)(2,1)}) fusion(f32[176,1,8,128]{3,2,0,1:T(8,128)S(1)} %bitcast.154, bf16[8,176,1408]{2,1,0:T(8,128)(2,1)S(1)} %fusion.3, bf16[1408,1,1,128]{3,2,0,1:T(2,128)(2,1)S(1)} %get-tuple-element.14), kind=kOutput, calls=%fused_computation.27 | convolution fusion | flops 508050048 | bytes 5412352 | tf_op jit(solution)/shard_map/gjqk,kgd->qgjd/dot_general | solution.py:73
  65.9 2.9 %fusion.8 = bf16[8,176,1408]{2,1,0:T(8,128)(2,1)S(1)} fusion(f32[8,176]{1,0:T(8,128)S(1)} %bitcast.165, f32[1,8,176,1408]{3,2,1,0:T(8,128)S(1)} %get-tuple-element.19, f32[8,176]{1,0:T(8,128)S(1)} %log_add_fusion, pred[176,1408]{1,0:T(8,128)(4,1)S(1)} %broadcast_compare_fusion, bf16[1408,1,1,128]{3,2,0,1:T(2,128)(2,1)S(1)} %get-tuple-element.14, ...), kind=kOutput, calls=%fused_computation.12 | convolution fusion | flops 517423104 | bytes 12874752 | tf_op jit(solution)/shard_map/qgjd,kgd->gjqk/dot_general | solution.py:77
  68.8 1.9 %copy-done.1 = bf16[8,176,1408]{2,1,0:T(8,128)(2,1)} copy-done((bf16[8,176,1408]{2,1,0:T(8,128)(2,1)}, bf16[8,176,1408]{2,1,0:T(8,128)(2,1)S(1)}, u32[]{:S(2)}) %copy-start.1) | copy-done | bytes 3964952
  70.6 0.9 fusion.24
  71.5 0.1 pad_maximum_fusion
  71.6 1.0 copy.88
  72.6 1.3 %convert_element_type.59 = bf16[64,22,256]{2,1,0:T(8,128)(2,1)} reshape(bf16[1408,1,2,128]{3,2,0,1:T(2,128)(2,1)S(1)} %copy.88) | data formatting | bytes 1441792 | tf_op jit(solution)/shard_map/convert_element_type | solution.py:89
  74.0 4.9 %all-to-all-start.1 = ((bf16[64,22,256]{2,1,0:T(8,128)(2,1)}), bf16[64,22,256]{2,1,0:T(8,128)(2,1)S(1)}, u32[]{:S(2)}, u32[]{:S(2)}) async-start(bf16[64,22,256]{2,1,0:T(8,128)(2,1)} %convert_element_type.59), calls=%async_computation.1 | async-start | bytes 1572864 | tf_op jit(solution)/shard_map/all_to_all | solution.py:88
  78.9 3.3 %fusion.31 = bf16[176,1,8,128]{3,0,2,1:T(8,128)(2,1)S(1)} fusion(bf16[8,176,1408]{2,1,0:T(8,128)(2,1)} %copy-done.1, bf16[1408,1,1,128]{3,2,0,1:T(2,128)(2,1)S(1)} %get-tuple-element.15), kind=kOutput, calls=%fused_computation.23 | convolution fusion | flops 507871232 | bytes 4685824 | tf_op jit(solution)/shard_map/gjqk,kgd->qgjd/dot_general | solution.py:80
  82.3 0.1 copy.85
  82.4 0.9 broadcast_in_dim_reshape.13
  83.2 1.1 %copy.82 = bf16[176,1,8,128]{3,2,0,1:T(8,128)(2,1)S(1)} copy(bf16[176,1,8,128]{3,0,2,1:T(8,128)(2,1)} %get-tuple-element.13) | data formatting | bytes 720896 | tf_op jit(solution)/shard_map/convert_element_type | solution.py:85
  84.3 0.9 broadcast_in_dim_reshape.12
  85.2 17.5 %all-to-all-done.1 = bf16[64,22,256]{2,1,0:T(8,128)(2,1)S(1)} async-done(((bf16[64,22,256]{2,1,0:T(8,128)(2,1)}), bf16[64,22,256]{2,1,0:T(8,128)(2,1)S(1)}, u32[]{:S(2)}, u32[]{:S(2)}) %all-to-all-start.1) | async-done | bytes 720928 | tf_op jit(solution)/shard_map/all_to_all | solution.py:88
  102.7 1.3 %copy_convert_fusion = f32[64,22,256]{2,0,1:T(8,128)} fusion(bf16[64,22,256]{2,1,0:T(8,128)(2,1)S(1)} %all-to-all-done.1), kind=kLoop, calls=%fused_computation.25 | loop fusion | flops 360448 | bytes 2162688 | tf_op jit(solution)/shard_map/convert_element_type | solution.py:92
  104.0 2.0 %reshape.203 = f32[8,8,22,2,128]{4,3,1,0,2:T(2,128)S(1)} reshape(f32[64,22,256]{2,0,1:T(8,128)} %copy_convert_fusion) | data formatting | bytes 2883584 | tf_op jit(solution)/shard_map/convert_element_type | solution.py:92
  106.0 0.7 reduce_sum.34
  106.8 0.8 slice_bitcast_fusion
  (28 shorter events, 0.3 us)
Async XLA Ops:
  0.6 31.8 %copy-start = (bf16[1,2,176,1024]{3,2,1,0:T(8,128)(2,1)S(1)}, bf16[1,2,176,1024]{3,2,1,0:T(8,128)(2,1)}, u32[]{:S(2)}) copy-start(bf16[1,2,176,1024]{3,2,1,0:T(8,128)(2,1)} %param.8) | copy-start | bytes 2162692
  0.6 34.3 %copy-start.5 = (bf16[1,176,1024]{2,1,0:T(8,128)(2,1)S(1)}, bf16[1,176,1024]{2,1,0:T(8,128)(2,1)}, u32[]{:S(2)}) copy-start(bf16[1,176,1024]{2,1,0:T(8,128)(2,1)} %param.11) | copy-start | bytes 1081348
  0.7 33.8 %copy-start.6 = (s32[16]{0:T(128)S(1)}, s32[16]{0:T(128)}, u32[]{:S(2)}) copy-start(s32[16]{0:T(128)} %param.6) | copy-start | bytes 196
  5.6 14.0 %collective-permute-start = (bf16[22,2048]{1,0:T(8,128)(2,1)S(1)}, bf16[22,2048]{1,0:T(8,128)(2,1)S(1)}, u32[]{:S(2)}, u32[]{:S(2)}) collective-permute-start(bf16[22,2048]{1,0:T(8,128)(2,1)S(1)} %reshape.192), channel_id=1, source_target_pairs={{448,0},{0,64},{64,128},{128,192},{192,256},{256,320},{320,384},{3... | collective-permute-start | bytes 270344 | tf_op jit(solution)/shard_map/ppermute | solution.py:15
  21.0 35.2 %all-to-all-start = ((bf16[64,22,256]{2,1,0:T(8,128)(2,1)}), bf16[64,22,256]{2,1,0:T(8,128)(2,1)S(1)}, u32[]{:S(2)}, u32[]{:S(2)}) async-start(bf16[64,22,256]{2,1,0:T(8,128)(2,1)} %all_to_all.10), calls=%async_computation | async-start | bytes 1572864 | tf_op jit(solution)/shard_map/all_to_all | solution.py:50
  32.4 12.6 %collective-permute-start.1 = (bf16[176,1024]{1,0:T(8,128)(2,1)S(1)}, bf16[176,1024]{1,0:T(8,128)(2,1)S(1)}, u32[]{:S(2)}, u32[]{:S(2)}) collective-permute-start(bf16[176,1024]{1,0:T(8,128)(2,1)S(1)} %dynamic-slice_bitcast_fusion), channel_id=1, source_target_pairs={{448,0},{0,64},{64,128},{128,192},{192,256},{256,320},{320,384},{3... | collective-permute-start | bytes 1081352 | tf_op jit(solution)/shard_map/ppermute | solution.py:15
  34.9 11.6 %collective-permute-start.2 = (bf16[176,1024]{1,0:T(8,128)(2,1)S(1)}, bf16[176,1024]{1,0:T(8,128)(2,1)S(1)}, u32[]{:S(2)}, u32[]{:S(2)}) collective-permute-start(bf16[176,1024]{1,0:T(8,128)(2,1)S(1)} %bitcast.167), channel_id=1, source_target_pairs={{64,0},{128,64},{192,128},{256,192},{320,256},{384,320},{448,384},... | collective-permute-start | bytes 1081352 | tf_op jit(solution)/shard_map/ppermute | solution.py:15
  61.5 1.5 %copy-start.4 = (bf16[22,8,8,128]{3,2,1,0:T(8,128)(2,1)S(1)}, bf16[22,8,8,128]{3,2,1,0:T(8,128)(2,1)}, u32[]{:S(2)}) copy-start(bf16[22,8,8,128]{3,2,1,0:T(8,128)(2,1)} %copy.99) | copy-start | bytes 1081348
  61.5 2.3 %copy-start.2 = (f32[22,8,8,128]{3,2,1,0:T(8,128)S(1)}, f32[22,8,8,128]{3,2,1,0:T(8,128)}, u32[]{:S(2)}) copy-start(f32[22,8,8,128]{3,2,1,0:T(8,128)} %copy.97) | copy-start | bytes 2162692
  63.8 6.8 %copy-start.3 = (bf16[22,8,8,128]{3,2,1,0:T(8,128)(2,1)S(1)}, bf16[22,8,8,128]{3,2,1,0:T(8,128)(2,1)}, u32[]{:S(2)}) copy-start(bf16[22,8,8,128]{3,2,1,0:T(8,128)(2,1)} %copy.98) | copy-start | bytes 1081348
  68.8 1.9 %copy-start.1 = (bf16[8,176,1408]{2,1,0:T(8,128)(2,1)}, bf16[8,176,1408]{2,1,0:T(8,128)(2,1)S(1)}, u32[]{:S(2)}) copy-start(bf16[8,176,1408]{2,1,0:T(8,128)(2,1)S(1)} %fusion.8) | copy-start | bytes 11894788
  74.0 28.7 %all-to-all-start.1 = ((bf16[64,22,256]{2,1,0:T(8,128)(2,1)}), bf16[64,22,256]{2,1,0:T(8,128)(2,1)S(1)}, u32[]{:S(2)}, u32[]{:S(2)}) async-start(bf16[64,22,256]{2,1,0:T(8,128)(2,1)} %convert_element_type.59), calls=%async_computation.1 | async-start | bytes 1572864 | tf_op jit(solution)/shard_map/all_to_all | solution.py:88

commit v7 on v3

--- a/solution.py
+++ b/solution.py
@@ -1,12 +1,90 @@
+import functools
+
 import jax
 import jax.numpy as jnp
 from jax import lax
 from jax.sharding import PartitionSpec as P
+from jax.experimental import pallas as pl
+from jax.experimental.pallas import tpu as pltpu
 
 HEAD_DIM = 128
 
 
 NEG = -1e30
+
+
+NT = (((1,), (1,)), ((), ()))
+
+
+def head_kernel(scale, qpos_ref, kpos_ref, q_ref, do_ref, k_ref, v_ref, att_ref, dq_ref, dkv_ref, acc_ref):
+    h = pl.program_id(0)
+    width = k_ref.shape[1]
+
+    @pl.when(h == 0)
+    def _():
+        acc_ref[...] = jnp.zeros_like(acc_ref)
+
+    q = q_ref[...]
+    do = do_ref[...]
+    k = k_ref[...]
+    v = v_ref[...]
+    visible = kpos_ref[...] <= qpos_ref[...]
+    scores = lax.dot_general(q, k, NT, preferred_element_type=jnp.float32) * scale
+    scores = jnp.where(visible, scores, NEG)
+    top = jnp.max(scores, axis=1, keepdims=True)
+    totals = jnp.sum(jnp.where(visible, jnp.exp(scores - top), 0.0), axis=1, keepdims=True)
+    log_total = top + jnp.log(totals)
+    probs = jnp.where(visible, jnp.exp(scores - log_total), 0.0)
+    probs_low = probs.astype(jnp.bfloat16)
+    attended = jnp.dot(probs_low, v, preferred_element_type=jnp.float32)
+    att_ref[...] = attended.astype(att_ref.dtype)
+    delta = jnp.sum(do.astype(jnp.float32) * attended, axis=1, keepdims=True)
+    dprobs = lax.dot_general(do, v, NT, preferred_element_type=jnp.float32)
+    dscores_f = probs * (dprobs - delta)
+    dscores = dscores_f.astype(jnp.bfloat16)
+    dq = jnp.dot(dscores, k, preferred_element_type=jnp.float32) * scale
+    dq_ref[...] = dq.astype(dq_ref.dtype)
+    acc_ref[:, :width] += jnp.dot(
+        dscores_f.T.astype(jnp.bfloat16), q, preferred_element_type=jnp.float32
+    )
+    acc_ref[:, width:] += jnp.dot(probs.T.astype(jnp.bfloat16), do, preferred_element_type=jnp.float32)
+
+    @pl.when(h == pl.num_programs(0) - 1)
+    def _():
+        dkv_ref[:, :width] = (acc_ref[:, :width] * scale).astype(dkv_ref.dtype)
+        dkv_ref[:, width:] = acc_ref[:, width:].astype(dkv_ref.dtype)
+
+
+def head_attention(queries, cotangent, kv_full, query_pos, key_pos, head_size):
+    rows, features = queries.shape
+    seq = kv_full.shape[0]
+    heads = features // head_size
+    scale = head_size ** (-0.5)
+    head_block = pl.BlockSpec((rows, head_size), lambda h: (0, h))
+    flops = heads * 6 * 2 * rows * seq * head_size
+    return pl.pallas_call(
+        functools.partial(head_kernel, scale),
+        grid=(heads,),
+        in_specs=[
+            pl.BlockSpec((rows, 1), lambda h: (0, 0)),
+            pl.BlockSpec((1, seq), lambda h: (0, 0)),
+            head_block,
+            head_block,
+            pl.BlockSpec((seq, head_size), lambda h: (0, 0)),
+            pl.BlockSpec((seq, head_size), lambda h: (0, 1)),
+        ],
+        out_specs=[head_block, head_block, pl.BlockSpec((seq, 2 * head_size), lambda h: (0, 0))],
+        out_shape=[
+            jax.ShapeDtypeStruct((rows, features), jnp.bfloat16),
+            jax.ShapeDtypeStruct((rows, features), jnp.bfloat16),
+            jax.ShapeDtypeStruct((seq, 2 * head_size), jnp.bfloat16),
+        ],
+        scratch_shapes=[pltpu.VMEM((seq, 2 * head_size), jnp.float32)],
+        compiler_params=pltpu.CompilerParams(dimension_semantics=("arbitrary",)),
+        cost_estimate=pl.CostEstimate(
+            flops=flops, transcendentals=2 * heads * rows * seq, bytes_accessed=4 * rows * features * 2 + seq * 2 * head_size * 4
+        ),
+    )(query_pos.reshape(rows, 1), key_pos.reshape(1, seq), queries, cotangent, kv_full, kv_full)
 
 
 def passed_along(block, axis, distance):
@@ -47,9 +125,6 @@
     kv_pieces = jnp.broadcast_to(kv_pieces, (ctx_count, tp_count, kv_rows, 2 * kv_width))
     kv_pieces = kv_pieces.reshape(ctx_count * tp_count * kv_rows, 2 * kv_width)
     kv_full = lax.all_to_all(kv_pieces, plane, split_axis=0, concat_axis=0, tiled=True)
-    kv_full = kv_full.reshape(seq_rows, kv_local, 2, head_size)
-    key_heads = kv_full[:, :, 0, :]
-    value_heads = kv_full[:, :, 1, :]
     ctx_rank = lax.axis_index("ctx")
 
     positions = (
@@ -57,35 +132,13 @@
     ).reshape(ctx_count, tok_rows)
     key_pos = positions.reshape(seq_rows)
     query_pos = lax.dynamic_index_in_dim(positions, ctx_rank, 0, keepdims=False)
-    visible = (key_pos[None, :] <= query_pos[:, None])[None, None]
+    attended_flat, q_grad_flat, grad_terms = head_attention(
+        queries, cotangent, kv_full.reshape(seq_rows, 2 * kv_width), query_pos, key_pos, head_size
+    )
 
-    q4 = queries.reshape(tok_rows, kv_local, group, head_size)
-    do4 = cotangent.reshape(tok_rows, kv_local, group, head_size)
-    scores = jnp.einsum("qgjd,kgd->gjqk", q4, key_heads, preferred_element_type=jnp.float32) * scale
-    scores = jnp.where(visible, scores, NEG)
-    top_score = jnp.max(scores, axis=-1, keepdims=True)
-    totals = jnp.sum(jnp.where(visible, jnp.exp(scores - top_score), 0.0), axis=-1, keepdims=True)
-    log_total = top_score + jnp.log(totals)
-    probs = jnp.where(visible, jnp.exp(scores - log_total), 0.0)
-    probs_low = probs.astype(jnp.bfloat16)
-    attended = jnp.einsum(
-        "gjqk,kgd->qgjd", probs_low, value_heads, preferred_element_type=jnp.float32
-    )
-    delta = jnp.sum(do4.astype(jnp.float32) * attended, axis=-1)
-    dprobs = jnp.einsum("qgjd,kgd->gjqk", do4, value_heads, preferred_element_type=jnp.float32)
-    dscores = (probs * (dprobs - jnp.transpose(delta, (1, 2, 0))[..., None])).astype(jnp.bfloat16)
-    q_grad = (
-        jnp.einsum("gjqk,kgd->qgjd", dscores, key_heads, preferred_element_type=jnp.float32) * scale
-    ).astype(jnp.bfloat16)
-    key_grad = jnp.einsum("gjqk,qgjd->kgd", dscores, q4, preferred_element_type=jnp.float32) * scale
-    value_grad = jnp.einsum("gjqk,qgjd->kgd", probs_low, do4, preferred_element_type=jnp.float32)
-
-    attended_flat = attended.astype(jnp.bfloat16).reshape(tok_rows, heads_local * head_size)
-    q_grad_flat = q_grad.reshape(tok_rows, heads_local * head_size)
-    grad_terms = jnp.stack([key_grad, value_grad], axis=2).reshape(seq_rows, 2 * kv_width)
     grad_parts = lax.all_to_all(grad_terms, plane, split_axis=0, concat_axis=0, tiled=True)
     grad_parts = grad_parts.reshape(ctx_count, tp_count, kv_rows, kv_local, 2, head_size)
-    own_grads = jnp.sum(grad_parts, axis=0)
+    own_grads = jnp.sum(grad_parts.astype(jnp.float32), axis=0)
     k_grad_tokens = own_grads[:, :, :, 0, :].transpose(1, 0, 2, 3).reshape(kv_rows, -1)
     v_grad_tokens = own_grads[:, :, :, 1, :].transpose(1, 0, 2, 3).reshape(kv_rows, -1)
     return (attended_flat[None], q_grad_flat[None], k_grad_tokens[None], v_grad_tokens[None])

time: 125 us -> 111 us (0.89)
  blocking collectives: 0 us -> 28.5 us
  waiting for transfers between devices: 51.7 us -> 24.5 us
  Pallas kernels: 0 us -> 17.6 us
  matrix products: 14.1 us -> 0 us
  starting transfers between devices: 31.6 us -> 22.7 us
  local copies, waits for them, and re-layouts: 18.6 us -> 12.4 us
  other arithmetic: 5.03 us -> 2.13 us
    all_to_all x1 -> x0, waiting for transfers between devices: 32.7 us -> none  [body(): lax.all_to_all(grad_terms, plane, split_axis=0, concat_axis=0, tiled=True)]
    all_to_all x0 -> x1, blocking collectives: none -> 28.5 us  [body(): lax.all_to_all(grad_terms, plane, split_axis=0, concat_axis=0, tiled=True)]
    pallas_call x0 -> x1, Pallas kernels: none -> 17.6 us  [head_attention(): pl.pallas_call(functools.partial(head_kernel, scale), grid=(heads,), in_s...]
    dot_general x6 -> x0, matrix products: 14.1 us -> none  [the longest x1 3.31 us: body(): jnp.einsum('gjqk,kgd->qgjd', dscores, key_heads, preferred_element_type=j...]
    all_to_all x1, waiting for transfers between devices: 10.3 us -> 15.4 us  [body(): lax.all_to_all(kv_pieces, plane, split_axis=0, concat_axis=0, tiled=True)]
    all_to_all x1 -> x0, starting transfers between devices: 4.93 us -> none  [body(): lax.all_to_all(grad_terms, plane, split_axis=0, concat_axis=0, tiled=True)]
    ppermute x3, starting transfers between devices: 15.3 us -> 11.3 us  [passed_along(): return lax.ppermute(block, axis, route)]
    another operation x3 -> x0, local copies, waits for them, and re-layouts: 3.94 us -> none  [the longest x1 2.15 us: body(): jnp.stack([key_grad, value_grad], axis=2).reshape(seq_rows, 2 * kv_width)]
  transfers between devices with their start and end apart: 5 -> 4, of which waited for: 4 -> 2; matrix products, arithmetic and copies ran while one was open for 9% -> 2% of each run, Pallas kernels for 0% -> 0%
where the time goes in v7:
time: 111 us
  blocking collectives  28.5 us (26%)
  waiting for transfers between devices  24.5 us (22%)
  starting transfers between devices  22.7 us (20%)
  Pallas kernels  17.6 us (16%)
  local copies, waits for them, and re-layouts  12.4 us (11%)
  between operations  2.8 us (3%)
  other arithmetic  2.13 us (2%)
    all_to_all x1, blocking collectives, body(): lax.all_to_all(grad_terms, plane, split_axis=0, concat_axis=0, tiled=True)  28.5 us
    pallas_call x1, Pallas kernels, head_attention(): pl.pallas_call(functools.partial(head_kernel, scale), grid=(heads,), in_s...  17.6 us
    all_to_all x1, waiting for transfers between devices, body(): lax.all_to_all(kv_pieces, plane, split_axis=0, concat_axis=0, tiled=True)  15.4 us
    all_to_all x1, starting transfers between devices, body(): lax.all_to_all(kv_pieces, plane, split_axis=0, concat_axis=0, tiled=True)  11.4 us
    ppermute x3, starting transfers between devices, passed_along(): return lax.ppermute(block, axis, route)  11.3 us
    ppermute x3, waiting for transfers between devices, passed_along(): return lax.ppermute(block, axis, route)  9.16 us
  transfers between devices with their start and end apart: 4, of which 2 were waited for; matrix products, arithmetic and copies ran while one was open for 2% of the time, Pallas kernels for 0%

profile of v7, /device:TPU:1, one launch (start us, length us, event | category | flops | bytes accessed | tf_op | source)
XLA Modules:
  0.0 110.6 jit_solution(10549936378383891160)
XLA Ops:
  0.6 0.0 copy-start
  0.7 1.3 %dynamic_slice.20 = s32[1]{0:T(128)} dynamic-slice(s32[8]{0:T(128)} %param.7, s32[]{:T(128)S(6)} %select_n.24), dynamic_slice_sizes={1} | dynamic-slice | bytes 12 | tf_op jit(solution)/shard_map/jit(dynamic_index_in_dim)/dynamic_slice | solution.py:113
  3.9 1.5 %dynamic-slice_reduce_fusion = (bf16[22,1024]{1,0:T(8,128)(2,1)S(1)}, bf16[22,1024]{1,0:T(8,128)(2,1)S(1)}) fusion(bf16[1,2,22,1024]{3,1,2,0:T(2,128)(2,1)} %param.10, s32[]{:T(128)S(6)} %select_n.25, bf16[1,2,22,1024]{3,1,2,0:T(2,128)(2,1)} %param.9), kind=kLoop, calls=%fused_computation.6 | loop fusion | bytes 180228 | tf_op jit(solution)/shard_map/jit(dynamic_index_in_dim)/dynamic_slice | solution.py:116
  5.5 0.1 copy.28
  5.6 4.8 %collective-permute-start.2 = (bf16[22,2048]{1,0:T(8,128)(2,1)S(1)}, bf16[22,2048]{1,0:T(8,128)(2,1)S(1)}, u32[]{:S(2)}, u32[]{:S(2)}) collective-permute-start(bf16[22,2048]{1,0:T(8,128)(2,1)S(1)} %reshape.80), channel_id=1, source_target_pairs={{448,0},{0,64},{64,128},{128,192},{192,256},{256,320},{320,384},{3... | collective-permute-start | bytes 270344 | tf_op jit(solution)/shard_map/ppermute | solution.py:93
  10.4 9.2 %collective-permute-done.2 = bf16[22,2048]{1,0:T(8,128)(2,1)S(1)} collective-permute-done((bf16[22,2048]{1,0:T(8,128)(2,1)S(1)}, bf16[22,2048]{1,0:T(8,128)(2,1)S(1)}, u32[]{:S(2)}, u32[]{:S(2)}) %collective-permute-start.2) | collective-permute-done | bytes 90144 | tf_op jit(solution)/shard_map/ppermute | solution.py:93
  19.6 0.0 copy-start.1
  19.7 0.0 copy-start.4
  19.7 0.9 broadcast_in_dim.16
  20.6 11.4 %all-to-all-start = ((bf16[64,22,256]{2,1,0:T(8,128)(2,1)}), bf16[64,22,256]{2,1,0:T(8,128)(2,1)S(1)}, u32[]{:S(2)}, u32[]{:S(2)}) async-start(bf16[64,22,256]{2,1,0:T(8,128)(2,1)} %bitcast.6), calls=%async_computation | async-start | bytes 1572864 | tf_op jit(solution)/shard_map/all_to_all | solution.py:127
  32.0 0.0 copy-done
  32.0 1.9 %collective-permute-start = (bf16[176,1024]{1,0:T(8,128)(2,1)S(1)}, bf16[176,1024]{1,0:T(8,128)(2,1)S(1)}, u32[]{:S(2)}, u32[]{:S(2)}) collective-permute-start(bf16[176,1024]{1,0:T(8,128)(2,1)S(1)} %dynamic-slice_bitcast_fusion), channel_id=1, source_target_pairs={{448,0},{0,64},{64,128},{128,192},{192,256},{256,320},{320,384},{3... | collective-permute-start | bytes 1081352 | tf_op jit(solution)/shard_map/ppermute | solution.py:93
  34.0 0.0 copy-done.1
  34.0 4.6 %collective-permute-start.1 = (bf16[176,1024]{1,0:T(8,128)(2,1)S(1)}, bf16[176,1024]{1,0:T(8,128)(2,1)S(1)}, u32[]{:S(2)}, u32[]{:S(2)}) collective-permute-start(bf16[176,1024]{1,0:T(8,128)(2,1)S(1)} %bitcast.52), channel_id=1, source_target_pairs={{64,0},{128,64},{192,128},{256,192},{320,256},{384,320},{448,384},... | collective-permute-start | bytes 1081352 | tf_op jit(solution)/shard_map/ppermute | solution.py:93
  38.6 0.1 add.64
  38.7 0.0 copy-done.4
  38.7 0.1 add.60
  38.7 0.1 add.61
  38.8 0.1 add.62
  38.9 0.1 iota_add_fusion
  39.0 0.7 add.71.kpos_ref
  39.7 0.8 copy.30.qpos_ref
  40.4 15.4 %all-to-all-done = bf16[64,22,256]{2,1,0:T(8,128)(2,1)S(1)} async-done(((bf16[64,22,256]{2,1,0:T(8,128)(2,1)}), bf16[64,22,256]{2,1,0:T(8,128)(2,1)S(1)}, u32[]{:S(2)}, u32[]{:S(2)}) %all-to-all-start) | async-done | bytes 720928 | tf_op jit(solution)/shard_map/all_to_all | solution.py:127
  55.8 1.1 all_to_all.15.k_ref.v_ref
  56.9 0.0 collective-permute-done.q_ref
  56.9 0.0 copy-start.2
  56.9 0.0 collective-permute-done.1.do_ref
  56.9 0.7 copy-done.2
  57.6 0.0 copy-start.3
  57.6 0.7 copy-done.3
  58.3 17.6 %shard_map.93 = (bf16[176,1024]{1,0:T(8,128)(2,1)}, bf16[176,1024]{1,0:T(8,128)(2,1)}, bf16[1408,256]{1,0:T(8,128)(2,1)}) custom-call(s32[176,1]{1,0:T(8,128)} %copy.30.qpos_ref, s32[1,1408]{1,0:T(1,128)} %add.71.kpos_ref, bf16[176,1024]{1,0:T(8,128)(2,1)} %copy-done.2, bf16[176,1024]{1,0:T(8,128)(2,1)} %copy-done.3, ...), custom_call_target="tpu_custom_call" | custom-call | flops 3045064704 | bytes 2883584 | tf_op jit(solution)/shard_map/pallas_call | solution.py:65
  75.9 1.3 %all_to_all.16 = bf16[64,22,256]{2,1,0:T(8,128)(2,1)S(1)} reshape(bf16[1408,256]{1,0:T(8,128)(2,1)} %get-tuple-element.9) | data formatting | bytes 1441792 | tf_op jit(solution)/shard_map/all_to_all | solution.py:139
  77.2 28.5 %all_to_all.20 = bf16[64,22,256]{2,1,0:T(8,128)(2,1)S(1)} all-to-all(bf16[64,22,256]{2,1,0:T(8,128)(2,1)S(1)} %all_to_all.16), channel_id=1, replica_groups=mesh['section'=8,'ctx'=8,'tp'=8] {'ctx','tp'}, dimensions={0} | all-to-all | bytes 1441792 | tf_op jit(solution)/shard_map/all_to_all | solution.py:139
  105.8 1.3 %copy_convert_fusion = f32[64,22,256]{2,0,1:T(8,128)} fusion(bf16[64,22,256]{2,1,0:T(8,128)(2,1)S(1)} %all_to_all.20), kind=kLoop, calls=%fused_computation | loop fusion | flops 360448 | bytes 2162688 | tf_op jit(solution)/shard_map/convert_element_type | solution.py:141
  107.1 2.0 %reshape.82 = f32[8,8,22,2,128]{4,3,1,0,2:T(2,128)S(1)} reshape(f32[64,22,256]{2,0,1:T(8,128)} %copy_convert_fusion) | data formatting | bytes 2883584 | tf_op jit(solution)/shard_map/convert_element_type | solution.py:141
  109.1 0.7 reduce_sum.11
  109.8 0.8 slice_bitcast_fusion
  (13 shorter events, 0.2 us)
Async XLA Ops:
  0.6 31.4 %copy-start = (bf16[1,2,176,1024]{3,2,1,0:T(8,128)(2,1)S(1)}, bf16[1,2,176,1024]{3,2,1,0:T(8,128)(2,1)}, u32[]{:S(2)}) copy-start(bf16[1,2,176,1024]{3,2,1,0:T(8,128)(2,1)} %param.8) | copy-start | bytes 2162692
  5.6 14.0 %collective-permute-start.2 = (bf16[22,2048]{1,0:T(8,128)(2,1)S(1)}, bf16[22,2048]{1,0:T(8,128)(2,1)S(1)}, u32[]{:S(2)}, u32[]{:S(2)}) collective-permute-start(bf16[22,2048]{1,0:T(8,128)(2,1)S(1)} %reshape.80), channel_id=1, source_target_pairs={{448,0},{0,64},{64,128},{128,192},{192,256},{256,320},{320,384},{3... | collective-permute-start | bytes 270344 | tf_op jit(solution)/shard_map/ppermute | solution.py:93
  19.6 14.3 %copy-start.1 = (bf16[1,176,1024]{2,1,0:T(8,128)(2,1)S(1)}, bf16[1,176,1024]{2,1,0:T(8,128)(2,1)}, u32[]{:S(2)}) copy-start(bf16[1,176,1024]{2,1,0:T(8,128)(2,1)} %param.11) | copy-start | bytes 1081348
  19.7 19.0 %copy-start.4 = (s32[16]{0:T(128)S(1)}, s32[16]{0:T(128)}, u32[]{:S(2)}) copy-start(s32[16]{0:T(128)} %param.6) | copy-start | bytes 196
  20.6 35.2 %all-to-all-start = ((bf16[64,22,256]{2,1,0:T(8,128)(2,1)}), bf16[64,22,256]{2,1,0:T(8,128)(2,1)S(1)}, u32[]{:S(2)}, u32[]{:S(2)}) async-start(bf16[64,22,256]{2,1,0:T(8,128)(2,1)} %bitcast.6), calls=%async_computation | async-start | bytes 1572864 | tf_op jit(solution)/shard_map/all_to_all | solution.py:127
  32.0 24.8 %collective-permute-start = (bf16[176,1024]{1,0:T(8,128)(2,1)S(1)}, bf16[176,1024]{1,0:T(8,128)(2,1)S(1)}, u32[]{:S(2)}, u32[]{:S(2)}) collective-permute-start(bf16[176,1024]{1,0:T(8,128)(2,1)S(1)} %dynamic-slice_bitcast_fusion), channel_id=1, source_target_pairs={{448,0},{0,64},{64,128},{128,192},{192,256},{256,320},{320,384},{3... | collective-permute-start | bytes 1081352 | tf_op jit(solution)/shard_map/ppermute | solution.py:93
  34.0 22.9 %collective-permute-start.1 = (bf16[176,1024]{1,0:T(8,128)(2,1)S(1)}, bf16[176,1024]{1,0:T(8,128)(2,1)S(1)}, u32[]{:S(2)}, u32[]{:S(2)}) collective-permute-start(bf16[176,1024]{1,0:T(8,128)(2,1)S(1)} %bitcast.52), channel_id=1, source_target_pairs={{64,0},{128,64},{192,128},{256,192},{320,256},{384,320},{448,384},... | collective-permute-start | bytes 1081352 | tf_op jit(solution)/shard_map/ppermute | solution.py:93
  56.9 0.7 copy-start.2
  57.6 0.7 copy-start.3

commit v8 on v5

--- a/solution.py
+++ b/solution.py
@@ -64,9 +64,9 @@
     scores = jnp.einsum("qgjd,kgd->gjqk", q4, key_heads, preferred_element_type=jnp.float32) * scale
     scores = jnp.where(visible, scores, NEG)
     top_score = jnp.max(scores, axis=-1, keepdims=True)
-    totals = jnp.sum(jnp.where(visible, jnp.exp(scores - top_score), 0.0), axis=-1, keepdims=True)
-    log_total = top_score + jnp.log(totals)
-    probs = jnp.where(visible, jnp.exp(scores - log_total), 0.0)
+    shifted = jnp.exp(scores - top_score)
+    totals = jnp.sum(shifted, axis=-1, keepdims=True)
+    probs = shifted / totals
     probs_low = probs.astype(jnp.bfloat16)
     attended = jnp.einsum(
         "gjqk,kgd->qgjd", probs_low, value_heads, preferred_element_type=jnp.float32
@@ -84,12 +84,12 @@
     q_grad_flat = q_grad.reshape(tok_rows, heads_local * head_size)
     grad_terms = jnp.stack([key_grad, value_grad], axis=2).reshape(seq_rows, 2 * kv_width)
     grad_parts = lax.all_to_all(
-        grad_terms.astype(jnp.bfloat16), plane, split_axis=0, concat_axis=0, tiled=True
+        grad_terms.astype(jnp.bfloat16), plane, split_axis=0, concat_axis=1, tiled=True
     )
-    grad_parts = grad_parts.reshape(ctx_count, tp_count, kv_rows, kv_local, 2, head_size)
-    own_grads = jnp.sum(grad_parts.astype(jnp.float32), axis=0)
-    k_grad_tokens = own_grads[:, :, :, 0, :].transpose(1, 0, 2, 3).reshape(kv_rows, -1)
-    v_grad_tokens = own_grads[:, :, :, 1, :].transpose(1, 0, 2, 3).reshape(kv_rows, -1)
+    grad_parts = grad_parts.reshape(kv_rows, ctx_count, tp_count * kv_local, 2, head_size)
+    own_grads = jnp.sum(grad_parts.astype(jnp.float32), axis=1)
+    k_grad_tokens = own_grads[:, :, 0, :].reshape(kv_rows, -1)
+    v_grad_tokens = own_grads[:, :, 1, :].reshape(kv_rows, -1)
     return (attended_flat[None], q_grad_flat[None], k_grad_tokens[None], v_grad_tokens[None])
 
 

time: 105 us -> 104 us (level)
  local copies, waits for them, and re-layouts: 14.7 us -> 12.7 us
  matrix products: 12.6 us -> 14.5 us
  other arithmetic: 5.15 us -> 3.9 us
    convert_element_type x1 -> x0, local copies, waits for them, and re-layouts: 1.99 us -> none  [body(): own_grads = jnp.sum(grad_parts.astype(jnp.float32), axis=0)]
    convert_element_type x1, other arithmetic: 1.29 us -> 0.12 us  [body(): own_grads = jnp.sum(grad_parts.astype(jnp.float32), axis=1)]
where the time goes in v8:
time: 104 us; the launch traced here: 103 us
  waiting for transfers between devices  37.6 us (36%)
  starting transfers between devices  31.6 us (30%)
  matrix products  14.5 us (14%)
  local copies, waits for them, and re-layouts  12.7 us (12%)
  other arithmetic  3.9 us (4%)
  between operations  2.92 us (3%)
    all_to_all x1, waiting for transfers between devices, body(): lax.all_to_all(grad_terms.astype(jnp.bfloat16), plane, split_axis=0, conc...  18.5 us
    ppermute x3, starting transfers between devices, passed_along(): return lax.ppermute(block, axis, route)  15.3 us
    all_to_all x1, starting transfers between devices, body(): lax.all_to_all(kv_pieces, plane, split_axis=0, concat_axis=0, tiled=True)  11.4 us
    all_to_all x1, waiting for transfers between devices, body(): lax.all_to_all(kv_pieces, plane, split_axis=0, concat_axis=0, tiled=True)  10.3 us
    ppermute x3, waiting for transfers between devices, passed_along(): return lax.ppermute(block, axis, route)  8.77 us
    all_to_all x1, starting transfers between devices, body(): lax.all_to_all(grad_terms.astype(jnp.bfloat16), plane, split_axis=0, conc...  4.93 us
    dot_general x1, matrix products, body(): jnp.einsum('qgjd,kgd->gjqk', do4, value_heads, preferred_element_type=jnp...  3.42 us
    dot_general x1, matrix products, body(): jnp.einsum('gjqk,kgd->qgjd', dscores, key_heads, preferred_element_type=j...  3.32 us
  transfers between devices with their start and end apart: 5, of which 4 were waited for; matrix products, arithmetic and copies ran while one was open for 9% of the time, Pallas kernels for 0%

profile of v8, /device:TPU:1, one launch (start us, length us, event | category | flops | bytes accessed | tf_op | source)
XLA Modules:
  0.0 103.3 jit_solution(18265247911589904308)
XLA Ops:
  0.6 0.0 copy-start
  0.7 1.3 %dynamic_slice.19 = s32[1]{0:T(128)} dynamic-slice(s32[8]{0:T(128)} %param.7, s32[]{:T(128)S(6)} %select_n.27), dynamic_slice_sizes={1} | dynamic-slice | bytes 12 | tf_op jit(solution)/shard_map/jit(dynamic_index_in_dim)/dynamic_slice | solution.py:35
  3.9 1.5 %dynamic-slice_reduce_fusion = (bf16[22,1024]{1,0:T(8,128)(2,1)S(1)}, bf16[22,1024]{1,0:T(8,128)(2,1)S(1)}) fusion(bf16[1,2,22,1024]{3,1,2,0:T(2,128)(2,1)} %param.10, s32[]{:T(128)S(6)} %select_n.28, bf16[1,2,22,1024]{3,1,2,0:T(2,128)(2,1)} %param.9), kind=kLoop, calls=%fused_computation.46 | loop fusion | bytes 180228 | tf_op jit(solution)/shard_map/jit(dynamic_index_in_dim)/dynamic_slice | solution.py:38
  5.5 0.1 copy.55
  5.6 4.8 %collective-permute-start = (bf16[22,2048]{1,0:T(8,128)(2,1)S(1)}, bf16[22,2048]{1,0:T(8,128)(2,1)S(1)}, u32[]{:S(2)}, u32[]{:S(2)}) collective-permute-start(bf16[22,2048]{1,0:T(8,128)(2,1)S(1)} %reshape.168), channel_id=1, source_target_pairs={{448,0},{0,64},{64,128},{128,192},{192,256},{256,320},{320,384},{3... | collective-permute-start | bytes 270344 | tf_op jit(solution)/shard_map/ppermute | solution.py:15
  10.4 8.6 %collective-permute-start.2 = (bf16[176,1024]{1,0:T(8,128)(2,1)}, bf16[176,1024]{1,0:T(8,128)(2,1)S(1)}, u32[]{:S(2)}, u32[]{:S(2)}) collective-permute-start(bf16[176,1024]{1,0:T(8,128)(2,1)} %bitcast.193), channel_id=1, source_target_pairs={{64,0},{128,64},{192,128},{256,192},{320,256},{384,320},{448,384},... | collective-permute-start | bytes 1081352 | tf_op jit(solution)/shard_map/ppermute | solution.py:15
  19.0 0.6 collective-permute-done
  19.6 0.9 broadcast_in_dim.17
  20.6 11.4 %all-to-all-start = ((bf16[64,22,256]{2,1,0:T(8,128)(2,1)}), bf16[64,22,256]{2,1,0:T(8,128)(2,1)S(1)}, u32[]{:S(2)}, u32[]{:S(2)}) async-start(bf16[64,22,256]{2,1,0:T(8,128)(2,1)} %bitcast.3), calls=%async_computation | async-start | bytes 1572864 | tf_op jit(solution)/shard_map/all_to_all | solution.py:49
  31.9 0.0 copy-done
  32.0 1.9 %collective-permute-start.1 = (bf16[176,1024]{1,0:T(8,128)(2,1)S(1)}, bf16[176,1024]{1,0:T(8,128)(2,1)S(1)}, u32[]{:S(2)}, u32[]{:S(2)}) collective-permute-start(bf16[176,1024]{1,0:T(8,128)(2,1)S(1)} %dynamic-slice_bitcast_fusion), channel_id=1, source_target_pairs={{448,0},{0,64},{64,128},{128,192},{192,256},{256,320},{320,384},{3... | collective-permute-start | bytes 1081352 | tf_op jit(solution)/shard_map/ppermute | solution.py:15
  33.9 0.7 broadcast_multiply_fusion
  34.6 0.1 add.65
  34.7 0.1 iota_add_fusion
  34.7 0.1 add.64
  34.8 0.1 add.66
  34.9 0.1 add.67
  35.0 0.1 add.69
  35.1 0.2 broadcast_compare_fusion
  35.3 0.0 collective-permute-done.2
  35.3 0.1 convert_bitcast_fusion.1
  35.4 1.0 copy.78
  36.4 8.2 %collective-permute-done.1 = bf16[176,1024]{1,0:T(8,128)(2,1)S(1)} collective-permute-done((bf16[176,1024]{1,0:T(8,128)(2,1)S(1)}, bf16[176,1024]{1,0:T(8,128)(2,1)S(1)}, u32[]{:S(2)}, u32[]{:S(2)}) %collective-permute-start.1) | collective-permute-done | bytes 360480 | tf_op jit(solution)/shard_map/ppermute | solution.py:15
  44.6 0.8 copy.79
  45.4 10.3 %all-to-all-done = bf16[64,22,256]{2,1,0:T(8,128)(2,1)S(1)} async-done(((bf16[64,22,256]{2,1,0:T(8,128)(2,1)}), bf16[64,22,256]{2,1,0:T(8,128)(2,1)S(1)}, u32[]{:S(2)}, u32[]{:S(2)}) %all-to-all-start) | async-done | bytes 720928 | tf_op jit(solution)/shard_map/all_to_all | solution.py:49
  55.8 0.3 reshape.170
  56.0 1.2 %fusion.49 = (bf16[1408,1,1,128]{3,2,0,1:T(2,128)(2,1)S(1)}, bf16[1408,1,1,128]{3,2,0,1:T(2,128)(2,1)S(1)}) fusion(bf16[1408,1,2,128]{3,2,0,1:T(2,128)(2,1)S(1)} %reshape.170), kind=kLoop, calls=%fused_computation.53 | loop fusion | bytes 1441792 | tf_op jit(solution)/shard_map/slice | solution.py:51
  57.3 1.9 %fusion.4 = (f32[8,176]{1,0:T(8,128)S(1)}, f32[1408,176,8]{0,1,2:T(8,128)S(1)}) fusion(pred[176,1408]{1,0:T(8,128)(4,1)S(1)} %broadcast_compare_fusion, bf16[1408,1,1,128]{3,2,0,1:T(2,128)(2,1)S(1)} %get-tuple-element.10, bf16[176,1024]{1,0:T(8,128)(2,1)S(1)} %collective-permute-done.1), kind=kOutput, calls=%fused_computation.7 | convolution fusion | flops 513456768 | bytes 8904192 | tf_op jit(solution)/shard_map/qgjd,kgd->gjqk/dot_general | solution.py:64
  59.2 2.3 %fusion.3 = f32[8,176]{1,0:T(8,128)S(1)} fusion(f32[1408,176,8]{0,1,2:T(8,128)S(1)} %get-tuple-element.15, f32[8,176]{1,0:T(8,128)S(1)} %get-tuple-element.14, pred[176,1408]{1,0:T(8,128)(4,1)S(1)} %broadcast_compare_fusion), kind=kLoop, calls=%fused_computation.6 | loop fusion | flops 7928448 | bytes 8188928 | tf_op jit(solution)/shard_map/reduce_sum | solution.py:68
  61.5 0.0 copy-done.2
  61.5 2.5 %fusion.39 = (f32[176,8]{0,1:T(8,128)S(1)}, bf16[176,1,8,128]{3,0,2,1:T(8,128)(2,1)S(1)}) fusion(f32[176,1,8,128]{3,2,0,1:T(8,128)S(1)} %bitcast.182, f32[8,176]{1,0:T(8,128)S(1)} %fusion.3, f32[8,176]{1,0:T(8,128)S(1)} %get-tuple-element.14, f32[1408,176,8]{0,1,2:T(8,128)S(1)} %get-tuple-element.15, pred[176,1408]{1,0:T(8,128)(4,1)S(1)} %broadcast_compare_fusion, ...), kind=kOutput, calls=%fused_computation.31 | convolution fusion | flops 517962368 | bytes 9636352 | tf_op jit(solution)/shard_map/gjqk,kgd->qgjd/dot_general | solution.py:71
  64.0 0.0 copy-start.3
  64.0 3.4 %fusion.12 = bf16[8,176,1408]{2,1,0:T(8,128)(2,1)S(1)} fusion(f32[8,176]{1,0:T(8,128)S(1)} %bitcast.194, f32[8,176]{1,0:T(8,128)S(1)} %fusion.3, f32[8,176]{1,0:T(8,128)S(1)} %get-tuple-element.14, f32[1408,176,8]{0,1,2:T(8,128)S(1)} %get-tuple-element.15, pred[176,1408]{1,0:T(8,128)(4,1)S(1)} %broadcast_compare_fusion, ...), kind=kOutput, calls=%fused_computation.15 | convolution fusion | flops 521388032 | bytes 12880384 | tf_op jit(solution)/shard_map/qgjd,kgd->gjqk/dot_general | solution.py:75
  67.4 0.9 fusion.28
  68.3 2.6 %fusion.31 = bf16[1408,1,1,128]{0,3,2,1:T(8,128)(2,1)S(1)} fusion(f32[8,176]{1,0:T(8,128)S(1)} %fusion.3, f32[8,176]{1,0:T(8,128)S(1)} %get-tuple-element.14, f32[1408,176,8]{0,1,2:T(8,128)S(1)} %get-tuple-element.15, pred[176,1408]{1,0:T(8,128)(4,1)S(1)} %broadcast_compare_fusion, bf16[176,1024]{1,0:T(8,128)(2,1)S(1)} %collective-permute-done.2), kind=kOutput, calls=%fused_computation.22 | convolution fusion | flops 517603328 | bytes 8909824 | tf_op jit(solution)/shard_map/gjqk,qgjd->kgd/dot_general | solution.py:81
  70.9 0.1 pad_maximum_fusion
  71.0 1.0 %copy.67 = bf16[1408,1,2,128]{3,2,0,1:T(2,128)(2,1)S(1)} copy(bf16[1408,1,2,128]{0,3,2,1:T(8,128)(2,1)S(1)} %pad_maximum_fusion) | data formatting | bytes 1441792 | tf_op jit(solution)/shard_map/stack | solution.py:85
  72.0 1.3 %convert_element_type.54 = bf16[64,22,256]{2,1,0:T(8,128)(2,1)} reshape(bf16[1408,1,2,128]{3,2,0,1:T(2,128)(2,1)S(1)} %copy.67) | data formatting | bytes 1441792 | tf_op jit(solution)/shard_map/convert_element_type | solution.py:87
  73.3 4.9 %all-to-all-start.1 = ((bf16[64,22,256]{2,1,0:T(8,128)(2,1)}), bf16[64,22,256]{2,1,0:T(8,128)(2,1)S(1)}, u32[]{:S(2)}, u32[]{:S(2)}) async-start(bf16[64,22,256]{2,1,0:T(8,128)(2,1)} %convert_element_type.54), calls=%async_computation.1 | async-start | bytes 1572864 | tf_op jit(solution)/shard_map/all_to_all | solution.py:86
  78.3 0.1 copy.60
  78.4 0.9 broadcast_in_dim_reshape.6
  79.3 3.3 %fusion.38 = bf16[176,1,8,128]{3,0,2,1:T(8,128)(2,1)S(1)} fusion(bf16[8,176,1408]{2,1,0:T(8,128)(2,1)} %copy-done.1, bf16[1408,1,1,128]{3,2,0,1:T(2,128)(2,1)S(1)} %get-tuple-element.10), kind=kOutput, calls=%fused_computation.28 | convolution fusion | flops 507871232 | bytes 4685824 | tf_op jit(solution)/shard_map/gjqk,kgd->qgjd/dot_general | solution.py:78
  82.6 0.1 copy.63
  82.7 0.9 broadcast_in_dim_reshape.7
  83.6 18.5 %all-to-all-done.1 = bf16[64,22,256]{2,1,0:T(8,128)(2,1)S(1)} async-done(((bf16[64,22,256]{2,1,0:T(8,128)(2,1)}), bf16[64,22,256]{2,1,0:T(8,128)(2,1)S(1)}, u32[]{:S(2)}, u32[]{:S(2)}) %all-to-all-start.1) | async-done | bytes 720928 | tf_op jit(solution)/shard_map/all_to_all | solution.py:86
  102.1 0.1 convert_bitcast_fusion
  102.2 0.4 bitcast_reduce_fusion
  102.6 0.7 fusion.50
  (16 shorter events, 0.2 us)
Async XLA Ops:
  0.6 31.3 %copy-start = (bf16[1,2,176,1024]{3,2,1,0:T(8,128)(2,1)S(1)}, bf16[1,2,176,1024]{3,2,1,0:T(8,128)(2,1)}, u32[]{:S(2)}) copy-start(bf16[1,2,176,1024]{3,2,1,0:T(8,128)(2,1)} %param.8) | copy-start | bytes 2162692
  5.6 14.0 %collective-permute-start = (bf16[22,2048]{1,0:T(8,128)(2,1)S(1)}, bf16[22,2048]{1,0:T(8,128)(2,1)S(1)}, u32[]{:S(2)}, u32[]{:S(2)}) collective-permute-start(bf16[22,2048]{1,0:T(8,128)(2,1)S(1)} %reshape.168), channel_id=1, source_target_pairs={{448,0},{0,64},{64,128},{128,192},{192,256},{256,320},{320,384},{3... | collective-permute-start | bytes 270344 | tf_op jit(solution)/shard_map/ppermute | solution.py:15
  10.4 24.9 %collective-permute-start.2 = (bf16[176,1024]{1,0:T(8,128)(2,1)}, bf16[176,1024]{1,0:T(8,128)(2,1)S(1)}, u32[]{:S(2)}, u32[]{:S(2)}) collective-permute-start(bf16[176,1024]{1,0:T(8,128)(2,1)} %bitcast.193), channel_id=1, source_target_pairs={{64,0},{128,64},{192,128},{256,192},{320,256},{384,320},{448,384},... | collective-permute-start | bytes 1081352 | tf_op jit(solution)/shard_map/ppermute | solution.py:15
  20.6 35.2 %all-to-all-start = ((bf16[64,22,256]{2,1,0:T(8,128)(2,1)}), bf16[64,22,256]{2,1,0:T(8,128)(2,1)S(1)}, u32[]{:S(2)}, u32[]{:S(2)}) async-start(bf16[64,22,256]{2,1,0:T(8,128)(2,1)} %bitcast.3), calls=%async_computation | async-start | bytes 1572864 | tf_op jit(solution)/shard_map/all_to_all | solution.py:49
  32.0 12.6 %collective-permute-start.1 = (bf16[176,1024]{1,0:T(8,128)(2,1)S(1)}, bf16[176,1024]{1,0:T(8,128)(2,1)S(1)}, u32[]{:S(2)}, u32[]{:S(2)}) collective-permute-start(bf16[176,1024]{1,0:T(8,128)(2,1)S(1)} %dynamic-slice_bitcast_fusion), channel_id=1, source_target_pairs={{448,0},{0,64},{64,128},{128,192},{192,256},{256,320},{320,384},{3... | collective-permute-start | bytes 1081352 | tf_op jit(solution)/shard_map/ppermute | solution.py:15
  57.3 4.2 %copy-start.2 = (f32[22,8,8,128]{3,2,1,0:T(8,128)S(1)}, f32[22,8,8,128]{3,2,1,0:T(8,128)}, u32[]{:S(2)}) copy-start(f32[22,8,8,128]{3,2,1,0:T(8,128)} %copy.78) | copy-start | bytes 2162692
  64.0 3.5 %copy-start.3 = (bf16[22,8,8,128]{3,2,1,0:T(8,128)(2,1)S(1)}, bf16[22,8,8,128]{3,2,1,0:T(8,128)(2,1)}, u32[]{:S(2)}) copy-start(bf16[22,8,8,128]{3,2,1,0:T(8,128)(2,1)} %copy.79) | copy-start | bytes 1081348
  67.4 3.5 %copy-start.1 = (bf16[8,176,1408]{2,1,0:T(8,128)(2,1)}, bf16[8,176,1408]{2,1,0:T(8,128)(2,1)S(1)}, u32[]{:S(2)}) copy-start(bf16[8,176,1408]{2,1,0:T(8,128)(2,1)S(1)} %fusion.12) | copy-start | bytes 11894788
  73.3 28.7 %all-to-all-start.1 = ((bf16[64,22,256]{2,1,0:T(8,128)(2,1)}), bf16[64,22,256]{2,1,0:T(8,128)(2,1)S(1)}, u32[]{:S(2)}, u32[]{:S(2)}) async-start(bf16[64,22,256]{2,1,0:T(8,128)(2,1)} %convert_element_type.54), calls=%async_computation.1 | async-start | bytes 1572864 | tf_op jit(solution)/shard_map/all_to_all | solution.py:86

commit v9 on v8

--- a/solution.py
+++ b/solution.py
@@ -37,19 +37,22 @@
     k_send = lax.dynamic_index_in_dim(k_box[0], wanted, 0, keepdims=False)
     v_send = lax.dynamic_index_in_dim(v_box[0], wanted, 0, keepdims=False)
     kv_send = jnp.stack(
-        [k_send.reshape(kv_rows, -1, head_size), v_send.reshape(kv_rows, -1, head_size)], axis=2
-    ).reshape(kv_rows, -1)
+        [
+            k_send.reshape(kv_rows, tp_count, kv_width).transpose(1, 0, 2),
+            v_send.reshape(kv_rows, tp_count, kv_width).transpose(1, 0, 2),
+        ],
+        axis=1,
+    ).reshape(tp_count, 2 * kv_rows, kv_width)
     queries, kv_rows_in = passed_along((q_send, kv_send), "section", 1)
     cotangent = passed_along(grad_out[0], "section", -1)
 
     plane = ("ctx", "tp")
-    kv_pieces = kv_rows_in.reshape(1, kv_rows, tp_count, 2 * kv_width).transpose(0, 2, 1, 3)
-    kv_pieces = jnp.broadcast_to(kv_pieces, (ctx_count, tp_count, kv_rows, 2 * kv_width))
-    kv_pieces = kv_pieces.reshape(ctx_count * tp_count * kv_rows, 2 * kv_width)
+    kv_pieces = jnp.broadcast_to(kv_rows_in[None], (ctx_count, tp_count, 2 * kv_rows, kv_width))
+    kv_pieces = kv_pieces.reshape(ctx_count * tp_count * 2 * kv_rows, kv_width)
     kv_full = lax.all_to_all(kv_pieces, plane, split_axis=0, concat_axis=0, tiled=True)
-    kv_full = kv_full.reshape(seq_rows, kv_local, 2, head_size)
-    key_heads = kv_full[:, :, 0, :]
-    value_heads = kv_full[:, :, 1, :]
+    kv_full = kv_full.reshape(ctx_count * tp_count, 2, kv_rows, kv_local, head_size)
+    key_heads = kv_full[:, 0].reshape(seq_rows, kv_local, head_size)
+    value_heads = kv_full[:, 1].reshape(seq_rows, kv_local, head_size)
     ctx_rank = lax.axis_index("ctx")
 
     positions = (
@@ -82,14 +85,20 @@
 
     attended_flat = attended.astype(jnp.bfloat16).reshape(tok_rows, heads_local * head_size)
     q_grad_flat = q_grad.reshape(tok_rows, heads_local * head_size)
-    grad_terms = jnp.stack([key_grad, value_grad], axis=2).reshape(seq_rows, 2 * kv_width)
+    grad_terms = jnp.stack(
+        [
+            key_grad.reshape(ctx_count * tp_count, kv_rows, kv_width),
+            value_grad.reshape(ctx_count * tp_count, kv_rows, kv_width),
+        ],
+        axis=1,
+    ).reshape(seq_rows * 2, kv_width)
     grad_parts = lax.all_to_all(
-        grad_terms.astype(jnp.bfloat16), plane, split_axis=0, concat_axis=1, tiled=True
+        grad_terms.astype(jnp.bfloat16), plane, split_axis=0, concat_axis=0, tiled=True
     )
-    grad_parts = grad_parts.reshape(kv_rows, ctx_count, tp_count * kv_local, 2, head_size)
-    own_grads = jnp.sum(grad_parts.astype(jnp.float32), axis=1)
-    k_grad_tokens = own_grads[:, :, 0, :].reshape(kv_rows, -1)
-    v_grad_tokens = own_grads[:, :, 1, :].reshape(kv_rows, -1)
+    grad_parts = grad_parts.reshape(ctx_count, tp_count, 2, kv_rows, kv_width)
+    own_grads = jnp.sum(grad_parts.astype(jnp.float32), axis=0)
+    k_grad_tokens = own_grads[:, 0].transpose(1, 0, 2).reshape(kv_rows, -1)
+    v_grad_tokens = own_grads[:, 1].transpose(1, 0, 2).reshape(kv_rows, -1)
     return (attended_flat[None], q_grad_flat[None], k_grad_tokens[None], v_grad_tokens[None])
 
 

time: 104 us -> 111 us (1.067)
  matrix products: 14.5 us -> 18.8 us
  local copies, waits for them, and re-layouts: 12.7 us -> 16 us
    dot_general x1, matrix products: 2.51 us -> 6.26 us  [body(): jnp.einsum('gjqk,kgd->qgjd', probs_low, value_heads, preferred_element_ty...]
    unnamed x13 -> x24, local copies, waits for them, and re-layouts: 1.88 us -> 3.55 us
    another operation x4 -> x7, local copies, waits for them, and re-layouts: 1.12 us -> 2.3 us  [the longest x3 1.34 us: body(): jnp.stack([key_grad.reshape(ctx_count * tp_count, kv_rows, kv_width), val...]
where the time goes in v9:
time: 111 us
  waiting for transfers between devices  37.5 us (34%)
  starting transfers between devices  31.6 us (28%)
  matrix products  18.8 us (17%)
  local copies, waits for them, and re-layouts  16 us (14%)
  other arithmetic  3.66 us (3%)
  between operations  2.94 us (3%)
    all_to_all x1, waiting for transfers between devices, body(): lax.all_to_all(grad_terms.astype(jnp.bfloat16), plane, split_axis=0, conc...  18.5 us
    ppermute x3, starting transfers between devices, passed_along(): return lax.ppermute(block, axis, route)  15.3 us
    all_to_all x1, starting transfers between devices, body(): lax.all_to_all(kv_pieces, plane, split_axis=0, concat_axis=0, tiled=True)  11.4 us
    ppermute x3, waiting for transfers between devices, passed_along(): return lax.ppermute(block, axis, route)  9.67 us
    all_to_all x1, waiting for transfers between devices, body(): lax.all_to_all(kv_pieces, plane, split_axis=0, concat_axis=0, tiled=True)  9.39 us
    dot_general x1, matrix products, body(): jnp.einsum('gjqk,kgd->qgjd', probs_low, value_heads, preferred_element_ty...  6.26 us
    all_to_all x1, starting transfers between devices, body(): lax.all_to_all(grad_terms.astype(jnp.bfloat16), plane, split_axis=0, conc...  4.93 us
    unnamed x24, local copies, waits for them, and re-layouts  3.55 us
  transfers between devices with their start and end apart: 5, of which 4 were waited for; matrix products, arithmetic and copies ran while one was open for 9% of the time, Pallas kernels for 0%

profile of v9, /device:TPU:1, one launch (start us, length us, event | category | flops | bytes accessed | tf_op | source)
XLA Modules:
  0.0 110.5 jit_solution(2121959914494993512)
XLA Ops:
  0.7 1.3 %dynamic_slice.19 = s32[1]{0:T(128)} dynamic-slice(s32[8]{0:T(128)} %param.7, s32[]{:T(128)S(6)} %select_n.27), dynamic_slice_sizes={1} | dynamic-slice | bytes 12 | tf_op jit(solution)/shard_map/jit(dynamic_index_in_dim)/dynamic_slice | solution.py:35
  3.9 1.5 %dynamic-slice_reduce_fusion = (bf16[22,1024]{1,0:T(8,128)(2,1)S(1)}, bf16[22,1024]{1,0:T(8,128)(2,1)S(1)}) fusion(bf16[1,2,22,1024]{3,1,2,0:T(2,128)(2,1)} %param.10, s32[]{:T(128)S(6)} %select_n.28, bf16[1,2,22,1024]{3,1,2,0:T(2,128)(2,1)} %param.9), kind=kLoop, calls=%fused_computation.42 | loop fusion | bytes 180228 | tf_op jit(solution)/shard_map/jit(dynamic_index_in_dim)/dynamic_slice | solution.py:38
  5.5 4.8 %collective-permute-start = (bf16[8,44,128]{2,0,1:T(8,128)(2,1)S(1)}, bf16[8,44,128]{2,0,1:T(8,128)(2,1)S(1)}, u32[]{:S(2)}, u32[]{:S(2)}) collective-permute-start(bf16[8,44,128]{2,0,1:T(8,128)(2,1)S(1)} %bitcast.183), channel_id=1, source_target_pairs={{448,0},{0,64},{64,128},{128,192},{192,256},{256,320},{320,384},{3... | collective-permute-start | bytes 270344 | tf_op jit(solution)/shard_map/ppermute | solution.py:15
  10.3 8.6 %collective-permute-start.2 = (bf16[176,1024]{1,0:T(8,128)(2,1)}, bf16[176,1024]{1,0:T(8,128)(2,1)S(1)}, u32[]{:S(2)}, u32[]{:S(2)}) collective-permute-start(bf16[176,1024]{1,0:T(8,128)(2,1)} %bitcast.187), channel_id=1, source_target_pairs={{64,0},{128,64},{192,128},{256,192},{320,256},{384,320},{448,384},... | collective-permute-start | bytes 1081352 | tf_op jit(solution)/shard_map/ppermute | solution.py:15
  18.9 0.4 collective-permute-done
  19.3 1.0 broadcast_in_dim.10
  20.3 11.4 %all-to-all-start = ((bf16[64,44,128]{2,1,0:T(8,128)(2,1)}), bf16[64,44,128]{2,1,0:T(8,128)(2,1)S(1)}, u32[]{:S(2)}, u32[]{:S(2)}) async-start(bf16[64,44,128]{2,1,0:T(8,128)(2,1)} %bitcast.6), calls=%async_computation | async-start | bytes 1572864 | tf_op jit(solution)/shard_map/all_to_all | solution.py:52
  31.7 0.8 dynamic-slice_bitcast_fusion
  32.4 1.9 %collective-permute-start.1 = (bf16[176,1024]{1,0:T(8,128)(2,1)}, bf16[176,1024]{1,0:T(8,128)(2,1)S(1)}, u32[]{:S(2)}, u32[]{:S(2)}) collective-permute-start(bf16[176,1024]{1,0:T(8,128)(2,1)} %dynamic-slice_bitcast_fusion), channel_id=1, source_target_pairs={{448,0},{0,64},{64,128},{128,192},{192,256},{256,320},{320,384},{3... | collective-permute-start | bytes 1081352 | tf_op jit(solution)/shard_map/ppermute | solution.py:15
  34.4 0.7 broadcast_multiply_fusion
  35.0 0.1 add.65
  35.2 0.1 add.64
  35.3 0.1 add.67
  35.4 0.1 add.69
  35.5 0.2 broadcast_compare_fusion
  35.8 0.1 copy.41
  36.0 9.3 %collective-permute-done.1 = bf16[176,1024]{1,0:T(8,128)(2,1)S(1)} collective-permute-done((bf16[176,1024]{1,0:T(8,128)(2,1)}, bf16[176,1024]{1,0:T(8,128)(2,1)S(1)}, u32[]{:S(2)}, u32[]{:S(2)}) %collective-permute-start.1) | collective-permute-done | bytes 360480 | tf_op jit(solution)/shard_map/ppermute | solution.py:15
  45.3 0.8 copy.42
  46.1 9.4 %all-to-all-done = bf16[64,44,128]{2,1,0:T(8,128)(2,1)S(1)} async-done(((bf16[64,44,128]{2,1,0:T(8,128)(2,1)}), bf16[64,44,128]{2,1,0:T(8,128)(2,1)S(1)}, u32[]{:S(2)}, u32[]{:S(2)}) %all-to-all-start) | async-done | bytes 720928 | tf_op jit(solution)/shard_map/all_to_all | solution.py:52
  55.5 0.2 copy.23
  55.7 0.2 copy.24
  56.0 0.8 reshape.184
  56.8 0.2 copy.25
  57.1 0.1 reshape.183
  57.2 1.9 %fusion.4 = (f32[8,176]{1,0:T(8,128)S(1)}, f32[1408,176,8]{0,1,2:T(8,128)S(1)}) fusion(pred[176,1408]{1,0:T(8,128)(4,1)S(1)} %broadcast_compare_fusion, bf16[1408,128,1]{1,0,2:T(8,128)(2,1)S(1)} %reshape.183, bf16[176,1024]{1,0:T(8,128)(2,1)S(1)} %collective-permute-done.1), kind=kOutput, calls=%fused_computation.7 | convolution fusion | flops 513456768 | bytes 8904192 | tf_op jit(solution)/shard_map/qgjd,kgd->gjqk/dot_general | solution.py:67
  59.0 2.4 %fusion.3 = f32[8,176]{1,0:T(8,128)S(1)} fusion(f32[1408,176,8]{0,1,2:T(8,128)S(1)} %get-tuple-element.11, f32[8,176]{1,0:T(8,128)S(1)} %get-tuple-element.10, pred[176,1408]{1,0:T(8,128)(4,1)S(1)} %broadcast_compare_fusion), kind=kLoop, calls=%fused_computation.6 | loop fusion | flops 7928448 | bytes 8188928 | tf_op jit(solution)/shard_map/reduce_sum | solution.py:71
  61.5 0.7 copy-done.1
  62.1 3.2 %fusion.31 = bf16[1408,1,128]{2,0,1:T(8,128)(2,1)} fusion(f32[8,176]{1,0:T(8,128)S(1)} %fusion.3, f32[8,176]{1,0:T(8,128)S(1)} %get-tuple-element.10, f32[1408,176,8]{0,1,2:T(8,128)S(1)} %get-tuple-element.11, pred[176,1408]{1,0:T(8,128)(4,1)S(1)} %broadcast_compare_fusion, bf16[176,1024]{1,0:T(8,128)(2,1)S(1)} %copy-done.5), kind=kOutput, calls=%fused_computation.22 | convolution fusion | flops 517603328 | bytes 8909824 | tf_op jit(solution)/shard_map/gjqk,qgjd->kgd/dot_general | solution.py:84
  65.3 1.1 stack_reshape.9
  66.4 6.3 %fusion.39 = (f32[176,8]{0,1:T(8,128)S(1)}, bf16[176,1,8,128]{3,0,2,1:T(8,128)(2,1)}) fusion(f32[176,1,8,128]{3,2,0,1:T(8,128)S(1)} %bitcast.177, bf16[1408,128,1]{1,0,2:T(8,128)(2,1)S(1)} %copy-done.8, f32[8,176]{1,0:T(8,128)S(1)} %fusion.3, f32[8,176]{1,0:T(8,128)S(1)} %get-tuple-element.10, f32[1408,176,8]{0,1,2:T(8,128)} %copy-done.1, ...), kind=kOutput, calls=%fused_computation.30 | convolution fusion | flops 517962368 | bytes 9636352 | tf_op jit(solution)/shard_map/gjqk,kgd->qgjd/dot_general | solution.py:74
  72.7 3.4 %fusion.12 = bf16[8,176,1408]{2,1,0:T(8,128)(2,1)S(1)} fusion(f32[8,176]{1,0:T(8,128)S(1)} %bitcast.188, bf16[1408,128,1]{1,0,2:T(8,128)(2,1)S(1)} %copy-done.9, f32[8,176]{1,0:T(8,128)S(1)} %fusion.3, f32[8,176]{1,0:T(8,128)S(1)} %get-tuple-element.10, f32[1408,176,8]{0,1,2:T(8,128)S(1)} %copy-done.2, pred[176,1408]{1,0:T(8,128)(4,1)S(1)} %broadcast_compare_fusion, ...), kind=kOutput, calls=%fused_computation.15 | convolution fusion | flops 521388032 | bytes 12880384 | tf_op jit(solution)/shard_map/qgjd,kgd->gjqk/dot_general | solution.py:78
  76.1 1.9 %copy-done.3 = bf16[8,176,1408]{2,1,0:T(8,128)(2,1)} copy-done((bf16[8,176,1408]{2,1,0:T(8,128)(2,1)}, bf16[8,176,1408]{2,1,0:T(8,128)(2,1)S(1)}, u32[]{:S(2)}) %copy-start.3) | copy-done | bytes 3964952
  77.9 0.9 fusion.28
  78.8 0.2 copy.32
  79.0 0.1 stack_reshape.8
  79.1 0.1 pad_maximum_fusion
  79.3 0.2 copy.34
  79.4 1.4 %copy.35 = bf16[64,44,128]{2,1,0:T(8,128)(2,1)} copy(bf16[64,44,128]{2,0,1:T(8,128)(2,1)S(1)} %bitcast.174) | data formatting | bytes 1441792 | tf_op jit(solution)/shard_map/convert_element_type | solution.py:96
  80.8 4.9 %all-to-all-start.1 = ((bf16[64,44,128]{2,1,0:T(8,128)(2,1)}), bf16[64,44,128]{2,1,0:T(8,128)(2,1)S(1)}, u32[]{:S(2)}, u32[]{:S(2)}) async-start(bf16[64,44,128]{2,1,0:T(8,128)(2,1)} %copy.35), calls=%async_computation.1 | async-start | bytes 1572864 | tf_op jit(solution)/shard_map/all_to_all | solution.py:95
  85.7 0.1 copy.27
  85.8 0.9 broadcast_in_dim_reshape.12
  86.7 3.3 %fusion.38 = bf16[176,1,8,128]{3,0,2,1:T(8,128)(2,1)S(1)} fusion(bf16[1408,128,1]{1,0,2:T(8,128)(2,1)S(1)} %reshape.183, bf16[8,176,1408]{2,1,0:T(8,128)(2,1)} %copy-done.3), kind=kOutput, calls=%fused_computation.27 | convolution fusion | flops 507871232 | bytes 4685824 | tf_op jit(solution)/shard_map/gjqk,kgd->qgjd/dot_general | solution.py:81
  90.1 0.1 copy.30
  90.2 0.9 broadcast_in_dim_reshape.13
  91.1 18.5 %all-to-all-done.1 = bf16[64,44,128]{2,1,0:T(8,128)(2,1)S(1)} async-done(((bf16[64,44,128]{2,1,0:T(8,128)(2,1)}), bf16[64,44,128]{2,1,0:T(8,128)(2,1)S(1)}, u32[]{:S(2)}, u32[]{:S(2)}) %all-to-all-start.1) | async-done | bytes 720928 | tf_op jit(solution)/shard_map/all_to_all | solution.py:95
  109.5 0.2 copy.36
  109.7 0.1 convert_reduce_fusion
  109.9 0.7 fusion.50
  (31 shorter events, 0.4 us)
Async XLA Ops:
  0.6 31.0 %copy-start = (bf16[1,2,176,1024]{3,2,1,0:T(8,128)(2,1)S(1)}, bf16[1,2,176,1024]{3,2,1,0:T(8,128)(2,1)}, u32[]{:S(2)}) copy-start(bf16[1,2,176,1024]{3,2,1,0:T(8,128)(2,1)} %param.8) | copy-start | bytes 2162692
  5.5 13.8 %collective-permute-start = (bf16[8,44,128]{2,0,1:T(8,128)(2,1)S(1)}, bf16[8,44,128]{2,0,1:T(8,128)(2,1)S(1)}, u32[]{:S(2)}, u32[]{:S(2)}) collective-permute-start(bf16[8,44,128]{2,0,1:T(8,128)(2,1)S(1)} %bitcast.183), channel_id=1, source_target_pairs={{448,0},{0,64},{64,128},{128,192},{192,256},{256,320},{320,384},{3... | collective-permute-start | bytes 270344 | tf_op jit(solution)/shard_map/ppermute | solution.py:15
  10.3 25.4 %collective-permute-start.2 = (bf16[176,1024]{1,0:T(8,128)(2,1)}, bf16[176,1024]{1,0:T(8,128)(2,1)S(1)}, u32[]{:S(2)}, u32[]{:S(2)}) collective-permute-start(bf16[176,1024]{1,0:T(8,128)(2,1)} %bitcast.187), channel_id=1, source_target_pairs={{64,0},{128,64},{192,128},{256,192},{320,256},{384,320},{448,384},... | collective-permute-start | bytes 1081352 | tf_op jit(solution)/shard_map/ppermute | solution.py:15
  20.3 35.2 %all-to-all-start = ((bf16[64,44,128]{2,1,0:T(8,128)(2,1)}), bf16[64,44,128]{2,1,0:T(8,128)(2,1)S(1)}, u32[]{:S(2)}, u32[]{:S(2)}) async-start(bf16[64,44,128]{2,1,0:T(8,128)(2,1)} %bitcast.6), calls=%async_computation | async-start | bytes 1572864 | tf_op jit(solution)/shard_map/all_to_all | solution.py:52
  32.4 12.8 %collective-permute-start.1 = (bf16[176,1024]{1,0:T(8,128)(2,1)}, bf16[176,1024]{1,0:T(8,128)(2,1)S(1)}, u32[]{:S(2)}, u32[]{:S(2)}) collective-permute-start(bf16[176,1024]{1,0:T(8,128)(2,1)} %dynamic-slice_bitcast_fusion), channel_id=1, source_target_pairs={{448,0},{0,64},{64,128},{128,192},{192,256},{256,320},{320,384},{3... | collective-permute-start | bytes 1081352 | tf_op jit(solution)/shard_map/ppermute | solution.py:15
  35.8 19.9 %copy-start.4 = (bf16[176,1024]{1,0:T(8,128)(2,1)}, bf16[176,1024]{1,0:T(8,128)(2,1)S(1)}, u32[]{:S(2)}) copy-start(bf16[176,1024]{1,0:T(8,128)(2,1)S(1)} %collective-permute-done.2) | copy-start | bytes 1081348
  57.2 4.9 %copy-start.5 = (bf16[176,1024]{1,0:T(8,128)(2,1)S(1)}, bf16[176,1024]{1,0:T(8,128)(2,1)}, u32[]{:S(2)}) copy-start(bf16[176,1024]{1,0:T(8,128)(2,1)} %copy-done.4) | copy-start | bytes 1081348
  59.0 3.1 %copy-start.1 = (f32[1408,176,8]{0,1,2:T(8,128)}, f32[1408,176,8]{0,1,2:T(8,128)S(1)}, u32[]{:S(2)}) copy-start(f32[1408,176,8]{0,1,2:T(8,128)S(1)} %get-tuple-element.11) | copy-start | bytes 23789572
  62.1 4.3 %copy-start.8 = (bf16[1408,128,1]{1,0,2:T(8,128)(2,1)S(1)}, bf16[1408,128,1]{1,0,2:T(8,128)(2,1)}, u32[]{:S(2)}) copy-start(bf16[1408,128,1]{1,0,2:T(8,128)(2,1)} %reshape.184) | copy-start | bytes 1081348
  66.4 6.3 %copy-start.2 = (f32[1408,176,8]{0,1,2:T(8,128)S(1)}, f32[1408,176,8]{0,1,2:T(8,128)}, u32[]{:S(2)}) copy-start(f32[1408,176,8]{0,1,2:T(8,128)} %copy-done.1) | copy-start | bytes 23789572
  66.4 6.3 %copy-start.9 = (bf16[1408,128,1]{1,0,2:T(8,128)(2,1)S(1)}, bf16[1408,128,1]{1,0,2:T(8,128)(2,1)}, u32[]{:S(2)}) copy-start(bf16[1408,128,1]{1,0,2:T(8,128)(2,1)} %reshape.184) | copy-start | bytes 1081348
  72.7 5.3 %copy-start.6 = (bf16[22,8,8,128]{3,2,1,0:T(8,128)(2,1)S(1)}, bf16[22,8,8,128]{3,2,1,0:T(8,128)(2,1)}, u32[]{:S(2)}) copy-start(bf16[22,8,8,128]{3,2,1,0:T(8,128)(2,1)} %copy.42) | copy-start | bytes 1081348
  76.0 1.9 %copy-start.3 = (bf16[8,176,1408]{2,1,0:T(8,128)(2,1)}, bf16[8,176,1408]{2,1,0:T(8,128)(2,1)S(1)}, u32[]{:S(2)}) copy-start(bf16[8,176,1408]{2,1,0:T(8,128)(2,1)S(1)} %fusion.12) | copy-start | bytes 11894788
  76.1 9.7 %copy-start.7 = (bf16[176,1,8,128]{3,0,2,1:T(8,128)(2,1)S(1)}, bf16[176,1,8,128]{3,0,2,1:T(8,128)(2,1)}, u32[]{:S(2)}) copy-start(bf16[176,1,8,128]{3,0,2,1:T(8,128)(2,1)} %get-tuple-element.5) | copy-start | bytes 1081348
  80.8 28.7 %all-to-all-start.1 = ((bf16[64,44,128]{2,1,0:T(8,128)(2,1)}), bf16[64,44,128]{2,1,0:T(8,128)(2,1)S(1)}, u32[]{:S(2)}, u32[]{:S(2)}) async-start(bf16[64,44,128]{2,1,0:T(8,128)(2,1)} %copy.35), calls=%async_computation.1 | async-start | bytes 1572864 | tf_op jit(solution)/shard_map/all_to_all | solution.py:95

commit v10 on v8

--- a/solution.py
+++ b/solution.py
@@ -64,9 +64,9 @@
     scores = jnp.einsum("qgjd,kgd->gjqk", q4, key_heads, preferred_element_type=jnp.float32) * scale
     scores = jnp.where(visible, scores, NEG)
     top_score = jnp.max(scores, axis=-1, keepdims=True)
-    shifted = jnp.exp(scores - top_score)
-    totals = jnp.sum(shifted, axis=-1, keepdims=True)
-    probs = shifted / totals
+    totals = jnp.sum(jnp.where(visible, jnp.exp(scores - top_score), 0.0), axis=-1, keepdims=True)
+    log_total = top_score + jnp.log(totals)
+    probs = jnp.where(visible, jnp.exp(scores - log_total), 0.0)
     probs_low = probs.astype(jnp.bfloat16)
     attended = jnp.einsum(
         "gjqk,kgd->qgjd", probs_low, value_heads, preferred_element_type=jnp.float32

time: 104 us -> 101 us (0.971)
  matrix products: 14.5 us -> 12.6 us
where the time goes in v10:
time: 101 us
  waiting for transfers between devices  37.6 us (37%)
  starting transfers between devices  31.6 us (31%)
  matrix products  12.6 us (12%)
  local copies, waits for them, and re-layouts  12.5 us (12%)
  other arithmetic  3.64 us (4%)
  between operations  2.93 us (3%)
    all_to_all x1, waiting for transfers between devices, body(): lax.all_to_all(grad_terms.astype(jnp.bfloat16), plane, split_axis=0, conc...  18.5 us
    ppermute x3, starting transfers between devices, passed_along(): return lax.ppermute(block, axis, route)  15.3 us
    all_to_all x1, starting transfers between devices, body(): lax.all_to_all(kv_pieces, plane, split_axis=0, concat_axis=0, tiled=True)  11.4 us
    all_to_all x1, waiting for transfers between devices, body(): lax.all_to_all(kv_pieces, plane, split_axis=0, concat_axis=0, tiled=True)  10.3 us
    ppermute x3, waiting for transfers between devices, passed_along(): return lax.ppermute(block, axis, route)  8.77 us
    all_to_all x1, starting transfers between devices, body(): lax.all_to_all(grad_terms.astype(jnp.bfloat16), plane, split_axis=0, conc...  4.93 us
    dot_general x1, matrix products, body(): jnp.einsum('gjqk,kgd->qgjd', dscores, key_heads, preferred_element_type=j...  3.32 us
    dot_general x1, matrix products, body(): jnp.einsum('qgjd,kgd->gjqk', do4, value_heads, preferred_element_type=jnp...  2.92 us
  transfers between devices with their start and end apart: 5, of which 4 were waited for; matrix products, arithmetic and copies ran while one was open for 9% of the time, Pallas kernels for 0%

profile of v10, /device:TPU:1, one launch (start us, length us, event | category | flops | bytes accessed | tf_op | source)
XLA Modules:
  0.0 100.9 jit_solution(3128940508814382255)
XLA Ops:
  0.6 0.0 copy-start
  0.7 1.3 %dynamic_slice.19 = s32[1]{0:T(128)} dynamic-slice(s32[8]{0:T(128)} %param.7, s32[]{:T(128)S(6)} %select_n.33), dynamic_slice_sizes={1} | dynamic-slice | bytes 12 | tf_op jit(solution)/shard_map/jit(dynamic_index_in_dim)/dynamic_slice | solution.py:35
  3.9 1.5 %dynamic-slice_reduce_fusion = (bf16[22,1024]{1,0:T(8,128)(2,1)S(1)}, bf16[22,1024]{1,0:T(8,128)(2,1)S(1)}) fusion(bf16[1,2,22,1024]{3,1,2,0:T(2,128)(2,1)} %param.10, s32[]{:T(128)S(6)} %select_n.34, bf16[1,2,22,1024]{3,1,2,0:T(2,128)(2,1)} %param.9), kind=kLoop, calls=%fused_computation.40 | loop fusion | bytes 180228 | tf_op jit(solution)/shard_map/jit(dynamic_index_in_dim)/dynamic_slice | solution.py:38
  5.5 0.1 copy.55
  5.6 4.8 %collective-permute-start = (bf16[22,2048]{1,0:T(8,128)(2,1)S(1)}, bf16[22,2048]{1,0:T(8,128)(2,1)S(1)}, u32[]{:S(2)}, u32[]{:S(2)}) collective-permute-start(bf16[22,2048]{1,0:T(8,128)(2,1)S(1)} %reshape.178), channel_id=1, source_target_pairs={{448,0},{0,64},{64,128},{128,192},{192,256},{256,320},{320,384},{3... | collective-permute-start | bytes 270344 | tf_op jit(solution)/shard_map/ppermute | solution.py:15
  10.4 8.6 %collective-permute-start.2 = (bf16[176,1024]{1,0:T(8,128)(2,1)}, bf16[176,1024]{1,0:T(8,128)(2,1)S(1)}, u32[]{:S(2)}, u32[]{:S(2)}) collective-permute-start(bf16[176,1024]{1,0:T(8,128)(2,1)} %bitcast.165), channel_id=1, source_target_pairs={{64,0},{128,64},{192,128},{256,192},{320,256},{384,320},{448,384},... | collective-permute-start | bytes 1081352 | tf_op jit(solution)/shard_map/ppermute | solution.py:15
  19.0 0.6 collective-permute-done
  19.6 0.9 broadcast_in_dim.37
  20.6 11.4 %all-to-all-start = ((bf16[64,22,256]{2,1,0:T(8,128)(2,1)}), bf16[64,22,256]{2,1,0:T(8,128)(2,1)S(1)}, u32[]{:S(2)}, u32[]{:S(2)}) async-start(bf16[64,22,256]{2,1,0:T(8,128)(2,1)} %bitcast.3), calls=%async_computation | async-start | bytes 1572864 | tf_op jit(solution)/shard_map/all_to_all | solution.py:49
  32.0 1.9 %collective-permute-start.1 = (bf16[176,1024]{1,0:T(8,128)(2,1)S(1)}, bf16[176,1024]{1,0:T(8,128)(2,1)S(1)}, u32[]{:S(2)}, u32[]{:S(2)}) collective-permute-start(bf16[176,1024]{1,0:T(8,128)(2,1)S(1)} %dynamic-slice_bitcast_fusion), channel_id=1, source_target_pairs={{448,0},{0,64},{64,128},{128,192},{192,256},{256,320},{320,384},{3... | collective-permute-start | bytes 1081352 | tf_op jit(solution)/shard_map/ppermute | solution.py:15
  33.9 0.7 broadcast_multiply_fusion
  34.6 0.1 add.73
  34.7 0.1 iota_add_fusion
  34.7 0.1 add.72
  34.8 0.1 add.74
  34.9 0.1 add.75
  35.0 0.1 add.77
  35.1 0.2 broadcast_compare_fusion
  35.3 0.0 collective-permute-done.2
  35.3 0.1 convert_bitcast_fusion.1
  35.4 1.0 %copy.78 = f32[22,8,8,128]{3,2,1,0:T(8,128)} copy(f32[22,8,8,128]{3,1,2,0:T(8,128)S(1)} %convert_bitcast_fusion.1) | data formatting | bytes 1441792
  36.4 8.2 %collective-permute-done.1 = bf16[176,1024]{1,0:T(8,128)(2,1)S(1)} collective-permute-done((bf16[176,1024]{1,0:T(8,128)(2,1)S(1)}, bf16[176,1024]{1,0:T(8,128)(2,1)S(1)}, u32[]{:S(2)}, u32[]{:S(2)}) %collective-permute-start.1) | collective-permute-done | bytes 360480 | tf_op jit(solution)/shard_map/ppermute | solution.py:15
  44.6 0.8 copy.79
  45.4 10.3 %all-to-all-done = bf16[64,22,256]{2,1,0:T(8,128)(2,1)S(1)} async-done(((bf16[64,22,256]{2,1,0:T(8,128)(2,1)}), bf16[64,22,256]{2,1,0:T(8,128)(2,1)S(1)}, u32[]{:S(2)}, u32[]{:S(2)}) %all-to-all-start) | async-done | bytes 720928 | tf_op jit(solution)/shard_map/all_to_all | solution.py:49
  55.8 0.3 reshape.180
  56.0 1.1 %fusion.34 = (bf16[1408,1,1,128]{3,2,0,1:T(2,128)(2,1)S(1)}, bf16[1408,1,1,128]{3,2,0,1:T(2,128)(2,1)S(1)}) fusion(bf16[1408,1,2,128]{3,2,0,1:T(2,128)(2,1)S(1)} %reshape.180), kind=kLoop, calls=%fused_computation.50 | loop fusion | bytes 1441792 | tf_op jit(solution)/shard_map/slice | solution.py:52
  57.1 0.0 copy-start.2
  57.1 1.9 %fusion.36 = (f32[8,176]{1,0:T(8,128)S(1)}, f32[1,8,176,1408]{3,2,1,0:T(8,128)S(1)}) fusion(bf16[1408,1,1,128]{3,2,0,1:T(2,128)(2,1)S(1)} %get-tuple-element.11, pred[176,1408]{1,0:T(8,128)(4,1)S(1)} %broadcast_compare_fusion, bf16[176,1024]{1,0:T(8,128)(2,1)S(1)} %collective-permute-done.1), kind=kOutput, calls=%fused_computation.52 | convolution fusion | flops 513456768 | bytes 8904192 | tf_op jit(solution)/shard_map/qgjd,kgd->gjqk/dot_general | solution.py:64
  59.0 2.0 %select_reduce_fusion = f32[8,176]{1,0:T(8,128)S(1)} fusion(f32[1,8,176,1408]{3,2,1,0:T(8,128)S(1)} %get-tuple-element.15, f32[8,176]{1,0:T(8,128)S(1)} %get-tuple-element.14, pred[176,1408]{1,0:T(8,128)(4,1)S(1)} %broadcast_compare_fusion), kind=kLoop, calls=%fused_computation.5 | loop fusion | flops 5945984 | bytes 8188928 | tf_op jit(solution)/shard_map/reduce_sum | solution.py:67
  61.1 1.9 %fusion.23 = (f32[176,8]{0,1:T(8,128)S(1)}, bf16[176,1,8,128]{3,0,2,1:T(8,128)(2,1)S(1)}) fusion(f32[176,1,8,128]{3,2,0,1:T(8,128)S(1)} %bitcast.153, f32[1,8,176,1408]{3,2,1,0:T(8,128)S(1)} %get-tuple-element.15, f32[8,176]{1,0:T(8,128)S(1)} %log_add_fusion, pred[176,1408]{1,0:T(8,128)(4,1)S(1)} %broadcast_compare_fusion, ...), kind=kOutput, calls=%fused_computation.26 | convolution fusion | flops 513997440 | bytes 9630720 | tf_op jit(solution)/shard_map/gjqk,kgd->qgjd/dot_general | solution.py:71
  63.0 0.0 copy-start.3
  63.0 2.9 %fusion.6 = bf16[8,176,1408]{2,1,0:T(8,128)(2,1)S(1)} fusion(f32[8,176]{1,0:T(8,128)S(1)} %bitcast.163, f32[1,8,176,1408]{3,2,1,0:T(8,128)S(1)} %get-tuple-element.15, f32[8,176]{1,0:T(8,128)S(1)} %log_add_fusion, pred[176,1408]{1,0:T(8,128)(4,1)S(1)} %broadcast_compare_fusion, bf16[1408,1,1,128]{3,2,0,1:T(2,128)(2,1)S(1)} %get-tuple-element.10, ...), kind=kOutput, calls=%fused_computation.10 | convolution fusion | flops 517423104 | bytes 12874752 | tf_op jit(solution)/shard_map/qgjd,kgd->gjqk/dot_general | solution.py:75
  66.0 0.9 fusion.17
  66.8 1.7 %fusion.20 = bf16[1408,1,1,128]{0,3,2,1:T(8,128)(2,1)S(1)} fusion(f32[1,8,176,1408]{3,2,1,0:T(8,128)S(1)} %get-tuple-element.15, f32[8,176]{1,0:T(8,128)S(1)} %log_add_fusion, pred[176,1408]{1,0:T(8,128)(4,1)S(1)} %broadcast_compare_fusion, bf16[176,1024]{1,0:T(8,128)(2,1)S(1)} %collective-permute-done.2), kind=kOutput, calls=%fused_computation.17 | convolution fusion | flops 513638400 | bytes 8904192 | tf_op jit(solution)/shard_map/gjqk,qgjd->kgd/dot_general | solution.py:81
  68.5 0.0 copy-done.1
  68.5 0.1 pad_maximum_fusion
  68.6 1.0 %copy.67 = bf16[1408,1,2,128]{3,2,0,1:T(2,128)(2,1)S(1)} copy(bf16[1408,1,2,128]{0,3,2,1:T(8,128)(2,1)S(1)} %pad_maximum_fusion) | data formatting | bytes 1441792 | tf_op jit(solution)/shard_map/stack | solution.py:85
  69.6 1.3 %convert_element_type.54 = bf16[64,22,256]{2,1,0:T(8,128)(2,1)} reshape(bf16[1408,1,2,128]{3,2,0,1:T(2,128)(2,1)S(1)} %copy.67) | data formatting | bytes 1441792 | tf_op jit(solution)/shard_map/convert_element_type | solution.py:87
  71.0 4.9 %all-to-all-start.1 = ((bf16[64,22,256]{2,1,0:T(8,128)(2,1)}), bf16[64,22,256]{2,1,0:T(8,128)(2,1)S(1)}, u32[]{:S(2)}, u32[]{:S(2)}) async-start(bf16[64,22,256]{2,1,0:T(8,128)(2,1)} %convert_element_type.54), calls=%async_computation.1 | async-start | bytes 1572864 | tf_op jit(solution)/shard_map/all_to_all | solution.py:86
  75.9 0.1 copy.60
  76.0 0.9 broadcast_in_dim_reshape.6
  76.9 3.3 %fusion.22 = bf16[176,1,8,128]{3,0,2,1:T(8,128)(2,1)S(1)} fusion(bf16[8,176,1408]{2,1,0:T(8,128)(2,1)} %copy-done.1, bf16[1408,1,1,128]{3,2,0,1:T(2,128)(2,1)S(1)} %get-tuple-element.11), kind=kOutput, calls=%fused_computation.23 | convolution fusion | flops 507871232 | bytes 4685824 | tf_op jit(solution)/shard_map/gjqk,kgd->qgjd/dot_general | solution.py:78
  80.2 0.1 copy.63
  80.3 0.9 broadcast_in_dim_reshape.7
  81.2 18.5 %all-to-all-done.1 = bf16[64,22,256]{2,1,0:T(8,128)(2,1)S(1)} async-done(((bf16[64,22,256]{2,1,0:T(8,128)(2,1)}), bf16[64,22,256]{2,1,0:T(8,128)(2,1)S(1)}, u32[]{:S(2)}, u32[]{:S(2)}) %all-to-all-start.1) | async-done | bytes 720928 | tf_op jit(solution)/shard_map/all_to_all | solution.py:86
  99.7 0.1 convert_bitcast_fusion
  99.8 0.4 bitcast_reduce_fusion
  100.2 0.7 fusion.35
  (17 shorter events, 0.2 us)
Async XLA Ops:
  0.6 31.3 %copy-start = (bf16[1,2,176,1024]{3,2,1,0:T(8,128)(2,1)S(1)}, bf16[1,2,176,1024]{3,2,1,0:T(8,128)(2,1)}, u32[]{:S(2)}) copy-start(bf16[1,2,176,1024]{3,2,1,0:T(8,128)(2,1)} %param.8) | copy-start | bytes 2162692
  5.6 14.0 %collective-permute-start = (bf16[22,2048]{1,0:T(8,128)(2,1)S(1)}, bf16[22,2048]{1,0:T(8,128)(2,1)S(1)}, u32[]{:S(2)}, u32[]{:S(2)}) collective-permute-start(bf16[22,2048]{1,0:T(8,128)(2,1)S(1)} %reshape.178), channel_id=1, source_target_pairs={{448,0},{0,64},{64,128},{128,192},{192,256},{256,320},{320,384},{3... | collective-permute-start | bytes 270344 | tf_op jit(solution)/shard_map/ppermute | solution.py:15
  10.4 24.9 %collective-permute-start.2 = (bf16[176,1024]{1,0:T(8,128)(2,1)}, bf16[176,1024]{1,0:T(8,128)(2,1)S(1)}, u32[]{:S(2)}, u32[]{:S(2)}) collective-permute-start(bf16[176,1024]{1,0:T(8,128)(2,1)} %bitcast.165), channel_id=1, source_target_pairs={{64,0},{128,64},{192,128},{256,192},{320,256},{384,320},{448,384},... | collective-permute-start | bytes 1081352 | tf_op jit(solution)/shard_map/ppermute | solution.py:15
  20.6 35.2 %all-to-all-start = ((bf16[64,22,256]{2,1,0:T(8,128)(2,1)}), bf16[64,22,256]{2,1,0:T(8,128)(2,1)S(1)}, u32[]{:S(2)}, u32[]{:S(2)}) async-start(bf16[64,22,256]{2,1,0:T(8,128)(2,1)} %bitcast.3), calls=%async_computation | async-start | bytes 1572864 | tf_op jit(solution)/shard_map/all_to_all | solution.py:49
  32.0 12.6 %collective-permute-start.1 = (bf16[176,1024]{1,0:T(8,128)(2,1)S(1)}, bf16[176,1024]{1,0:T(8,128)(2,1)S(1)}, u32[]{:S(2)}, u32[]{:S(2)}) collective-permute-start(bf16[176,1024]{1,0:T(8,128)(2,1)S(1)} %dynamic-slice_bitcast_fusion), channel_id=1, source_target_pairs={{448,0},{0,64},{64,128},{128,192},{192,256},{256,320},{320,384},{3... | collective-permute-start | bytes 1081352 | tf_op jit(solution)/shard_map/ppermute | solution.py:15
  57.1 4.0 %copy-start.2 = (f32[22,8,8,128]{3,2,1,0:T(8,128)S(1)}, f32[22,8,8,128]{3,2,1,0:T(8,128)}, u32[]{:S(2)}) copy-start(f32[22,8,8,128]{3,2,1,0:T(8,128)} %copy.78) | copy-start | bytes 2162692
  63.0 3.0 %copy-start.3 = (bf16[22,8,8,128]{3,2,1,0:T(8,128)(2,1)S(1)}, bf16[22,8,8,128]{3,2,1,0:T(8,128)(2,1)}, u32[]{:S(2)}) copy-start(bf16[22,8,8,128]{3,2,1,0:T(8,128)(2,1)} %copy.79) | copy-start | bytes 1081348
  65.9 2.6 %copy-start.1 = (bf16[8,176,1408]{2,1,0:T(8,128)(2,1)}, bf16[8,176,1408]{2,1,0:T(8,128)(2,1)S(1)}, u32[]{:S(2)}) copy-start(bf16[8,176,1408]{2,1,0:T(8,128)(2,1)S(1)} %fusion.6) | copy-start | bytes 11894788
  71.0 28.7 %all-to-all-start.1 = ((bf16[64,22,256]{2,1,0:T(8,128)(2,1)}), bf16[64,22,256]{2,1,0:T(8,128)(2,1)S(1)}, u32[]{:S(2)}, u32[]{:S(2)}) async-start(bf16[64,22,256]{2,1,0:T(8,128)(2,1)} %convert_element_type.54), calls=%async_computation.1 | async-start | bytes 1572864 | tf_op jit(solution)/shard_map/all_to_all | solution.py:86

commit v11 on v10

--- a/solution.py
+++ b/solution.py
@@ -33,9 +33,16 @@
 
     receiver = (section_rank + 1) % section_count
     wanted = lax.dynamic_index_in_dim(plan, receiver, 0, keepdims=False)
-    q_send = lax.dynamic_index_in_dim(q_box[0], wanted, 0, keepdims=False)
-    k_send = lax.dynamic_index_in_dim(k_box[0], wanted, 0, keepdims=False)
-    v_send = lax.dynamic_index_in_dim(v_box[0], wanted, 0, keepdims=False)
+    def pick(box):
+        slots = box[0]
+        chosen = slots[0]
+        for slot in range(1, slots.shape[0]):
+            chosen = jnp.where(wanted == slot, slots[slot], chosen)
+        return chosen
+
+    q_send = pick(q_box)
+    k_send = pick(k_box)
+    v_send = pick(v_box)
     kv_send = jnp.stack(
         [k_send.reshape(kv_rows, -1, head_size), v_send.reshape(kv_rows, -1, head_size)], axis=2
     ).reshape(kv_rows, -1)

time: 101 us -> 101 us (level)
  other arithmetic: 3.64 us -> 6.34 us
  local copies, waits for them, and re-layouts: 12.5 us -> 10.1 us
  between operations: 2.93 us -> 1.61 us
    select_n x0 -> x2, other arithmetic: none -> 2.7 us  [pick(): chosen = jnp.where(wanted == slot, slots[slot], chosen)]
    dynamic_slice x1 -> x0, local copies, waits for them, and re-layouts: 1.47 us -> none  [body(): v_send = lax.dynamic_index_in_dim(v_box[0], wanted, 0, keepdims=False)]
    all_to_all x1, waiting for transfers between devices: 10.3 us -> 9.24 us  [body(): lax.all_to_all(kv_pieces, plane, split_axis=0, concat_axis=0, tiled=True)]
  transfers between devices with their start and end apart: 5 -> 5, of which waited for: 4 -> 4; matrix products, arithmetic and copies ran while one was open for 9% -> 10% of each run, Pallas kernels for 0% -> 0%
where the time goes in v11:
time: 101 us; the launch traced here: 100 us
  waiting for transfers between devices  37.4 us (37%)
  starting transfers between devices  31.6 us (31%)
  matrix products  13.1 us (13%)
  local copies, waits for them, and re-layouts  10.1 us (10%)
  other arithmetic  6.34 us (6%)
  between operations  1.61 us (2%)
    all_to_all x1, waiting for transfers between devices, body(): lax.all_to_all(grad_terms.astype(jnp.bfloat16), plane, split_axis=0, conc...  18.5 us
    ppermute x3, starting transfers between devices, passed_along(): return lax.ppermute(block, axis, route)  15.3 us
    all_to_all x1, starting transfers between devices, body(): lax.all_to_all(kv_pieces, plane, split_axis=0, concat_axis=0, tiled=True)  11.4 us
    ppermute x3, waiting for transfers between devices, passed_along(): return lax.ppermute(block, axis, route)  9.64 us
    all_to_all x1, waiting for transfers between devices, body(): lax.all_to_all(kv_pieces, plane, split_axis=0, concat_axis=0, tiled=True)  9.24 us
    all_to_all x1, starting transfers between devices, body(): lax.all_to_all(grad_terms.astype(jnp.bfloat16), plane, split_axis=0, conc...  4.93 us
    dot_general x1, matrix products, body(): jnp.einsum('gjqk,kgd->qgjd', dscores, key_heads, preferred_element_type=j...  3.32 us
    dot_general x1, matrix products, body(): jnp.einsum('qgjd,kgd->gjqk', do4, value_heads, preferred_element_type=jnp...  2.89 us
  transfers between devices with their start and end apart: 5, of which 4 were waited for; matrix products, arithmetic and copies ran while one was open for 10% of the time, Pallas kernels for 0%

profile of v11, /device:TPU:1, one launch (start us, length us, event | category | flops | bytes accessed | tf_op | source)
XLA Modules:
  0.0 100.2 jit_solution(13942801022565249801)
XLA Ops:
  0.6 1.2 %dynamic_slice.8 = s32[1]{0:T(128)} dynamic-slice(s32[8]{0:T(128)} %param.7, s32[]{:T(128)S(6)} %select_n.69), dynamic_slice_sizes={1} | dynamic-slice | bytes 12 | tf_op jit(solution)/shard_map/jit(dynamic_index_in_dim)/dynamic_slice | solution.py:35
  2.5 1.6 %fusion.32 = (bf16[22,1024]{1,0:T(8,128)(2,1)S(1)}, bf16[22,1024]{1,0:T(8,128)(2,1)S(1)}) fusion(pred[]{:T(512)} %bitcast, bf16[1,2,22,1024]{3,1,2,0:T(2,128)(2,1)} %param.9, bf16[1,2,22,1024]{3,1,2,0:T(2,128)(2,1)} %param.10), kind=kLoop, calls=%fused_computation.40 | loop fusion | flops 45056 | bytes 270337 | tf_op jit(solution)/shard_map/jit(_where)/select_n | solution.py:40
  4.2 0.1 copy.55
  4.3 4.8 %collective-permute-start = (bf16[22,2048]{1,0:T(8,128)(2,1)S(1)}, bf16[22,2048]{1,0:T(8,128)(2,1)S(1)}, u32[]{:S(2)}, u32[]{:S(2)}) collective-permute-start(bf16[22,2048]{1,0:T(8,128)(2,1)S(1)} %reshape.224), channel_id=1, source_target_pairs={{448,0},{0,64},{64,128},{128,192},{192,256},{256,320},{320,384},{3... | collective-permute-start | bytes 270344 | tf_op jit(solution)/shard_map/ppermute | solution.py:15
  9.1 8.6 %collective-permute-start.2 = (bf16[176,1024]{1,0:T(8,128)(2,1)}, bf16[176,1024]{1,0:T(8,128)(2,1)S(1)}, u32[]{:S(2)}, u32[]{:S(2)}) collective-permute-start(bf16[176,1024]{1,0:T(8,128)(2,1)} %bitcast.165), channel_id=1, source_target_pairs={{64,0},{128,64},{192,128},{256,192},{320,256},{384,320},{448,384},... | collective-permute-start | bytes 1081352 | tf_op jit(solution)/shard_map/ppermute | solution.py:15
  17.7 0.6 collective-permute-done
  18.4 0.9 broadcast_in_dim.37
  19.3 11.4 %all-to-all-start = ((bf16[64,22,256]{2,1,0:T(8,128)(2,1)}), bf16[64,22,256]{2,1,0:T(8,128)(2,1)S(1)}, u32[]{:S(2)}, u32[]{:S(2)}) async-start(bf16[64,22,256]{2,1,0:T(8,128)(2,1)} %bitcast.3), calls=%async_computation | async-start | bytes 1572864 | tf_op jit(solution)/shard_map/all_to_all | solution.py:56
  30.7 1.1 %select_bitcast_fusion = bf16[176,1024]{1,0:T(8,128)(2,1)S(1)} fusion(bf16[1,2,176,1024]{3,2,1,0:T(8,128)(2,1)} %param.8, pred[]{:T(512)} %bitcast), kind=kLoop, calls=%fused_computation.35 | loop fusion | flops 180224 | bytes 1081345 | tf_op jit(solution)/shard_map/jit(_where)/select_n | solution.py:40
  31.8 1.9 %collective-permute-start.1 = (bf16[176,1024]{1,0:T(8,128)(2,1)S(1)}, bf16[176,1024]{1,0:T(8,128)(2,1)S(1)}, u32[]{:S(2)}, u32[]{:S(2)}) collective-permute-start(bf16[176,1024]{1,0:T(8,128)(2,1)S(1)} %select_bitcast_fusion), channel_id=1, source_target_pairs={{448,0},{0,64},{64,128},{128,192},{192,256},{256,320},{320,384},{3... | collective-permute-start | bytes 1081352 | tf_op jit(solution)/shard_map/ppermute | solution.py:15
  33.7 0.7 broadcast_multiply_fusion
  34.4 0.1 add.65
  34.5 0.1 iota_add_fusion
  34.6 0.1 add.64
  34.6 0.1 add.66
  34.7 0.1 add.67
  34.8 0.1 add.69
  34.9 0.2 broadcast_compare_fusion
  35.1 0.0 collective-permute-done.2
  35.1 0.1 convert_bitcast_fusion.1
  35.2 0.1 copy.78
  35.3 9.1 %collective-permute-done.1 = bf16[176,1024]{1,0:T(8,128)(2,1)S(1)} collective-permute-done((bf16[176,1024]{1,0:T(8,128)(2,1)S(1)}, bf16[176,1024]{1,0:T(8,128)(2,1)S(1)}, u32[]{:S(2)}, u32[]{:S(2)}) %collective-permute-start.1) | collective-permute-done | bytes 360480 | tf_op jit(solution)/shard_map/ppermute | solution.py:15
  44.4 0.8 copy.79
  45.2 9.2 %all-to-all-done = bf16[64,22,256]{2,1,0:T(8,128)(2,1)S(1)} async-done(((bf16[64,22,256]{2,1,0:T(8,128)(2,1)}), bf16[64,22,256]{2,1,0:T(8,128)(2,1)S(1)}, u32[]{:S(2)}, u32[]{:S(2)}) %all-to-all-start) | async-done | bytes 720928 | tf_op jit(solution)/shard_map/all_to_all | solution.py:56
  54.5 0.3 reshape.226
  54.8 1.1 %fusion.36 = (bf16[1408,1,1,128]{3,2,0,1:T(2,128)(2,1)S(1)}, bf16[1408,1,1,128]{3,2,0,1:T(2,128)(2,1)S(1)}) fusion(bf16[1408,1,2,128]{3,2,0,1:T(2,128)(2,1)S(1)} %reshape.226), kind=kLoop, calls=%fused_computation.52 | loop fusion | bytes 1441792 | tf_op jit(solution)/shard_map/slice | solution.py:59
  55.8 1.9 %fusion.38 = (f32[8,176]{1,0:T(8,128)S(1)}, f32[1,8,176,1408]{3,2,1,0:T(8,128)S(1)}) fusion(bf16[1408,1,1,128]{3,2,0,1:T(2,128)(2,1)S(1)} %get-tuple-element.11, pred[176,1408]{1,0:T(8,128)(4,1)S(1)} %broadcast_compare_fusion, bf16[176,1024]{1,0:T(8,128)(2,1)S(1)} %collective-permute-done.1), kind=kOutput, calls=%fused_computation.54 | convolution fusion | flops 513456768 | bytes 8904192 | tf_op jit(solution)/shard_map/qgjd,kgd->gjqk/dot_general | solution.py:71
  57.7 2.0 %select_reduce_fusion = f32[8,176]{1,0:T(8,128)S(1)} fusion(f32[1,8,176,1408]{3,2,1,0:T(8,128)S(1)} %get-tuple-element.15, f32[8,176]{1,0:T(8,128)S(1)} %get-tuple-element.14, pred[176,1408]{1,0:T(8,128)(4,1)S(1)} %broadcast_compare_fusion), kind=kLoop, calls=%fused_computation.5 | loop fusion | flops 5945984 | bytes 8188928 | tf_op jit(solution)/shard_map/reduce_sum | solution.py:74
  59.8 2.5 %fusion.23 = (f32[176,8]{0,1:T(8,128)S(1)}, bf16[176,1,8,128]{3,0,2,1:T(8,128)(2,1)}) fusion(f32[176,1,8,128]{3,2,0,1:T(8,128)S(1)} %bitcast.153, f32[1,8,176,1408]{3,2,1,0:T(8,128)S(1)} %get-tuple-element.15, f32[8,176]{1,0:T(8,128)S(1)} %log_add_fusion, pred[176,1408]{1,0:T(8,128)(4,1)S(1)} %broadcast_compare_fusion, ...), kind=kOutput, calls=%fused_computation.26 | convolution fusion | flops 513997440 | bytes 9630720 | tf_op jit(solution)/shard_map/gjqk,kgd->qgjd/dot_general | solution.py:78
  62.3 2.9 %fusion.6 = bf16[8,176,1408]{2,1,0:T(8,128)(2,1)S(1)} fusion(f32[8,176]{1,0:T(8,128)S(1)} %bitcast.163, f32[1,8,176,1408]{3,2,1,0:T(8,128)S(1)} %get-tuple-element.15, f32[8,176]{1,0:T(8,128)S(1)} %log_add_fusion, pred[176,1408]{1,0:T(8,128)(4,1)S(1)} %broadcast_compare_fusion, bf16[1408,1,1,128]{3,2,0,1:T(2,128)(2,1)S(1)} %get-tuple-element.10, ...), kind=kOutput, calls=%fused_computation.10 | convolution fusion | flops 517423104 | bytes 12874752 | tf_op jit(solution)/shard_map/qgjd,kgd->gjqk/dot_general | solution.py:82
  65.2 0.0 copy-start
  65.2 0.9 fusion.17
  66.1 0.0 copy-start.2
  66.1 1.7 %fusion.20 = bf16[1408,1,1,128]{0,3,2,1:T(8,128)(2,1)S(1)} fusion(f32[1,8,176,1408]{3,2,1,0:T(8,128)S(1)} %get-tuple-element.15, f32[8,176]{1,0:T(8,128)S(1)} %log_add_fusion, pred[176,1408]{1,0:T(8,128)(4,1)S(1)} %broadcast_compare_fusion, bf16[176,1024]{1,0:T(8,128)(2,1)S(1)} %collective-permute-done.2), kind=kOutput, calls=%fused_computation.17 | convolution fusion | flops 513638400 | bytes 8904192 | tf_op jit(solution)/shard_map/gjqk,qgjd->kgd/dot_general | solution.py:88
  67.7 0.0 copy-done
  67.7 0.1 pad_maximum_fusion
  67.8 1.0 %copy.67 = bf16[1408,1,2,128]{3,2,0,1:T(2,128)(2,1)S(1)} copy(bf16[1408,1,2,128]{0,3,2,1:T(8,128)(2,1)S(1)} %pad_maximum_fusion) | data formatting | bytes 1441792 | tf_op jit(solution)/shard_map/stack | solution.py:92
  68.9 1.3 %convert_element_type.54 = bf16[64,22,256]{2,1,0:T(8,128)(2,1)} reshape(bf16[1408,1,2,128]{3,2,0,1:T(2,128)(2,1)S(1)} %copy.67) | data formatting | bytes 1441792 | tf_op jit(solution)/shard_map/convert_element_type | solution.py:94
  70.2 4.9 %all-to-all-start.1 = ((bf16[64,22,256]{2,1,0:T(8,128)(2,1)}), bf16[64,22,256]{2,1,0:T(8,128)(2,1)S(1)}, u32[]{:S(2)}, u32[]{:S(2)}) async-start(bf16[64,22,256]{2,1,0:T(8,128)(2,1)} %convert_element_type.54), calls=%async_computation.1 | async-start | bytes 1572864 | tf_op jit(solution)/shard_map/all_to_all | solution.py:93
  75.1 0.1 copy.60
  75.3 0.9 broadcast_in_dim_reshape.6
  76.1 3.3 %fusion.22 = bf16[176,1,8,128]{3,0,2,1:T(8,128)(2,1)S(1)} fusion(bf16[8,176,1408]{2,1,0:T(8,128)(2,1)} %copy-done, bf16[1408,1,1,128]{3,2,0,1:T(2,128)(2,1)S(1)} %get-tuple-element.11), kind=kOutput, calls=%fused_computation.23 | convolution fusion | flops 507871232 | bytes 4685824 | tf_op jit(solution)/shard_map/gjqk,kgd->qgjd/dot_general | solution.py:85
  79.5 0.1 copy.63
  79.6 0.9 broadcast_in_dim_reshape.7
  80.5 18.5 %all-to-all-done.1 = bf16[64,22,256]{2,1,0:T(8,128)(2,1)S(1)} async-done(((bf16[64,22,256]{2,1,0:T(8,128)(2,1)}), bf16[64,22,256]{2,1,0:T(8,128)(2,1)S(1)}, u32[]{:S(2)}, u32[]{:S(2)}) %all-to-all-start.1) | async-done | bytes 720928 | tf_op jit(solution)/shard_map/all_to_all | solution.py:93
  98.9 0.1 convert_bitcast_fusion
  99.1 0.4 bitcast_reduce_fusion
  99.5 0.7 fusion.37
  (15 shorter events, 0.2 us)
Async XLA Ops:
  4.3 14.0 %collective-permute-start = (bf16[22,2048]{1,0:T(8,128)(2,1)S(1)}, bf16[22,2048]{1,0:T(8,128)(2,1)S(1)}, u32[]{:S(2)}, u32[]{:S(2)}) collective-permute-start(bf16[22,2048]{1,0:T(8,128)(2,1)S(1)} %reshape.224), channel_id=1, source_target_pairs={{448,0},{0,64},{64,128},{128,192},{192,256},{256,320},{320,384},{3... | collective-permute-start | bytes 270344 | tf_op jit(solution)/shard_map/ppermute | solution.py:15
  9.1 26.0 %collective-permute-start.2 = (bf16[176,1024]{1,0:T(8,128)(2,1)}, bf16[176,1024]{1,0:T(8,128)(2,1)S(1)}, u32[]{:S(2)}, u32[]{:S(2)}) collective-permute-start(bf16[176,1024]{1,0:T(8,128)(2,1)} %bitcast.165), channel_id=1, source_target_pairs={{64,0},{128,64},{192,128},{256,192},{320,256},{384,320},{448,384},... | collective-permute-start | bytes 1081352 | tf_op jit(solution)/shard_map/ppermute | solution.py:15
  19.3 35.2 %all-to-all-start = ((bf16[64,22,256]{2,1,0:T(8,128)(2,1)}), bf16[64,22,256]{2,1,0:T(8,128)(2,1)S(1)}, u32[]{:S(2)}, u32[]{:S(2)}) async-start(bf16[64,22,256]{2,1,0:T(8,128)(2,1)} %bitcast.3), calls=%async_computation | async-start | bytes 1572864 | tf_op jit(solution)/shard_map/all_to_all | solution.py:56
  31.8 12.6 %collective-permute-start.1 = (bf16[176,1024]{1,0:T(8,128)(2,1)S(1)}, bf16[176,1024]{1,0:T(8,128)(2,1)S(1)}, u32[]{:S(2)}, u32[]{:S(2)}) collective-permute-start(bf16[176,1024]{1,0:T(8,128)(2,1)S(1)} %select_bitcast_fusion), channel_id=1, source_target_pairs={{448,0},{0,64},{64,128},{128,192},{192,256},{256,320},{320,384},{3... | collective-permute-start | bytes 1081352 | tf_op jit(solution)/shard_map/ppermute | solution.py:15
  62.2 2.9 %copy-start.1 = (bf16[22,8,8,128]{3,2,1,0:T(8,128)(2,1)S(1)}, bf16[22,8,8,128]{3,2,1,0:T(8,128)(2,1)}, u32[]{:S(2)}) copy-start(bf16[22,8,8,128]{3,2,1,0:T(8,128)(2,1)} %copy.79) | copy-start | bytes 1081348
  65.2 2.6 %copy-start = (bf16[8,176,1408]{2,1,0:T(8,128)(2,1)}, bf16[8,176,1408]{2,1,0:T(8,128)(2,1)S(1)}, u32[]{:S(2)}) copy-start(bf16[8,176,1408]{2,1,0:T(8,128)(2,1)S(1)} %fusion.6) | copy-start | bytes 11894788
  66.1 9.1 %copy-start.2 = (bf16[176,1,8,128]{3,0,2,1:T(8,128)(2,1)S(1)}, bf16[176,1,8,128]{3,0,2,1:T(8,128)(2,1)}, u32[]{:S(2)}) copy-start(bf16[176,1,8,128]{3,0,2,1:T(8,128)(2,1)} %get-tuple-element.9) | copy-start | bytes 1081348
  70.2 28.7 %all-to-all-start.1 = ((bf16[64,22,256]{2,1,0:T(8,128)(2,1)}), bf16[64,22,256]{2,1,0:T(8,128)(2,1)S(1)}, u32[]{:S(2)}, u32[]{:S(2)}) async-start(bf16[64,22,256]{2,1,0:T(8,128)(2,1)} %convert_element_type.54), calls=%async_computation.1 | async-start | bytes 1572864 | tf_op jit(solution)/shard_map/all_to_all | solution.py:93

commit v12 on v11

--- a/solution.py
+++ b/solution.py
@@ -33,6 +33,7 @@
 
     receiver = (section_rank + 1) % section_count
     wanted = lax.dynamic_index_in_dim(plan, receiver, 0, keepdims=False)
+
     def pick(box):
         slots = box[0]
         chosen = slots[0]
@@ -41,12 +42,19 @@
         return chosen
 
     q_send = pick(q_box)
-    k_send = pick(k_box)
-    v_send = pick(v_box)
-    kv_send = jnp.stack(
-        [k_send.reshape(kv_rows, -1, head_size), v_send.reshape(kv_rows, -1, head_size)], axis=2
-    ).reshape(kv_rows, -1)
-    queries, kv_rows_in = passed_along((q_send, kv_send), "section", 1)
+    slot_count = k_box.shape[1]
+    kv_both = jnp.stack(
+        [
+            k_box[0].reshape(slot_count, kv_rows, -1, head_size),
+            v_box[0].reshape(slot_count, kv_rows, -1, head_size),
+        ],
+        axis=3,
+    ).reshape(slot_count, kv_rows, -1)
+    queries, kv_both_in = passed_along((q_send, kv_both), "section", 1)
+    own_wanted = lax.dynamic_index_in_dim(plan, section_rank, 0, keepdims=False)
+    kv_rows_in = kv_both_in[0]
+    for slot in range(1, slot_count):
+        kv_rows_in = jnp.where(own_wanted == slot, kv_both_in[slot], kv_rows_in)
     cotangent = passed_along(grad_out[0], "section", -1)
 
     plane = ("ctx", "tp")

time: 101 us -> 102 us (level)
  local copies, waits for them, and re-layouts: 10.1 us -> 12 us
    another operation x1 -> x2, local copies, waits for them, and re-layouts: 0.07 us -> 1.92 us  [body(): jnp.stack([k_box[0].reshape(slot_count, kv_rows, -1, head_size), v_box[0]...]
    select_n x2 -> x1, other arithmetic: 2.7 us -> 1.14 us  [pick(): chosen = jnp.where(wanted == slot, slots[slot], chosen)]
  transfers between devices with their start and end apart: 5 -> 5, of which waited for: 4 -> 3; matrix products, arithmetic and copies ran while one was open for 10% -> 11% of each run, Pallas kernels for 0% -> 0%
where the time goes in v12:
time: 102 us; the launch traced here: 101 us
  waiting for transfers between devices  36.6 us (36%)
  starting transfers between devices  31.5 us (31%)
  matrix products  13.1 us (13%)
  local copies, waits for them, and re-layouts  12 us (12%)
  other arithmetic  5.67 us (6%)
  between operations  2.24 us (2%)
    all_to_all x1, waiting for transfers between devices, body(): lax.all_to_all(grad_terms.astype(jnp.bfloat16), plane, split_axis=0, conc...  18.5 us
    ppermute x3, starting transfers between devices, passed_along(): return lax.ppermute(block, axis, route)  15.5 us
    all_to_all x1, starting transfers between devices, body(): lax.all_to_all(kv_pieces, plane, split_axis=0, concat_axis=0, tiled=True)  11.1 us
    all_to_all x1, waiting for transfers between devices, body(): lax.all_to_all(kv_pieces, plane, split_axis=0, concat_axis=0, tiled=True)  9.24 us
    ppermute x3, waiting for transfers between devices, passed_along(): return lax.ppermute(block, axis, route)  8.91 us
    all_to_all x1, starting transfers between devices, body(): lax.all_to_all(grad_terms.astype(jnp.bfloat16), plane, split_axis=0, conc...  4.93 us
    dot_general x1, matrix products, body(): jnp.einsum('gjqk,kgd->qgjd', dscores, key_heads, preferred_element_type=j...  3.32 us
    dot_general x1, matrix products, body(): jnp.einsum('qgjd,kgd->gjqk', do4, value_heads, preferred_element_type=jnp...  2.89 us
  transfers between devices with their start and end apart: 5, of which 3 were waited for; matrix products, arithmetic and copies ran while one was open for 11% of the time, Pallas kernels for 0%

profile of v12, /device:TPU:1, one launch (start us, length us, event | category | flops | bytes accessed | tf_op | source)
XLA Modules:
  0.0 101.2 jit_solution(15213628876527427439)
XLA Ops:
  0.6 1.0 stack_reshape_squeeze.9
  1.6 1.0 stack_reshape_squeeze.8
  2.6 0.4 pad_maximum_fusion.1
  3.0 4.8 %collective-permute-start = (bf16[2,22,2048]{2,0,1:T(2,128)(2,1)S(1)}, bf16[2,22,2048]{2,0,1:T(2,128)(2,1)S(1)}, u32[]{:S(2)}, u32[]{:S(2)}) collective-permute-start(bf16[2,22,2048]{2,0,1:T(2,128)(2,1)S(1)} %reshape.197), channel_id=1, source_target_pairs={{448,0},{0,64},{64,128},{128,192},{192,256},{256,320},{320,384},{3... | collective-permute-start | bytes 540680 | tf_op jit(solution)/shard_map/ppermute | solution.py:15
  7.9 8.6 %collective-permute-start.2 = (bf16[176,1024]{1,0:T(8,128)(2,1)}, bf16[176,1024]{1,0:T(8,128)(2,1)S(1)}, u32[]{:S(2)}, u32[]{:S(2)}) collective-permute-start(bf16[176,1024]{1,0:T(8,128)(2,1)} %bitcast.156), channel_id=1, source_target_pairs={{64,0},{128,64},{192,128},{256,192},{320,256},{384,320},{448,384},... | collective-permute-start | bytes 1081352 | tf_op jit(solution)/shard_map/ppermute | solution.py:15
  16.5 1.3 %fusion.37 = (s32[1]{0:T(128)}, s32[1]{0:T(128)}) fusion(s32[8]{0:T(128)} %param.7, s32[]{:T(128)S(6)} %select_n.57, s32[]{:T(128)S(6)} %select_n.63), kind=kLoop, calls=%fused_computation.50 | loop fusion | bytes 24 | tf_op jit(solution)/shard_map/jit(dynamic_index_in_dim)/dynamic_slice | solution.py:54
  19.1 0.0 collective-permute-done
  19.1 0.5 fusion.32
  19.7 0.9 broadcast_in_dim.37
  20.6 11.1 %all-to-all-start = ((bf16[64,22,256]{2,1,0:T(8,128)(2,1)}), bf16[64,22,256]{2,1,0:T(8,128)(2,1)S(1)}, u32[]{:S(2)}, u32[]{:S(2)}) async-start(bf16[64,22,256]{2,1,0:T(8,128)(2,1)} %bitcast.3), calls=%async_computation | async-start | bytes 1572864 | tf_op jit(solution)/shard_map/all_to_all | solution.py:64
  31.7 1.1 %select_bitcast_fusion = bf16[176,1024]{1,0:T(8,128)(2,1)S(1)} fusion(bf16[1,2,176,1024]{3,2,1,0:T(8,128)(2,1)} %param.8, pred[]{:T(512)} %bitcast.9), kind=kLoop, calls=%fused_computation.35 | loop fusion | flops 180224 | bytes 1081345 | tf_op jit(solution)/shard_map/jit(_where)/select_n | solution.py:41
  32.8 2.1 %collective-permute-start.1 = (bf16[176,1024]{1,0:T(8,128)(2,1)S(1)}, bf16[176,1024]{1,0:T(8,128)(2,1)S(1)}, u32[]{:S(2)}, u32[]{:S(2)}) collective-permute-start(bf16[176,1024]{1,0:T(8,128)(2,1)S(1)} %select_bitcast_fusion), channel_id=1, source_target_pairs={{448,0},{0,64},{64,128},{128,192},{192,256},{256,320},{320,384},{3... | collective-permute-start | bytes 1081352 | tf_op jit(solution)/shard_map/ppermute | solution.py:15
  35.0 0.7 broadcast_multiply_fusion
  35.6 0.1 add.66
  35.7 0.1 iota_add_fusion
  35.8 0.1 add.65
  35.9 0.1 add.67
  35.9 0.1 add.68
  36.0 0.1 add.70
  36.1 0.2 broadcast_compare_fusion
  36.3 0.0 collective-permute-done.2
  36.3 0.1 convert_bitcast_fusion.1
  36.4 0.1 copy.80
  36.6 8.9 %collective-permute-done.1 = bf16[176,1024]{1,0:T(8,128)(2,1)S(1)} collective-permute-done((bf16[176,1024]{1,0:T(8,128)(2,1)S(1)}, bf16[176,1024]{1,0:T(8,128)(2,1)S(1)}, u32[]{:S(2)}, u32[]{:S(2)}) %collective-permute-start.1) | collective-permute-done | bytes 360480 | tf_op jit(solution)/shard_map/ppermute | solution.py:15
  45.5 0.8 copy.81
  46.3 9.2 %all-to-all-done = bf16[64,22,256]{2,1,0:T(8,128)(2,1)S(1)} async-done(((bf16[64,22,256]{2,1,0:T(8,128)(2,1)}), bf16[64,22,256]{2,1,0:T(8,128)(2,1)S(1)}, u32[]{:S(2)}, u32[]{:S(2)}) %all-to-all-start) | async-done | bytes 720928 | tf_op jit(solution)/shard_map/all_to_all | solution.py:64
  55.5 0.3 reshape.198
  55.8 1.1 %fusion.35 = (bf16[1408,1,1,128]{3,2,0,1:T(2,128)(2,1)S(1)}, bf16[1408,1,1,128]{3,2,0,1:T(2,128)(2,1)S(1)}) fusion(bf16[1408,1,2,128]{3,2,0,1:T(2,128)(2,1)S(1)} %reshape.198), kind=kLoop, calls=%fused_computation.48 | loop fusion | bytes 1441792 | tf_op jit(solution)/shard_map/slice | solution.py:67
  56.9 1.9 %fusion.38 = (f32[8,176]{1,0:T(8,128)S(1)}, f32[1,8,176,1408]{3,2,1,0:T(8,128)S(1)}) fusion(bf16[1408,1,1,128]{3,2,0,1:T(2,128)(2,1)S(1)} %get-tuple-element.11, pred[176,1408]{1,0:T(8,128)(4,1)S(1)} %broadcast_compare_fusion, bf16[176,1024]{1,0:T(8,128)(2,1)S(1)} %collective-permute-done.1), kind=kOutput, calls=%fused_computation.51 | convolution fusion | flops 513456768 | bytes 8904192 | tf_op jit(solution)/shard_map/qgjd,kgd->gjqk/dot_general | solution.py:79
  58.8 2.0 %select_reduce_fusion = f32[8,176]{1,0:T(8,128)S(1)} fusion(f32[1,8,176,1408]{3,2,1,0:T(8,128)S(1)} %get-tuple-element.17, f32[8,176]{1,0:T(8,128)S(1)} %get-tuple-element.16, pred[176,1408]{1,0:T(8,128)(4,1)S(1)} %broadcast_compare_fusion), kind=kLoop, calls=%fused_computation.5 | loop fusion | flops 5945984 | bytes 8188928 | tf_op jit(solution)/shard_map/reduce_sum | solution.py:82
  60.8 2.5 %fusion.23 = (f32[176,8]{0,1:T(8,128)S(1)}, bf16[176,1,8,128]{3,0,2,1:T(8,128)(2,1)}) fusion(f32[176,1,8,128]{3,2,0,1:T(8,128)S(1)} %bitcast.148, f32[1,8,176,1408]{3,2,1,0:T(8,128)S(1)} %get-tuple-element.17, f32[8,176]{1,0:T(8,128)S(1)} %log_add_fusion, pred[176,1408]{1,0:T(8,128)(4,1)S(1)} %broadcast_compare_fusion, ...), kind=kOutput, calls=%fused_computation.26 | convolution fusion | flops 513997440 | bytes 9630720 | tf_op jit(solution)/shard_map/gjqk,kgd->qgjd/dot_general | solution.py:86
  63.3 2.9 %fusion.6 = bf16[8,176,1408]{2,1,0:T(8,128)(2,1)S(1)} fusion(f32[8,176]{1,0:T(8,128)S(1)} %bitcast.154, f32[1,8,176,1408]{3,2,1,0:T(8,128)S(1)} %get-tuple-element.17, f32[8,176]{1,0:T(8,128)S(1)} %log_add_fusion, pred[176,1408]{1,0:T(8,128)(4,1)S(1)} %broadcast_compare_fusion, bf16[1408,1,1,128]{3,2,0,1:T(2,128)(2,1)S(1)} %get-tuple-element.10, ...), kind=kOutput, calls=%fused_computation.10 | convolution fusion | flops 517423104 | bytes 12874752 | tf_op jit(solution)/shard_map/qgjd,kgd->gjqk/dot_general | solution.py:90
  66.2 0.9 fusion.17
  67.1 0.0 copy-start.2
  67.1 1.7 %fusion.20 = bf16[1408,1,1,128]{0,3,2,1:T(8,128)(2,1)S(1)} fusion(f32[1,8,176,1408]{3,2,1,0:T(8,128)S(1)} %get-tuple-element.17, f32[8,176]{1,0:T(8,128)S(1)} %log_add_fusion, pred[176,1408]{1,0:T(8,128)(4,1)S(1)} %broadcast_compare_fusion, bf16[176,1024]{1,0:T(8,128)(2,1)S(1)} %collective-permute-done.2), kind=kOutput, calls=%fused_computation.17 | convolution fusion | flops 513638400 | bytes 8904192 | tf_op jit(solution)/shard_map/gjqk,qgjd->kgd/dot_general | solution.py:96
  68.8 0.1 pad_maximum_fusion
  68.9 1.0 %copy.71 = bf16[1408,1,2,128]{3,2,0,1:T(2,128)(2,1)S(1)} copy(bf16[1408,1,2,128]{0,3,2,1:T(8,128)(2,1)S(1)} %pad_maximum_fusion) | data formatting | bytes 1441792 | tf_op jit(solution)/shard_map/stack | solution.py:100
  69.9 1.4 %convert_element_type.54 = bf16[64,22,256]{2,1,0:T(8,128)(2,1)} reshape(bf16[1408,1,2,128]{3,2,0,1:T(2,128)(2,1)S(1)} %copy.71) | data formatting | bytes 1441792 | tf_op jit(solution)/shard_map/convert_element_type | solution.py:102
  71.2 4.9 %all-to-all-start.1 = ((bf16[64,22,256]{2,1,0:T(8,128)(2,1)}), bf16[64,22,256]{2,1,0:T(8,128)(2,1)S(1)}, u32[]{:S(2)}, u32[]{:S(2)}) async-start(bf16[64,22,256]{2,1,0:T(8,128)(2,1)} %convert_element_type.54), calls=%async_computation.1 | async-start | bytes 1572864 | tf_op jit(solution)/shard_map/all_to_all | solution.py:101
  76.2 0.1 copy.64
  76.3 0.9 broadcast_in_dim_reshape.6
  77.2 3.3 %fusion.22 = bf16[176,1,8,128]{3,0,2,1:T(8,128)(2,1)S(1)} fusion(bf16[8,176,1408]{2,1,0:T(8,128)(2,1)} %copy-done, bf16[1408,1,1,128]{3,2,0,1:T(2,128)(2,1)S(1)} %get-tuple-element.11), kind=kOutput, calls=%fused_computation.23 | convolution fusion | flops 507871232 | bytes 4685824 | tf_op jit(solution)/shard_map/gjqk,kgd->qgjd/dot_general | solution.py:93
  80.5 0.1 copy.67
  80.6 0.9 broadcast_in_dim_reshape.7
  81.5 18.5 %all-to-all-done.1 = bf16[64,22,256]{2,1,0:T(8,128)(2,1)S(1)} async-done(((bf16[64,22,256]{2,1,0:T(8,128)(2,1)}), bf16[64,22,256]{2,1,0:T(8,128)(2,1)S(1)}, u32[]{:S(2)}, u32[]{:S(2)}) %all-to-all-start.1) | async-done | bytes 720928 | tf_op jit(solution)/shard_map/all_to_all | solution.py:101
  100.0 0.1 convert_bitcast_fusion
  100.1 0.4 bitcast_reduce_fusion
  100.5 0.7 fusion.36
  (12 shorter events, 0.1 us)
Async XLA Ops:
  3.0 16.1 %collective-permute-start = (bf16[2,22,2048]{2,0,1:T(2,128)(2,1)S(1)}, bf16[2,22,2048]{2,0,1:T(2,128)(2,1)S(1)}, u32[]{:S(2)}, u32[]{:S(2)}) collective-permute-start(bf16[2,22,2048]{2,0,1:T(2,128)(2,1)S(1)} %reshape.197), channel_id=1, source_target_pairs={{448,0},{0,64},{64,128},{128,192},{192,256},{256,320},{320,384},{3... | collective-permute-start | bytes 540680 | tf_op jit(solution)/shard_map/ppermute | solution.py:15
  7.9 28.5 %collective-permute-start.2 = (bf16[176,1024]{1,0:T(8,128)(2,1)}, bf16[176,1024]{1,0:T(8,128)(2,1)S(1)}, u32[]{:S(2)}, u32[]{:S(2)}) collective-permute-start(bf16[176,1024]{1,0:T(8,128)(2,1)} %bitcast.156), channel_id=1, source_target_pairs={{64,0},{128,64},{192,128},{256,192},{320,256},{384,320},{448,384},... | collective-permute-start | bytes 1081352 | tf_op jit(solution)/shard_map/ppermute | solution.py:15
  20.6 34.9 %all-to-all-start = ((bf16[64,22,256]{2,1,0:T(8,128)(2,1)}), bf16[64,22,256]{2,1,0:T(8,128)(2,1)S(1)}, u32[]{:S(2)}, u32[]{:S(2)}) async-start(bf16[64,22,256]{2,1,0:T(8,128)(2,1)} %bitcast.3), calls=%async_computation | async-start | bytes 1572864 | tf_op jit(solution)/shard_map/all_to_all | solution.py:64
  32.8 12.6 %collective-permute-start.1 = (bf16[176,1024]{1,0:T(8,128)(2,1)S(1)}, bf16[176,1024]{1,0:T(8,128)(2,1)S(1)}, u32[]{:S(2)}, u32[]{:S(2)}) collective-permute-start(bf16[176,1024]{1,0:T(8,128)(2,1)S(1)} %select_bitcast_fusion), channel_id=1, source_target_pairs={{448,0},{0,64},{64,128},{128,192},{192,256},{256,320},{320,384},{3... | collective-permute-start | bytes 1081352 | tf_op jit(solution)/shard_map/ppermute | solution.py:15
  63.3 2.9 %copy-start.1 = (bf16[22,8,8,128]{3,2,1,0:T(8,128)(2,1)S(1)}, bf16[22,8,8,128]{3,2,1,0:T(8,128)(2,1)}, u32[]{:S(2)}) copy-start(bf16[22,8,8,128]{3,2,1,0:T(8,128)(2,1)} %copy.81) | copy-start | bytes 1081348
  66.2 2.6 %copy-start = (bf16[8,176,1408]{2,1,0:T(8,128)(2,1)}, bf16[8,176,1408]{2,1,0:T(8,128)(2,1)S(1)}, u32[]{:S(2)}) copy-start(bf16[8,176,1408]{2,1,0:T(8,128)(2,1)S(1)} %fusion.6) | copy-start | bytes 11894788
  67.1 9.1 %copy-start.2 = (bf16[176,1,8,128]{3,0,2,1:T(8,128)(2,1)S(1)}, bf16[176,1,8,128]{3,0,2,1:T(8,128)(2,1)}, u32[]{:S(2)}) copy-start(bf16[176,1,8,128]{3,0,2,1:T(8,128)(2,1)} %get-tuple-element.9) | copy-start | bytes 1081348
  71.2 28.7 %all-to-all-start.1 = ((bf16[64,22,256]{2,1,0:T(8,128)(2,1)}), bf16[64,22,256]{2,1,0:T(8,128)(2,1)S(1)}, u32[]{:S(2)}, u32[]{:S(2)}) async-start(bf16[64,22,256]{2,1,0:T(8,128)(2,1)} %convert_element_type.54), calls=%async_computation.1 | async-start | bytes 1572864 | tf_op jit(solution)/shard_map/all_to_all | solution.py:101

commit v13 on v11

--- a/solution.py
+++ b/solution.py
@@ -32,7 +32,8 @@
     section_rank = lax.axis_index("section")
 
     receiver = (section_rank + 1) % section_count
-    wanted = lax.dynamic_index_in_dim(plan, receiver, 0, keepdims=False)
+    wanted = jnp.sum(jnp.where(jnp.arange(section_count) == receiver, plan, 0))
+
     def pick(box):
         slots = box[0]
         chosen = slots[0]

time: 101 us -> 101 us (level)
  other arithmetic: 6.34 us -> 7.63 us
  local copies, waits for them, and re-layouts: 10.1 us -> 8.85 us
    reduce_sum x0 -> x1, other arithmetic: none -> 1.29 us  [body(): wanted = jnp.sum(jnp.where(jnp.arange(section_count) == receiver, plan, 0))]
    dynamic_slice x1 -> x0, local copies, waits for them, and re-layouts: 1.24 us -> none  [body(): wanted = lax.dynamic_index_in_dim(plan, receiver, 0, keepdims=False)]
where the time goes in v13:
time: 101 us; the launch traced here: 100 us
  waiting for transfers between devices  37.2 us (37%)
  starting transfers between devices  31.8 us (31%)
  matrix products  13.1 us (13%)
  local copies, waits for them, and re-layouts  8.85 us (9%)
  other arithmetic  7.63 us (8%)
  between operations  1.61 us (2%)
    all_to_all x1, waiting for transfers between devices, body(): lax.all_to_all(grad_terms.astype(jnp.bfloat16), plane, split_axis=0, conc...  18.5 us
    ppermute x3, starting transfers between devices, passed_along(): return lax.ppermute(block, axis, route)  15.5 us
    all_to_all x1, starting transfers between devices, body(): lax.all_to_all(kv_pieces, plane, split_axis=0, concat_axis=0, tiled=True)  11.4 us
    ppermute x3, waiting for transfers between devices, passed_along(): return lax.ppermute(block, axis, route)  9.46 us
    all_to_all x1, waiting for transfers between devices, body(): lax.all_to_all(kv_pieces, plane, split_axis=0, concat_axis=0, tiled=True)  9.24 us
    all_to_all x1, starting transfers between devices, body(): lax.all_to_all(grad_terms.astype(jnp.bfloat16), plane, split_axis=0, conc...  4.93 us
    dot_general x1, matrix products, body(): jnp.einsum('gjqk,kgd->qgjd', dscores, key_heads, preferred_element_type=j...  3.32 us
    dot_general x1, matrix products, body(): jnp.einsum('qgjd,kgd->gjqk', do4, value_heads, preferred_element_type=jnp...  2.89 us
  transfers between devices with their start and end apart: 5, of which 4 were waited for; matrix products, arithmetic and copies ran while one was open for 10% of the time, Pallas kernels for 0%

profile of v13, /device:TPU:1, one launch (start us, length us, event | category | flops | bytes accessed | tf_op | source)
XLA Modules:
  0.0 100.2 jit_solution(17057098716619329048)
XLA Ops:
  0.6 1.3 %fusion.34 = s32[]{:T(128)} fusion(s32[8]{0:T(128)} %param.7, s32[]{:T(128)S(6)} %select_n.68), kind=kLoop, calls=%fused_computation.50 | loop fusion | flops 23 | bytes 40 | tf_op jit(solution)/shard_map/reduce_sum | solution.py:35
  2.6 1.6 %fusion.32 = (bf16[22,1024]{1,0:T(8,128)(2,1)S(1)}, bf16[22,1024]{1,0:T(8,128)(2,1)S(1)}) fusion(pred[]{:T(512)S(6)} %eq.15, bf16[1,2,22,1024]{3,1,2,0:T(2,128)(2,1)} %param.9, bf16[1,2,22,1024]{3,1,2,0:T(2,128)(2,1)} %param.10), kind=kLoop, calls=%fused_computation.40 | loop fusion | flops 45056 | bytes 270337 | tf_op jit(solution)/shard_map/jit(_where)/select_n | solution.py:41
  4.2 0.1 copy.55
  4.4 4.8 %collective-permute-start = (bf16[22,2048]{1,0:T(8,128)(2,1)S(1)}, bf16[22,2048]{1,0:T(8,128)(2,1)S(1)}, u32[]{:S(2)}, u32[]{:S(2)}) collective-permute-start(bf16[22,2048]{1,0:T(8,128)(2,1)S(1)} %reshape.222), channel_id=1, source_target_pairs={{448,0},{0,64},{64,128},{128,192},{192,256},{256,320},{320,384},{3... | collective-permute-start | bytes 270344 | tf_op jit(solution)/shard_map/ppermute | solution.py:15
  9.2 8.6 %collective-permute-start.2 = (bf16[176,1024]{1,0:T(8,128)(2,1)}, bf16[176,1024]{1,0:T(8,128)(2,1)S(1)}, u32[]{:S(2)}, u32[]{:S(2)}) collective-permute-start(bf16[176,1024]{1,0:T(8,128)(2,1)} %bitcast.164), channel_id=1, source_target_pairs={{64,0},{128,64},{192,128},{256,192},{320,256},{384,320},{448,384},... | collective-permute-start | bytes 1081352 | tf_op jit(solution)/shard_map/ppermute | solution.py:15
  17.8 0.6 collective-permute-done
  18.4 0.9 broadcast_in_dim.42
  19.3 11.4 %all-to-all-start = ((bf16[64,22,256]{2,1,0:T(8,128)(2,1)}), bf16[64,22,256]{2,1,0:T(8,128)(2,1)S(1)}, u32[]{:S(2)}, u32[]{:S(2)}) async-start(bf16[64,22,256]{2,1,0:T(8,128)(2,1)} %bitcast.2), calls=%async_computation | async-start | bytes 1572864 | tf_op jit(solution)/shard_map/all_to_all | solution.py:57
  30.7 1.1 %select_bitcast_fusion = bf16[176,1024]{1,0:T(8,128)(2,1)S(1)} fusion(bf16[1,2,176,1024]{3,2,1,0:T(8,128)(2,1)} %param.8, pred[]{:T(512)S(6)} %eq.15), kind=kLoop, calls=%fused_computation.35 | loop fusion | flops 180224 | bytes 1081345 | tf_op jit(solution)/shard_map/jit(_where)/select_n | solution.py:41
  31.9 2.1 %collective-permute-start.1 = (bf16[176,1024]{1,0:T(8,128)(2,1)S(1)}, bf16[176,1024]{1,0:T(8,128)(2,1)S(1)}, u32[]{:S(2)}, u32[]{:S(2)}) collective-permute-start(bf16[176,1024]{1,0:T(8,128)(2,1)S(1)} %select_bitcast_fusion), channel_id=1, source_target_pairs={{448,0},{0,64},{64,128},{128,192},{192,256},{256,320},{320,384},{3... | collective-permute-start | bytes 1081352 | tf_op jit(solution)/shard_map/ppermute | solution.py:15
  34.0 0.7 broadcast_multiply_fusion
  34.6 0.1 add.60
  34.7 0.1 iota_add_fusion
  34.8 0.1 add.59
  34.9 0.1 add.61
  34.9 0.1 add.62
  35.0 0.1 add.64
  35.1 0.2 broadcast_compare_fusion
  35.3 0.0 collective-permute-done.2
  35.4 0.1 convert_bitcast_fusion.1
  35.4 0.1 copy.78
  35.6 8.9 %collective-permute-done.1 = bf16[176,1024]{1,0:T(8,128)(2,1)S(1)} collective-permute-done((bf16[176,1024]{1,0:T(8,128)(2,1)S(1)}, bf16[176,1024]{1,0:T(8,128)(2,1)S(1)}, u32[]{:S(2)}, u32[]{:S(2)}) %collective-permute-start.1) | collective-permute-done | bytes 360480 | tf_op jit(solution)/shard_map/ppermute | solution.py:15
  44.5 0.8 copy.79
  45.3 9.2 %all-to-all-done = bf16[64,22,256]{2,1,0:T(8,128)(2,1)S(1)} async-done(((bf16[64,22,256]{2,1,0:T(8,128)(2,1)}), bf16[64,22,256]{2,1,0:T(8,128)(2,1)S(1)}, u32[]{:S(2)}, u32[]{:S(2)}) %all-to-all-start) | async-done | bytes 720928 | tf_op jit(solution)/shard_map/all_to_all | solution.py:57
  54.5 0.3 reshape.224
  54.8 1.1 %fusion.37 = (bf16[1408,1,1,128]{3,2,0,1:T(2,128)(2,1)S(1)}, bf16[1408,1,1,128]{3,2,0,1:T(2,128)(2,1)S(1)}) fusion(bf16[1408,1,2,128]{3,2,0,1:T(2,128)(2,1)S(1)} %reshape.224), kind=kLoop, calls=%fused_computation.54 | loop fusion | bytes 1441792 | tf_op jit(solution)/shard_map/slice | solution.py:60
  55.9 1.9 %fusion.39 = (f32[8,176]{1,0:T(8,128)S(1)}, f32[1,8,176,1408]{3,2,1,0:T(8,128)S(1)}) fusion(bf16[1408,1,1,128]{3,2,0,1:T(2,128)(2,1)S(1)} %get-tuple-element.11, pred[176,1408]{1,0:T(8,128)(4,1)S(1)} %broadcast_compare_fusion, bf16[176,1024]{1,0:T(8,128)(2,1)S(1)} %collective-permute-done.1), kind=kOutput, calls=%fused_computation.56 | convolution fusion | flops 513456768 | bytes 8904192 | tf_op jit(solution)/shard_map/qgjd,kgd->gjqk/dot_general | solution.py:72
  57.8 2.0 %select_reduce_fusion = f32[8,176]{1,0:T(8,128)S(1)} fusion(f32[1,8,176,1408]{3,2,1,0:T(8,128)S(1)} %get-tuple-element.15, f32[8,176]{1,0:T(8,128)S(1)} %get-tuple-element.14, pred[176,1408]{1,0:T(8,128)(4,1)S(1)} %broadcast_compare_fusion), kind=kLoop, calls=%fused_computation.5 | loop fusion | flops 5945984 | bytes 8188928 | tf_op jit(solution)/shard_map/reduce_sum | solution.py:75
  59.8 2.5 %fusion.23 = (f32[176,8]{0,1:T(8,128)S(1)}, bf16[176,1,8,128]{3,0,2,1:T(8,128)(2,1)}) fusion(f32[176,1,8,128]{3,2,0,1:T(8,128)S(1)} %bitcast.152, f32[1,8,176,1408]{3,2,1,0:T(8,128)S(1)} %get-tuple-element.15, f32[8,176]{1,0:T(8,128)S(1)} %log_add_fusion, pred[176,1408]{1,0:T(8,128)(4,1)S(1)} %broadcast_compare_fusion, ...), kind=kOutput, calls=%fused_computation.26 | convolution fusion | flops 513997440 | bytes 9630720 | tf_op jit(solution)/shard_map/gjqk,kgd->qgjd/dot_general | solution.py:79
  62.3 2.9 %fusion.6 = bf16[8,176,1408]{2,1,0:T(8,128)(2,1)S(1)} fusion(f32[8,176]{1,0:T(8,128)S(1)} %bitcast.162, f32[1,8,176,1408]{3,2,1,0:T(8,128)S(1)} %get-tuple-element.15, f32[8,176]{1,0:T(8,128)S(1)} %log_add_fusion, pred[176,1408]{1,0:T(8,128)(4,1)S(1)} %broadcast_compare_fusion, bf16[1408,1,1,128]{3,2,0,1:T(2,128)(2,1)S(1)} %get-tuple-element.10, ...), kind=kOutput, calls=%fused_computation.10 | convolution fusion | flops 517423104 | bytes 12874752 | tf_op jit(solution)/shard_map/qgjd,kgd->gjqk/dot_general | solution.py:83
  65.2 0.0 copy-start
  65.2 0.0 copy-done.1
  65.2 0.9 fusion.17
  66.1 0.0 copy-start.2
  66.1 1.7 %fusion.20 = bf16[1408,1,1,128]{0,3,2,1:T(8,128)(2,1)S(1)} fusion(f32[1,8,176,1408]{3,2,1,0:T(8,128)S(1)} %get-tuple-element.15, f32[8,176]{1,0:T(8,128)S(1)} %log_add_fusion, pred[176,1408]{1,0:T(8,128)(4,1)S(1)} %broadcast_compare_fusion, bf16[176,1024]{1,0:T(8,128)(2,1)S(1)} %collective-permute-done.2), kind=kOutput, calls=%fused_computation.17 | convolution fusion | flops 513638400 | bytes 8904192 | tf_op jit(solution)/shard_map/gjqk,qgjd->kgd/dot_general | solution.py:89
  67.8 0.1 pad_maximum_fusion
  67.9 1.0 %copy.67 = bf16[1408,1,2,128]{3,2,0,1:T(2,128)(2,1)S(1)} copy(bf16[1408,1,2,128]{0,3,2,1:T(8,128)(2,1)S(1)} %pad_maximum_fusion) | data formatting | bytes 1441792 | tf_op jit(solution)/shard_map/stack | solution.py:93
  68.9 1.3 %convert_element_type.54 = bf16[64,22,256]{2,1,0:T(8,128)(2,1)} reshape(bf16[1408,1,2,128]{3,2,0,1:T(2,128)(2,1)S(1)} %copy.67) | data formatting | bytes 1441792 | tf_op jit(solution)/shard_map/convert_element_type | solution.py:95
  70.2 4.9 %all-to-all-start.1 = ((bf16[64,22,256]{2,1,0:T(8,128)(2,1)}), bf16[64,22,256]{2,1,0:T(8,128)(2,1)S(1)}, u32[]{:S(2)}, u32[]{:S(2)}) async-start(bf16[64,22,256]{2,1,0:T(8,128)(2,1)} %convert_element_type.54), calls=%async_computation.1 | async-start | bytes 1572864 | tf_op jit(solution)/shard_map/all_to_all | solution.py:94
  75.2 0.1 copy.60
  75.3 0.9 broadcast_in_dim_reshape.6
  76.2 3.3 %fusion.22 = bf16[176,1,8,128]{3,0,2,1:T(8,128)(2,1)S(1)} fusion(bf16[8,176,1408]{2,1,0:T(8,128)(2,1)} %copy-done, bf16[1408,1,1,128]{3,2,0,1:T(2,128)(2,1)S(1)} %get-tuple-element.11), kind=kOutput, calls=%fused_computation.23 | convolution fusion | flops 507871232 | bytes 4685824 | tf_op jit(solution)/shard_map/gjqk,kgd->qgjd/dot_general | solution.py:86
  79.5 0.1 copy.63
  79.6 0.9 broadcast_in_dim_reshape.7
  80.5 18.5 %all-to-all-done.1 = bf16[64,22,256]{2,1,0:T(8,128)(2,1)S(1)} async-done(((bf16[64,22,256]{2,1,0:T(8,128)(2,1)}), bf16[64,22,256]{2,1,0:T(8,128)(2,1)S(1)}, u32[]{:S(2)}, u32[]{:S(2)}) %all-to-all-start.1) | async-done | bytes 720928 | tf_op jit(solution)/shard_map/all_to_all | solution.py:94
  99.0 0.1 convert_bitcast_fusion
  99.1 0.4 bitcast_reduce_fusion
  99.5 0.7 fusion.38
  (15 shorter events, 0.2 us)
Async XLA Ops:
  4.4 14.0 %collective-permute-start = (bf16[22,2048]{1,0:T(8,128)(2,1)S(1)}, bf16[22,2048]{1,0:T(8,128)(2,1)S(1)}, u32[]{:S(2)}, u32[]{:S(2)}) collective-permute-start(bf16[22,2048]{1,0:T(8,128)(2,1)S(1)} %reshape.222), channel_id=1, source_target_pairs={{448,0},{0,64},{64,128},{128,192},{192,256},{256,320},{320,384},{3... | collective-permute-start | bytes 270344 | tf_op jit(solution)/shard_map/ppermute | solution.py:15
  9.2 26.2 %collective-permute-start.2 = (bf16[176,1024]{1,0:T(8,128)(2,1)}, bf16[176,1024]{1,0:T(8,128)(2,1)S(1)}, u32[]{:S(2)}, u32[]{:S(2)}) collective-permute-start(bf16[176,1024]{1,0:T(8,128)(2,1)} %bitcast.164), channel_id=1, source_target_pairs={{64,0},{128,64},{192,128},{256,192},{320,256},{384,320},{448,384},... | collective-permute-start | bytes 1081352 | tf_op jit(solution)/shard_map/ppermute | solution.py:15
  19.3 35.2 %all-to-all-start = ((bf16[64,22,256]{2,1,0:T(8,128)(2,1)}), bf16[64,22,256]{2,1,0:T(8,128)(2,1)S(1)}, u32[]{:S(2)}, u32[]{:S(2)}) async-start(bf16[64,22,256]{2,1,0:T(8,128)(2,1)} %bitcast.2), calls=%async_computation | async-start | bytes 1572864 | tf_op jit(solution)/shard_map/all_to_all | solution.py:57
  31.9 12.6 %collective-permute-start.1 = (bf16[176,1024]{1,0:T(8,128)(2,1)S(1)}, bf16[176,1024]{1,0:T(8,128)(2,1)S(1)}, u32[]{:S(2)}, u32[]{:S(2)}) collective-permute-start(bf16[176,1024]{1,0:T(8,128)(2,1)S(1)} %select_bitcast_fusion), channel_id=1, source_target_pairs={{448,0},{0,64},{64,128},{128,192},{192,256},{256,320},{320,384},{3... | collective-permute-start | bytes 1081352 | tf_op jit(solution)/shard_map/ppermute | solution.py:15
  62.3 2.9 %copy-start.1 = (bf16[22,8,8,128]{3,2,1,0:T(8,128)(2,1)S(1)}, bf16[22,8,8,128]{3,2,1,0:T(8,128)(2,1)}, u32[]{:S(2)}) copy-start(bf16[22,8,8,128]{3,2,1,0:T(8,128)(2,1)} %copy.79) | copy-start | bytes 1081348
  65.2 2.6 %copy-start = (bf16[8,176,1408]{2,1,0:T(8,128)(2,1)}, bf16[8,176,1408]{2,1,0:T(8,128)(2,1)S(1)}, u32[]{:S(2)}) copy-start(bf16[8,176,1408]{2,1,0:T(8,128)(2,1)S(1)} %fusion.6) | copy-start | bytes 11894788
  66.1 9.1 %copy-start.2 = (bf16[176,1,8,128]{3,0,2,1:T(8,128)(2,1)S(1)}, bf16[176,1,8,128]{3,0,2,1:T(8,128)(2,1)}, u32[]{:S(2)}) copy-start(bf16[176,1,8,128]{3,0,2,1:T(8,128)(2,1)} %get-tuple-element.9) | copy-start | bytes 1081348
  70.2 28.7 %all-to-all-start.1 = ((bf16[64,22,256]{2,1,0:T(8,128)(2,1)}), bf16[64,22,256]{2,1,0:T(8,128)(2,1)S(1)}, u32[]{:S(2)}, u32[]{:S(2)}) async-start(bf16[64,22,256]{2,1,0:T(8,128)(2,1)} %convert_element_type.54), calls=%async_computation.1 | async-start | bytes 1572864 | tf_op jit(solution)/shard_map/all_to_all | solution.py:94

commit v14 on v11

--- a/solution.py
+++ b/solution.py
@@ -43,10 +43,10 @@
     q_send = pick(q_box)
     k_send = pick(k_box)
     v_send = pick(v_box)
-    kv_send = jnp.stack(
-        [k_send.reshape(kv_rows, -1, head_size), v_send.reshape(kv_rows, -1, head_size)], axis=2
+    queries, k_in, v_in = passed_along((q_send, k_send, v_send), "section", 1)
+    kv_rows_in = jnp.stack(
+        [k_in.reshape(kv_rows, -1, head_size), v_in.reshape(kv_rows, -1, head_size)], axis=2
     ).reshape(kv_rows, -1)
-    queries, kv_rows_in = passed_along((q_send, kv_send), "section", 1)
     cotangent = passed_along(grad_out[0], "section", -1)
 
     plane = ("ctx", "tp")

time: 101 us -> 103 us (1.020)
  local copies, waits for them, and re-layouts: 10.1 us -> 12.2 us
  starting transfers between devices: 31.6 us -> 33.3 us
  other arithmetic: 6.34 us -> 4.85 us
    slice x0 -> x2, local copies, waits for them, and re-layouts: none -> 2.25 us  [pick(): chosen = jnp.where(wanted == slot, slots[slot], chosen)]
    ppermute x3 -> x4, starting transfers between devices: 15.3 us -> 17.2 us  [passed_along(): return lax.ppermute(block, axis, route)]
    select_n x2 -> x3, other arithmetic: 2.7 us -> 1.21 us  [pick(): chosen = jnp.where(wanted == slot, slots[slot], chosen)]
    ppermute x3 -> x4, waiting for transfers between devices: 9.64 us -> 9.09 us  [passed_along(): return lax.ppermute(block, axis, route)]
  transfers between devices with their start and end apart: 5 -> 6, of which waited for: 4 -> 3; matrix products, arithmetic and copies ran while one was open for 10% -> 11% of each run, Pallas kernels for 0% -> 0%
where the time goes in v14:
time: 103 us; the launch traced here: 102 us
  waiting for transfers between devices  36.8 us (36%)
  starting transfers between devices  33.3 us (32%)
  matrix products  13.1 us (13%)
  local copies, waits for them, and re-layouts  12.2 us (12%)
  other arithmetic  4.85 us (5%)
  between operations  1.62 us (2%)
    all_to_all x1, waiting for transfers between devices, body(): lax.all_to_all(grad_terms.astype(jnp.bfloat16), plane, split_axis=0, conc...  18.5 us
    ppermute x4, starting transfers between devices, passed_along(): return lax.ppermute(block, axis, route)  17.2 us
    all_to_all x1, starting transfers between devices, body(): lax.all_to_all(kv_pieces, plane, split_axis=0, concat_axis=0, tiled=True)  11.2 us
    all_to_all x1, waiting for transfers between devices, body(): lax.all_to_all(kv_pieces, plane, split_axis=0, concat_axis=0, tiled=True)  9.24 us
    ppermute x4, waiting for transfers between devices, passed_along(): return lax.ppermute(block, axis, route)  9.09 us
    all_to_all x1, starting transfers between devices, body(): lax.all_to_all(grad_terms.astype(jnp.bfloat16), plane, split_axis=0, conc...  4.92 us
    dot_general x1, matrix products, body(): jnp.einsum('gjqk,kgd->qgjd', dscores, key_heads, preferred_element_type=j...  3.32 us
    dot_general x1, matrix products, body(): jnp.einsum('qgjd,kgd->gjqk', do4, value_heads, preferred_element_type=jnp...  2.9 us
  transfers between devices with their start and end apart: 6, of which 3 were waited for; matrix products, arithmetic and copies ran while one was open for 11% of the time, Pallas kernels for 0%

profile of v14, /device:TPU:1, one launch (start us, length us, event | category | flops | bytes accessed | tf_op | source)
XLA Modules:
  0.0 102.0 jit_solution(14355931987559861313)
XLA Ops:
  0.6 1.1 %fusion.39 = (bf16[1,1,22,1024]{3,1,2,0:T(2,128)(2,1)S(1)}, bf16[1,1,22,1024]{3,1,2,0:T(2,128)(2,1)S(1)}) fusion(bf16[1,2,22,1024]{3,1,2,0:T(2,128)(2,1)} %param.10), kind=kLoop, calls=%fused_computation.54 | loop fusion | bytes 180224 | tf_op jit(solution)/shard_map/slice | solution.py:40
  1.8 1.2 %dynamic_slice.8 = s32[1]{0:T(128)} dynamic-slice(s32[8]{0:T(128)} %param.7, s32[]{:T(128)S(6)} %select_n.55), dynamic_slice_sizes={1} | dynamic-slice | bytes 12 | tf_op jit(solution)/shard_map/jit(dynamic_index_in_dim)/dynamic_slice | solution.py:35
  3.7 4.8 %collective-permute-start.1 = (bf16[22,1024]{1,0:T(8,128)(2,1)S(1)}, bf16[22,1024]{1,0:T(8,128)(2,1)S(1)}, u32[]{:S(2)}, u32[]{:S(2)}) collective-permute-start(bf16[22,1024]{1,0:T(8,128)(2,1)S(1)} %fusion.32), channel_id=1, source_target_pairs={{448,0},{0,64},{64,128},{128,192},{192,256},{256,320},{320,384},{3... | collective-permute-start | bytes 135176 | tf_op jit(solution)/shard_map/ppermute | solution.py:15
  8.5 1.1 %fusion.38 = (bf16[1,1,22,1024]{3,1,2,0:T(2,128)(2,1)S(1)}, bf16[1,1,22,1024]{3,1,2,0:T(2,128)(2,1)S(1)}) fusion(bf16[1,2,22,1024]{3,1,2,0:T(2,128)(2,1)} %param.9), kind=kLoop, calls=%fused_computation.53 | loop fusion | bytes 180224 | tf_op jit(solution)/shard_map/slice | solution.py:40
  9.7 4.0 %collective-permute-start = (bf16[22,1024]{1,0:T(8,128)(2,1)S(1)}, bf16[22,1024]{1,0:T(8,128)(2,1)S(1)}, u32[]{:S(2)}, u32[]{:S(2)}) collective-permute-start(bf16[22,1024]{1,0:T(8,128)(2,1)S(1)} %fusion.33), channel_id=1, source_target_pairs={{448,0},{0,64},{64,128},{128,192},{192,256},{256,320},{320,384},{3... | collective-permute-start | bytes 135176 | tf_op jit(solution)/shard_map/ppermute | solution.py:15
  13.7 6.5 %collective-permute-start.3 = (bf16[176,1024]{1,0:T(8,128)(2,1)}, bf16[176,1024]{1,0:T(8,128)(2,1)S(1)}, u32[]{:S(2)}, u32[]{:S(2)}) collective-permute-start(bf16[176,1024]{1,0:T(8,128)(2,1)} %bitcast.168), channel_id=1, source_target_pairs={{64,0},{128,64},{192,128},{256,192},{320,256},{384,320},{448,384},... | collective-permute-start | bytes 1081352 | tf_op jit(solution)/shard_map/ppermute | solution.py:15
  20.2 0.0 collective-permute-done.1
  20.3 0.0 collective-permute-done
  20.4 0.9 broadcast_in_dim.37
  21.3 11.2 %all-to-all-start = ((bf16[64,22,256]{2,1,0:T(8,128)(2,1)}), bf16[64,22,256]{2,1,0:T(8,128)(2,1)S(1)}, u32[]{:S(2)}, u32[]{:S(2)}) async-start(bf16[64,22,256]{2,1,0:T(8,128)(2,1)} %bitcast.8), calls=%async_computation | async-start | bytes 1572864 | tf_op jit(solution)/shard_map/all_to_all | solution.py:56
  32.5 1.1 %select_bitcast_fusion = bf16[176,1024]{1,0:T(8,128)(2,1)S(1)} fusion(bf16[1,2,176,1024]{3,2,1,0:T(8,128)(2,1)} %param.8, pred[]{:T(512)} %bitcast), kind=kLoop, calls=%fused_computation.35 | loop fusion | flops 180224 | bytes 1081345 | tf_op jit(solution)/shard_map/jit(_where)/select_n | solution.py:40
  33.6 1.9 %collective-permute-start.2 = (bf16[176,1024]{1,0:T(8,128)(2,1)S(1)}, bf16[176,1024]{1,0:T(8,128)(2,1)S(1)}, u32[]{:S(2)}, u32[]{:S(2)}) collective-permute-start(bf16[176,1024]{1,0:T(8,128)(2,1)S(1)} %select_bitcast_fusion), channel_id=1, source_target_pairs={{448,0},{0,64},{64,128},{128,192},{192,256},{256,320},{320,384},{3... | collective-permute-start | bytes 1081352 | tf_op jit(solution)/shard_map/ppermute | solution.py:15
  35.5 0.7 broadcast_multiply_fusion
  36.2 0.1 add.65
  36.3 0.1 iota_add_fusion
  36.4 0.1 add.64
  36.5 0.1 add.66
  36.5 0.1 add.67
  36.6 0.1 add.69
  36.7 0.2 broadcast_compare_fusion
  36.9 0.0 collective-permute-done.3
  36.9 0.1 convert_bitcast_fusion.1
  37.0 0.1 copy.101
  37.2 9.1 %collective-permute-done.2 = bf16[176,1024]{1,0:T(8,128)(2,1)S(1)} collective-permute-done((bf16[176,1024]{1,0:T(8,128)(2,1)S(1)}, bf16[176,1024]{1,0:T(8,128)(2,1)S(1)}, u32[]{:S(2)}, u32[]{:S(2)}) %collective-permute-start.2) | collective-permute-done | bytes 360480 | tf_op jit(solution)/shard_map/ppermute | solution.py:15
  46.2 0.8 copy.102
  47.0 9.2 %all-to-all-done = bf16[64,22,256]{2,1,0:T(8,128)(2,1)S(1)} async-done(((bf16[64,22,256]{2,1,0:T(8,128)(2,1)}), bf16[64,22,256]{2,1,0:T(8,128)(2,1)S(1)}, u32[]{:S(2)}, u32[]{:S(2)}) %all-to-all-start) | async-done | bytes 720928 | tf_op jit(solution)/shard_map/all_to_all | solution.py:56
  56.3 0.3 reshape.184
  56.6 1.1 %fusion.36 = (bf16[1408,1,1,128]{3,2,0,1:T(2,128)(2,1)S(1)}, bf16[1408,1,1,128]{3,2,0,1:T(2,128)(2,1)S(1)}) fusion(bf16[1408,1,2,128]{3,2,0,1:T(2,128)(2,1)S(1)} %reshape.184), kind=kLoop, calls=%fused_computation.51 | loop fusion | bytes 1441792 | tf_op jit(solution)/shard_map/slice | solution.py:59
  57.6 1.9 %fusion.40 = (f32[8,176]{1,0:T(8,128)S(1)}, f32[1,8,176,1408]{3,2,1,0:T(8,128)S(1)}) fusion(bf16[1408,1,1,128]{3,2,0,1:T(2,128)(2,1)S(1)} %get-tuple-element.11, pred[176,1408]{1,0:T(8,128)(4,1)S(1)} %broadcast_compare_fusion, bf16[176,1024]{1,0:T(8,128)(2,1)S(1)} %collective-permute-done.2), kind=kOutput, calls=%fused_computation.55 | convolution fusion | flops 513456768 | bytes 8904192 | tf_op jit(solution)/shard_map/qgjd,kgd->gjqk/dot_general | solution.py:71
  59.5 2.0 %select_reduce_fusion = f32[8,176]{1,0:T(8,128)S(1)} fusion(f32[1,8,176,1408]{3,2,1,0:T(8,128)S(1)} %get-tuple-element.19, f32[8,176]{1,0:T(8,128)S(1)} %get-tuple-element.18, pred[176,1408]{1,0:T(8,128)(4,1)S(1)} %broadcast_compare_fusion), kind=kLoop, calls=%fused_computation.5 | loop fusion | flops 5945984 | bytes 8188928 | tf_op jit(solution)/shard_map/reduce_sum | solution.py:74
  61.6 2.5 %fusion.23 = (f32[176,8]{0,1:T(8,128)S(1)}, bf16[176,1,8,128]{3,0,2,1:T(8,128)(2,1)}) fusion(f32[176,1,8,128]{3,2,0,1:T(8,128)S(1)} %bitcast.158, f32[1,8,176,1408]{3,2,1,0:T(8,128)S(1)} %get-tuple-element.19, f32[8,176]{1,0:T(8,128)S(1)} %log_add_fusion, pred[176,1408]{1,0:T(8,128)(4,1)S(1)} %broadcast_compare_fusion, ...), kind=kOutput, calls=%fused_computation.26 | convolution fusion | flops 513997440 | bytes 9630720 | tf_op jit(solution)/shard_map/gjqk,kgd->qgjd/dot_general | solution.py:78
  64.1 2.9 %fusion.6 = bf16[8,176,1408]{2,1,0:T(8,128)(2,1)S(1)} fusion(f32[8,176]{1,0:T(8,128)S(1)} %bitcast.166, f32[1,8,176,1408]{3,2,1,0:T(8,128)S(1)} %get-tuple-element.19, f32[8,176]{1,0:T(8,128)S(1)} %log_add_fusion, pred[176,1408]{1,0:T(8,128)(4,1)S(1)} %broadcast_compare_fusion, bf16[1408,1,1,128]{3,2,0,1:T(2,128)(2,1)S(1)} %get-tuple-element.10, ...), kind=kOutput, calls=%fused_computation.10 | convolution fusion | flops 517423104 | bytes 12874752 | tf_op jit(solution)/shard_map/qgjd,kgd->gjqk/dot_general | solution.py:82
  67.0 0.9 fusion.17
  67.9 0.0 copy-start.2
  67.9 1.7 %fusion.20 = bf16[1408,1,1,128]{0,3,2,1:T(8,128)(2,1)S(1)} fusion(f32[1,8,176,1408]{3,2,1,0:T(8,128)S(1)} %get-tuple-element.19, f32[8,176]{1,0:T(8,128)S(1)} %log_add_fusion, pred[176,1408]{1,0:T(8,128)(4,1)S(1)} %broadcast_compare_fusion, bf16[176,1024]{1,0:T(8,128)(2,1)S(1)} %collective-permute-done.3), kind=kOutput, calls=%fused_computation.17 | convolution fusion | flops 513638400 | bytes 8904192 | tf_op jit(solution)/shard_map/gjqk,qgjd->kgd/dot_general | solution.py:88
  69.5 0.1 pad_maximum_fusion
  69.6 1.0 %copy.87 = bf16[1408,1,2,128]{3,2,0,1:T(2,128)(2,1)S(1)} copy(bf16[1408,1,2,128]{0,3,2,1:T(8,128)(2,1)S(1)} %pad_maximum_fusion) | data formatting | bytes 1441792 | tf_op jit(solution)/shard_map/stack | solution.py:92
  70.7 1.4 %convert_element_type.54 = bf16[64,22,256]{2,1,0:T(8,128)(2,1)} reshape(bf16[1408,1,2,128]{3,2,0,1:T(2,128)(2,1)S(1)} %copy.87) | data formatting | bytes 1441792 | tf_op jit(solution)/shard_map/convert_element_type | solution.py:94
  72.0 4.9 %all-to-all-start.1 = ((bf16[64,22,256]{2,1,0:T(8,128)(2,1)}), bf16[64,22,256]{2,1,0:T(8,128)(2,1)S(1)}, u32[]{:S(2)}, u32[]{:S(2)}) async-start(bf16[64,22,256]{2,1,0:T(8,128)(2,1)} %convert_element_type.54), calls=%async_computation.1 | async-start | bytes 1572864 | tf_op jit(solution)/shard_map/all_to_all | solution.py:93
  77.0 0.1 copy.80
  77.1 0.9 broadcast_in_dim_reshape.6
  78.0 3.3 %fusion.22 = bf16[176,1,8,128]{3,0,2,1:T(8,128)(2,1)S(1)} fusion(bf16[8,176,1408]{2,1,0:T(8,128)(2,1)} %copy-done, bf16[1408,1,1,128]{3,2,0,1:T(2,128)(2,1)S(1)} %get-tuple-element.11), kind=kOutput, calls=%fused_computation.23 | convolution fusion | flops 507871232 | bytes 4685824 | tf_op jit(solution)/shard_map/gjqk,kgd->qgjd/dot_general | solution.py:85
  81.3 0.1 copy.83
  81.4 0.9 broadcast_in_dim_reshape.7
  82.3 18.5 %all-to-all-done.1 = bf16[64,22,256]{2,1,0:T(8,128)(2,1)S(1)} async-done(((bf16[64,22,256]{2,1,0:T(8,128)(2,1)}), bf16[64,22,256]{2,1,0:T(8,128)(2,1)S(1)}, u32[]{:S(2)}, u32[]{:S(2)}) %all-to-all-start.1) | async-done | bytes 720928 | tf_op jit(solution)/shard_map/all_to_all | solution.py:93
  100.8 0.1 convert_bitcast_fusion
  100.9 0.4 bitcast_reduce_fusion
  101.3 0.7 fusion.37
  (15 shorter events, 0.2 us)
Async XLA Ops:
  3.7 16.5 %collective-permute-start.1 = (bf16[22,1024]{1,0:T(8,128)(2,1)S(1)}, bf16[22,1024]{1,0:T(8,128)(2,1)S(1)}, u32[]{:S(2)}, u32[]{:S(2)}) collective-permute-start(bf16[22,1024]{1,0:T(8,128)(2,1)S(1)} %fusion.32), channel_id=1, source_target_pairs={{448,0},{0,64},{64,128},{128,192},{192,256},{256,320},{320,384},{3... | collective-permute-start | bytes 135176 | tf_op jit(solution)/shard_map/ppermute | solution.py:15
  9.7 10.6 %collective-permute-start = (bf16[22,1024]{1,0:T(8,128)(2,1)S(1)}, bf16[22,1024]{1,0:T(8,128)(2,1)S(1)}, u32[]{:S(2)}, u32[]{:S(2)}) collective-permute-start(bf16[22,1024]{1,0:T(8,128)(2,1)S(1)} %fusion.33), channel_id=1, source_target_pairs={{448,0},{0,64},{64,128},{128,192},{192,256},{256,320},{320,384},{3... | collective-permute-start | bytes 135176 | tf_op jit(solution)/shard_map/ppermute | solution.py:15
  13.7 23.2 %collective-permute-start.3 = (bf16[176,1024]{1,0:T(8,128)(2,1)}, bf16[176,1024]{1,0:T(8,128)(2,1)S(1)}, u32[]{:S(2)}, u32[]{:S(2)}) collective-permute-start(bf16[176,1024]{1,0:T(8,128)(2,1)} %bitcast.168), channel_id=1, source_target_pairs={{64,0},{128,64},{192,128},{256,192},{320,256},{384,320},{448,384},... | collective-permute-start | bytes 1081352 | tf_op jit(solution)/shard_map/ppermute | solution.py:15
  21.3 35.0 %all-to-all-start = ((bf16[64,22,256]{2,1,0:T(8,128)(2,1)}), bf16[64,22,256]{2,1,0:T(8,128)(2,1)S(1)}, u32[]{:S(2)}, u32[]{:S(2)}) async-start(bf16[64,22,256]{2,1,0:T(8,128)(2,1)} %bitcast.8), calls=%async_computation | async-start | bytes 1572864 | tf_op jit(solution)/shard_map/all_to_all | solution.py:56
  33.6 12.6 %collective-permute-start.2 = (bf16[176,1024]{1,0:T(8,128)(2,1)S(1)}, bf16[176,1024]{1,0:T(8,128)(2,1)S(1)}, u32[]{:S(2)}, u32[]{:S(2)}) collective-permute-start(bf16[176,1024]{1,0:T(8,128)(2,1)S(1)} %select_bitcast_fusion), channel_id=1, source_target_pairs={{448,0},{0,64},{64,128},{128,192},{192,256},{256,320},{320,384},{3... | collective-permute-start | bytes 1081352 | tf_op jit(solution)/shard_map/ppermute | solution.py:15
  64.1 2.9 %copy-start.1 = (bf16[22,8,8,128]{3,2,1,0:T(8,128)(2,1)S(1)}, bf16[22,8,8,128]{3,2,1,0:T(8,128)(2,1)}, u32[]{:S(2)}) copy-start(bf16[22,8,8,128]{3,2,1,0:T(8,128)(2,1)} %copy.102) | copy-start | bytes 1081348
  67.0 2.6 %copy-start = (bf16[8,176,1408]{2,1,0:T(8,128)(2,1)}, bf16[8,176,1408]{2,1,0:T(8,128)(2,1)S(1)}, u32[]{:S(2)}) copy-start(bf16[8,176,1408]{2,1,0:T(8,128)(2,1)S(1)} %fusion.6) | copy-start | bytes 11894788
  67.9 9.1 %copy-start.2 = (bf16[176,1,8,128]{3,0,2,1:T(8,128)(2,1)S(1)}, bf16[176,1,8,128]{3,0,2,1:T(8,128)(2,1)}, u32[]{:S(2)}) copy-start(bf16[176,1,8,128]{3,0,2,1:T(8,128)(2,1)} %get-tuple-element.9) | copy-start | bytes 1081348
  72.0 28.7 %all-to-all-start.1 = ((bf16[64,22,256]{2,1,0:T(8,128)(2,1)}), bf16[64,22,256]{2,1,0:T(8,128)(2,1)S(1)}, u32[]{:S(2)}, u32[]{:S(2)}) async-start(bf16[64,22,256]{2,1,0:T(8,128)(2,1)} %convert_element_type.54), calls=%async_computation.1 | async-start | bytes 1572864 | tf_op jit(solution)/shard_map/all_to_all | solution.py:93

commit v15 on v11

--- a/solution.py
+++ b/solution.py
@@ -71,9 +71,9 @@
     scores = jnp.einsum("qgjd,kgd->gjqk", q4, key_heads, preferred_element_type=jnp.float32) * scale
     scores = jnp.where(visible, scores, NEG)
     top_score = jnp.max(scores, axis=-1, keepdims=True)
-    totals = jnp.sum(jnp.where(visible, jnp.exp(scores - top_score), 0.0), axis=-1, keepdims=True)
+    totals = jnp.sum(jnp.exp(scores - top_score), axis=-1, keepdims=True)
     log_total = top_score + jnp.log(totals)
-    probs = jnp.where(visible, jnp.exp(scores - log_total), 0.0)
+    probs = jnp.exp(scores - log_total)
     probs_low = probs.astype(jnp.bfloat16)
     attended = jnp.einsum(
         "gjqk,kgd->qgjd", probs_low, value_heads, preferred_element_type=jnp.float32

time: 101 us -> 98.2 us (0.972)
  matrix products: 13.1 us -> 11.5 us
where the time goes in v15:
time: 98.2 us; the launch traced here: 97.7 us
  waiting for transfers between devices  37.4 us (38%)
  starting transfers between devices  31.6 us (32%)
  matrix products  11.5 us (12%)
  local copies, waits for them, and re-layouts  10.1 us (10%)
  other arithmetic  5.55 us (6%)
  between operations  1.6 us (2%)
    all_to_all x1, waiting for transfers between devices, body(): lax.all_to_all(grad_terms.astype(jnp.bfloat16), plane, split_axis=0, conc...  18.5 us
    ppermute x3, starting transfers between devices, passed_along(): return lax.ppermute(block, axis, route)  15.3 us
    all_to_all x1, starting transfers between devices, body(): lax.all_to_all(kv_pieces, plane, split_axis=0, concat_axis=0, tiled=True)  11.4 us
    ppermute x3, waiting for transfers between devices, passed_along(): return lax.ppermute(block, axis, route)  9.64 us
    all_to_all x1, waiting for transfers between devices, body(): lax.all_to_all(kv_pieces, plane, split_axis=0, concat_axis=0, tiled=True)  9.24 us
    all_to_all x1, starting transfers between devices, body(): lax.all_to_all(grad_terms.astype(jnp.bfloat16), plane, split_axis=0, conc...  4.92 us
    dot_general x1, matrix products, body(): jnp.einsum('gjqk,kgd->qgjd', dscores, key_heads, preferred_element_type=j...  3.31 us
    select_n x2, other arithmetic, pick(): chosen = jnp.where(wanted == slot, slots[slot], chosen)  2.7 us
  transfers between devices with their start and end apart: 5, of which 4 were waited for; matrix products, arithmetic and copies ran while one was open for 10% of the time, Pallas kernels for 0%

profile of v15, /device:TPU:1, one launch (start us, length us, event | category | flops | bytes accessed | tf_op | source)
XLA Modules:
  0.0 97.7 jit_solution(3275048713458376290)
XLA Ops:
  0.6 1.2 %dynamic_slice.8 = s32[1]{0:T(128)} dynamic-slice(s32[8]{0:T(128)} %param.7, s32[]{:T(128)S(6)} %select_n.63), dynamic_slice_sizes={1} | dynamic-slice | bytes 12 | tf_op jit(solution)/shard_map/jit(dynamic_index_in_dim)/dynamic_slice | solution.py:35
  2.5 1.6 %fusion.32 = (bf16[22,1024]{1,0:T(8,128)(2,1)S(1)}, bf16[22,1024]{1,0:T(8,128)(2,1)S(1)}) fusion(pred[]{:T(512)} %bitcast, bf16[1,2,22,1024]{3,1,2,0:T(2,128)(2,1)} %param.9, bf16[1,2,22,1024]{3,1,2,0:T(2,128)(2,1)} %param.10), kind=kLoop, calls=%fused_computation.40 | loop fusion | flops 45056 | bytes 270337 | tf_op jit(solution)/shard_map/jit(_where)/select_n | solution.py:40
  4.2 0.1 copy.55
  4.3 4.8 %collective-permute-start = (bf16[22,2048]{1,0:T(8,128)(2,1)S(1)}, bf16[22,2048]{1,0:T(8,128)(2,1)S(1)}, u32[]{:S(2)}, u32[]{:S(2)}) collective-permute-start(bf16[22,2048]{1,0:T(8,128)(2,1)S(1)} %reshape.224), channel_id=1, source_target_pairs={{448,0},{0,64},{64,128},{128,192},{192,256},{256,320},{320,384},{3... | collective-permute-start | bytes 270344 | tf_op jit(solution)/shard_map/ppermute | solution.py:15
  9.1 8.6 %collective-permute-start.2 = (bf16[176,1024]{1,0:T(8,128)(2,1)}, bf16[176,1024]{1,0:T(8,128)(2,1)S(1)}, u32[]{:S(2)}, u32[]{:S(2)}) collective-permute-start(bf16[176,1024]{1,0:T(8,128)(2,1)} %bitcast.165), channel_id=1, source_target_pairs={{64,0},{128,64},{192,128},{256,192},{320,256},{384,320},{448,384},... | collective-permute-start | bytes 1081352 | tf_op jit(solution)/shard_map/ppermute | solution.py:15
  17.7 0.6 collective-permute-done
  18.4 0.9 broadcast_in_dim.17
  19.3 11.4 %all-to-all-start = ((bf16[64,22,256]{2,1,0:T(8,128)(2,1)}), bf16[64,22,256]{2,1,0:T(8,128)(2,1)S(1)}, u32[]{:S(2)}, u32[]{:S(2)}) async-start(bf16[64,22,256]{2,1,0:T(8,128)(2,1)} %bitcast.3), calls=%async_computation | async-start | bytes 1572864 | tf_op jit(solution)/shard_map/all_to_all | solution.py:56
  30.7 1.1 %select_bitcast_fusion = bf16[176,1024]{1,0:T(8,128)(2,1)S(1)} fusion(bf16[1,2,176,1024]{3,2,1,0:T(8,128)(2,1)} %param.8, pred[]{:T(512)} %bitcast), kind=kLoop, calls=%fused_computation.35 | loop fusion | flops 180224 | bytes 1081345 | tf_op jit(solution)/shard_map/jit(_where)/select_n | solution.py:40
  31.8 1.9 %collective-permute-start.1 = (bf16[176,1024]{1,0:T(8,128)(2,1)S(1)}, bf16[176,1024]{1,0:T(8,128)(2,1)S(1)}, u32[]{:S(2)}, u32[]{:S(2)}) collective-permute-start(bf16[176,1024]{1,0:T(8,128)(2,1)S(1)} %select_bitcast_fusion), channel_id=1, source_target_pairs={{448,0},{0,64},{64,128},{128,192},{192,256},{256,320},{320,384},{3... | collective-permute-start | bytes 1081352 | tf_op jit(solution)/shard_map/ppermute | solution.py:15
  33.7 0.7 broadcast_multiply_fusion
  34.4 0.1 add.65
  34.5 0.1 iota_add_fusion
  34.6 0.1 add.64
  34.6 0.1 add.66
  34.7 0.1 add.67
  34.8 0.1 add.69
  34.9 0.2 broadcast_compare_fusion
  35.1 0.0 collective-permute-done.2
  35.1 0.1 convert_bitcast_fusion.1
  35.2 0.1 copy.78
  35.3 9.1 %collective-permute-done.1 = bf16[176,1024]{1,0:T(8,128)(2,1)S(1)} collective-permute-done((bf16[176,1024]{1,0:T(8,128)(2,1)S(1)}, bf16[176,1024]{1,0:T(8,128)(2,1)S(1)}, u32[]{:S(2)}, u32[]{:S(2)}) %collective-permute-start.1) | collective-permute-done | bytes 360480 | tf_op jit(solution)/shard_map/ppermute | solution.py:15
  44.4 0.8 copy.79
  45.2 9.2 %all-to-all-done = bf16[64,22,256]{2,1,0:T(8,128)(2,1)S(1)} async-done(((bf16[64,22,256]{2,1,0:T(8,128)(2,1)}), bf16[64,22,256]{2,1,0:T(8,128)(2,1)S(1)}, u32[]{:S(2)}, u32[]{:S(2)}) %all-to-all-start) | async-done | bytes 720928 | tf_op jit(solution)/shard_map/all_to_all | solution.py:56
  54.5 0.3 reshape.226
  54.8 1.1 %fusion.34 = (bf16[1408,1,1,128]{3,2,0,1:T(2,128)(2,1)S(1)}, bf16[1408,1,1,128]{3,2,0,1:T(2,128)(2,1)S(1)}) fusion(bf16[1408,1,2,128]{3,2,0,1:T(2,128)(2,1)S(1)} %reshape.226), kind=kLoop, calls=%fused_computation.50 | loop fusion | bytes 1441792 | tf_op jit(solution)/shard_map/slice | solution.py:59
  55.8 1.9 %fusion.36 = (f32[8,176]{1,0:T(8,128)S(1)}, f32[1,8,176,1408]{3,2,1,0:T(8,128)S(1)}) fusion(bf16[1408,1,1,128]{3,2,0,1:T(2,128)(2,1)S(1)} %get-tuple-element.11, pred[176,1408]{1,0:T(8,128)(4,1)S(1)} %broadcast_compare_fusion, bf16[176,1024]{1,0:T(8,128)(2,1)S(1)} %collective-permute-done.1), kind=kOutput, calls=%fused_computation.52 | convolution fusion | flops 513456768 | bytes 8904192 | tf_op jit(solution)/shard_map/qgjd,kgd->gjqk/dot_general | solution.py:71
  57.7 1.2 %exponential_reduce_fusion = f32[8,176]{1,0:T(8,128)S(1)} fusion(f32[1,8,176,1408]{3,2,1,0:T(8,128)S(1)} %get-tuple-element.15, f32[8,176]{1,0:T(8,128)S(1)} %get-tuple-element.14), kind=kLoop, calls=%fused_computation.5 | loop fusion | flops 3963520 | bytes 7941120 | tf_op jit(solution)/shard_map/reduce_sum | solution.py:74
  59.0 1.7 %fusion.25 = (f32[176,8]{0,1:T(8,128)S(1)}, bf16[176,1,8,128]{3,0,2,1:T(8,128)(2,1)S(1)}) fusion(f32[176,1,8,128]{3,2,0,1:T(8,128)S(1)} %bitcast.152, f32[1,8,176,1408]{3,2,1,0:T(8,128)S(1)} %get-tuple-element.15, f32[8,176]{1,0:T(8,128)S(1)} %log_add_fusion, bf16[1408,1,1,128]{3,2,0,1:T(2,128)(2,1)S(1)} %get-tuple-element.10), kind=kOutput, calls=%fused_computation.26 | convolution fusion | flops 512014976 | bytes 9382912 | tf_op jit(solution)/shard_map/gjqk,kgd->qgjd/dot_general | solution.py:78
  60.7 0.0 copy-start.1
  60.7 2.2 %fusion.6 = bf16[8,176,1408]{2,1,0:T(8,128)(2,1)S(1)} fusion(f32[8,176]{1,0:T(8,128)S(1)} %bitcast.163, f32[1,8,176,1408]{3,2,1,0:T(8,128)S(1)} %get-tuple-element.15, f32[8,176]{1,0:T(8,128)S(1)} %log_add_fusion, bf16[1408,1,1,128]{3,2,0,1:T(2,128)(2,1)S(1)} %get-tuple-element.10, bf16[176,1024]{1,0:T(8,128)(2,1)S(1)} %collective-permute-done.2), kind=kOutput, calls=%fused_computation.10 | convolution fusion | flops 515440640 | bytes 12626944 | tf_op jit(solution)/shard_map/qgjd,kgd->gjqk/dot_general | solution.py:82
  62.9 0.0 copy-start
  62.9 0.9 fusion.17
  63.8 1.5 %fusion.20 = bf16[1408,1,1,128]{0,3,2,1:T(8,128)(2,1)S(1)} fusion(f32[1,8,176,1408]{3,2,1,0:T(8,128)S(1)} %get-tuple-element.15, f32[8,176]{1,0:T(8,128)S(1)} %log_add_fusion, bf16[176,1024]{1,0:T(8,128)(2,1)S(1)} %collective-permute-done.2), kind=kOutput, calls=%fused_computation.17 | convolution fusion | flops 511655936 | bytes 8656384 | tf_op jit(solution)/shard_map/gjqk,qgjd->kgd/dot_general | solution.py:88
  65.3 0.0 copy-done
  65.3 0.1 pad_maximum_fusion
  65.4 1.0 %copy.67 = bf16[1408,1,2,128]{3,2,0,1:T(2,128)(2,1)S(1)} copy(bf16[1408,1,2,128]{0,3,2,1:T(8,128)(2,1)S(1)} %pad_maximum_fusion) | data formatting | bytes 1441792 | tf_op jit(solution)/shard_map/stack | solution.py:92
  66.5 1.3 %convert_element_type.54 = bf16[64,22,256]{2,1,0:T(8,128)(2,1)} reshape(bf16[1408,1,2,128]{3,2,0,1:T(2,128)(2,1)S(1)} %copy.67) | data formatting | bytes 1441792 | tf_op jit(solution)/shard_map/convert_element_type | solution.py:94
  67.8 4.9 %all-to-all-start.1 = ((bf16[64,22,256]{2,1,0:T(8,128)(2,1)}), bf16[64,22,256]{2,1,0:T(8,128)(2,1)S(1)}, u32[]{:S(2)}, u32[]{:S(2)}) async-start(bf16[64,22,256]{2,1,0:T(8,128)(2,1)} %convert_element_type.54), calls=%async_computation.1 | async-start | bytes 1572864 | tf_op jit(solution)/shard_map/all_to_all | solution.py:93
  72.7 0.1 copy.60
  72.8 0.9 broadcast_in_dim_reshape.6
  73.7 3.3 %fusion.22 = bf16[176,1,8,128]{3,0,2,1:T(8,128)(2,1)S(1)} fusion(bf16[8,176,1408]{2,1,0:T(8,128)(2,1)} %copy-done, bf16[1408,1,1,128]{3,2,0,1:T(2,128)(2,1)S(1)} %get-tuple-element.11), kind=kOutput, calls=%fused_computation.23 | convolution fusion | flops 507871232 | bytes 4685824 | tf_op jit(solution)/shard_map/gjqk,kgd->qgjd/dot_general | solution.py:85
  77.0 0.1 copy.63
  77.1 0.9 broadcast_in_dim_reshape.7
  78.0 18.5 %all-to-all-done.1 = bf16[64,22,256]{2,1,0:T(8,128)(2,1)S(1)} async-done(((bf16[64,22,256]{2,1,0:T(8,128)(2,1)}), bf16[64,22,256]{2,1,0:T(8,128)(2,1)S(1)}, u32[]{:S(2)}, u32[]{:S(2)}) %all-to-all-start.1) | async-done | bytes 720928 | tf_op jit(solution)/shard_map/all_to_all | solution.py:93
  96.5 0.1 convert_bitcast_fusion
  96.7 0.4 bitcast_reduce_fusion
  97.1 0.7 fusion.35
  (13 shorter events, 0.2 us)
Async XLA Ops:
  4.3 14.0 %collective-permute-start = (bf16[22,2048]{1,0:T(8,128)(2,1)S(1)}, bf16[22,2048]{1,0:T(8,128)(2,1)S(1)}, u32[]{:S(2)}, u32[]{:S(2)}) collective-permute-start(bf16[22,2048]{1,0:T(8,128)(2,1)S(1)} %reshape.224), channel_id=1, source_target_pairs={{448,0},{0,64},{64,128},{128,192},{192,256},{256,320},{320,384},{3... | collective-permute-start | bytes 270344 | tf_op jit(solution)/shard_map/ppermute | solution.py:15
  9.1 26.0 %collective-permute-start.2 = (bf16[176,1024]{1,0:T(8,128)(2,1)}, bf16[176,1024]{1,0:T(8,128)(2,1)S(1)}, u32[]{:S(2)}, u32[]{:S(2)}) collective-permute-start(bf16[176,1024]{1,0:T(8,128)(2,1)} %bitcast.165), channel_id=1, source_target_pairs={{64,0},{128,64},{192,128},{256,192},{320,256},{384,320},{448,384},... | collective-permute-start | bytes 1081352 | tf_op jit(solution)/shard_map/ppermute | solution.py:15
  19.3 35.2 %all-to-all-start = ((bf16[64,22,256]{2,1,0:T(8,128)(2,1)}), bf16[64,22,256]{2,1,0:T(8,128)(2,1)S(1)}, u32[]{:S(2)}, u32[]{:S(2)}) async-start(bf16[64,22,256]{2,1,0:T(8,128)(2,1)} %bitcast.3), calls=%async_computation | async-start | bytes 1572864 | tf_op jit(solution)/shard_map/all_to_all | solution.py:56
  31.8 12.6 %collective-permute-start.1 = (bf16[176,1024]{1,0:T(8,128)(2,1)S(1)}, bf16[176,1024]{1,0:T(8,128)(2,1)S(1)}, u32[]{:S(2)}, u32[]{:S(2)}) collective-permute-start(bf16[176,1024]{1,0:T(8,128)(2,1)S(1)} %select_bitcast_fusion), channel_id=1, source_target_pairs={{448,0},{0,64},{64,128},{128,192},{192,256},{256,320},{320,384},{3... | collective-permute-start | bytes 1081352 | tf_op jit(solution)/shard_map/ppermute | solution.py:15
  60.7 2.2 %copy-start.1 = (bf16[22,8,8,128]{3,2,1,0:T(8,128)(2,1)S(1)}, bf16[22,8,8,128]{3,2,1,0:T(8,128)(2,1)}, u32[]{:S(2)}) copy-start(bf16[22,8,8,128]{3,2,1,0:T(8,128)(2,1)} %copy.79) | copy-start | bytes 1081348
  62.9 2.4 %copy-start = (bf16[8,176,1408]{2,1,0:T(8,128)(2,1)}, bf16[8,176,1408]{2,1,0:T(8,128)(2,1)S(1)}, u32[]{:S(2)}) copy-start(bf16[8,176,1408]{2,1,0:T(8,128)(2,1)S(1)} %fusion.6) | copy-start | bytes 11894788
  67.8 28.7 %all-to-all-start.1 = ((bf16[64,22,256]{2,1,0:T(8,128)(2,1)}), bf16[64,22,256]{2,1,0:T(8,128)(2,1)S(1)}, u32[]{:S(2)}, u32[]{:S(2)}) async-start(bf16[64,22,256]{2,1,0:T(8,128)(2,1)} %convert_element_type.54), calls=%async_computation.1 | async-start | bytes 1572864 | tf_op jit(solution)/shard_map/all_to_all | solution.py:93
